TPU v7x, 32 devices: a whole 2x2x4 slice. The times are simulated.
32 devices in a mesh: row: 8 (over z, y), col: 4 (over x, core).
Axes of the slice: x: 2, y: 2, z: 4, core: 2. Of those that a mesh axis runs over, the one named last changes fastest.
Arguments:
- tokens: bfloat16 [2048, 4096], P('row', 'col'), may hold values from -6 to 6
- cotangent: bfloat16 [2048, 4096], P('row', 'col'), may hold values from -1.25 to 1.25
- w_up: float32 [4096, 12288], P('row', 'col'), may hold values from -0.1875 to 0.1875
- w_down: float32 [4096, 12288], P('row', 'col'), may hold values from -0.109375 to 0.109375
- mask_up: int32 [32, 96], P('row', 'col'), may hold values from 0 to 1, as said below
- mask_down: int32 [32, 96], P('row', 'col'), may hold values from 0 to 1, as said below
- moment_up: float32 [4096, 12288], P('row', 'col'), may hold values from -1.5 to 1.5
- second_up: float32 [4096, 12288], P('row', 'col'), may hold values from 0.01 to 0.2
- moment_down: float32 [4096, 12288], P('row', 'col'), may hold values from -1.5 to 1.5
- second_down: float32 [4096, 12288], P('row', 'col'), may hold values from 0.01 to 0.2
Outputs:
- token_grad: bfloat16 [2048, 4096], P('row', 'col')
- new_up: float32 [4096, 12288], P('row', 'col')
- new_moment_up: float32 [4096, 12288], P('row', 'col')
- new_second_up: float32 [4096, 12288], P('row', 'col')
- new_down: float32 [4096, 12288], P('row', 'col')
- new_moment_down: float32 [4096, 12288], P('row', 'col')
- new_second_down: float32 [4096, 12288], P('row', 'col')
Inputs may be any that keep to these rules, and one draw needn't show every extreme that they name: `mask_up`: 1 where the 128 x 128 block of the up projection is kept, else 0. Each tile of 4 x 24 blocks (the blocks of one device) holds at least 1 and at most 48 kept blocks, and some tile holds exactly 48. `mask_down`: 1 where the 128 x 128 block of the down projection is kept, else 0. Each tile of 4 x 24 blocks (the blocks of one device) holds at least 1 and at most 48 kept blocks, and some tile holds exactly 48.
All inputs are finite; a program needn't handle non-finite values.
Results may differ from a plain program's by a relative error of at most 0.018.
Values may be sent and summed in bfloat16 or wider, within the bound.
No kernel may reach another device: no remote copies, remote signals or barrier semaphores. Data moves between devices by JAX's collectives and lax.ppermute only.
A program may use at most 320 MiB of HBM per device.

v0:
```python
import jax
import jax.numpy as jnp
from jax import lax
from jax.sharding import PartitionSpec as P

inv_root_two = 0.7071067811865476
inv_root_two_pi = 0.3989422804014327
learn_rate = 0.001
bias_first = 1.0 - 0.9**10
bias_second = 1.0 - 0.95**10


def expand_mask(mask, block):
    blocks_r, blocks_c = mask.shape
    values = mask.astype(jnp.float32)[:, None, :, None]
    values = jnp.broadcast_to(values, (blocks_r, block, blocks_c, block))
    return values.reshape(blocks_r * block, blocks_c * block)


def gelu_parts(preact):
    normal_cdf = 0.5 * (1.0 + lax.erf(preact * inv_root_two))
    density = jnp.exp(-0.5 * preact * preact) * inv_root_two_pi
    return (preact * normal_cdf, normal_cdf + preact * density)


def adam_update(weight, moment, second, grad):
    moment_new = 0.9 * moment + 0.1 * grad
    second_new = 0.95 * second + 0.05 * grad * grad
    step_size = moment_new / bias_first / (jnp.sqrt(second_new / bias_second) + 1e-08)
    return (weight - learn_rate * step_size, moment_new, second_new)


def token_product(rows_full, other):
    return lax.dot_general(
        rows_full, other, (((0,), (0,)), ((), ())), preferred_element_type=jnp.float32
    )


def shards(
    tokens,
    cotangent,
    w_up,
    w_down,
    mask_up,
    mask_down,
    moment_up,
    second_up,
    moment_down,
    second_down,
):
    block = w_up.shape[0] // mask_up.shape[0]
    keep_up = expand_mask(mask_up, block)
    keep_down = expand_mask(mask_down, block)
    up_used = (w_up * keep_up).astype(jnp.bfloat16)
    down_used = (w_down * keep_down).astype(jnp.bfloat16)
    features, cot_rows = (
        lax.all_gather(tokens, "col", axis=1, tiled=True),
        lax.all_gather(cotangent, "col", axis=1, tiled=True),
    )
    up_whole = lax.all_gather(up_used, "row", axis=0, tiled=True)
    preact = jnp.dot(features, up_whole, preferred_element_type=jnp.float32)
    act_grad = jnp.dot(
        cot_rows,
        lax.all_gather(down_used, "row", axis=0, tiled=True),
        preferred_element_type=jnp.float32,
    )
    gelu_value, gelu_slope = gelu_parts(preact)
    activation = gelu_value.astype(jnp.bfloat16)
    pre_grad = (act_grad * gelu_slope).astype(jnp.bfloat16)
    partial_tokens = lax.dot_general(
        pre_grad, up_whole, (((1,), (1,)), ((), ())), preferred_element_type=jnp.float32
    )
    summed_down = lax.psum_scatter(
        token_product(cot_rows, activation).astype(jnp.bfloat16),
        "row",
        scatter_dimension=0,
        tiled=True,
    ).astype(jnp.float32)
    summed_up = lax.psum_scatter(
        token_product(features, pre_grad).astype(jnp.bfloat16),
        "row",
        scatter_dimension=0,
        tiled=True,
    ).astype(jnp.float32)
    token_grad = lax.psum_scatter(
        partial_tokens.astype(jnp.bfloat16), "col", scatter_dimension=1, tiled=True
    )
    grad_up = keep_up * summed_up
    grad_down = keep_down * summed_down
    new_up, new_moment_up, new_second_up = adam_update(w_up, moment_up, second_up, grad_up)
    new_down, new_moment_down, new_second_down = adam_update(
        w_down, moment_down, second_down, grad_down
    )
    return (
        token_grad,
        new_up,
        new_moment_up,
        new_second_up,
        new_down,
        new_moment_down,
        new_second_down,
    )


def solution(mesh):
    return jax.shard_map(
        shards,
        mesh=mesh,
        in_specs=(
            P("row", "col"),
            P("row", "col"),
            P("row", "col"),
            P("row", "col"),
            P("row", "col"),
            P("row", "col"),
            P("row", "col"),
            P("row", "col"),
            P("row", "col"),
            P("row", "col"),
        ),
        out_specs=(
            P("row", "col"),
            P("row", "col"),
            P("row", "col"),
            P("row", "col"),
            P("row", "col"),
            P("row", "col"),
            P("row", "col"),
        ),
        check_vma=False,
    )
```

profile of v0, /device:TPU:0, one launch (start us, length us, event | category | flops | bytes accessed | tf_op | source)
XLA Modules:
  0.0 1936.0 jit_solution(5846292603456907985)
XLA Ops:
  7.9 0.7 convert_element_type.41
  8.7 6.6 copy.20
  15.3 0.9 broadcast_in_dim.5
  16.2 3.2 copy-done.1
  19.4 1.0 copy-done
  20.4 2.8 fusion.2
  24.0 10.8 all-gather.11.cloned.1.call-done
  34.9 482.6 %all-gather.9.cloned.1.call-done = bf16[4096,3072]{0,1:T(8,128)(2,1)} async-done(((bf16[512,3072]{0,1:T(8,128)(2,1)}), bf16[4096,3072]{0,1:T(8,128)(2,1)}) %all-gather.9.cloned.1.call-update) | async-done | bytes 25165840 | tf_op jit(solution)/shard_map/all_gather | solution.py:60
  517.5 12.5 convolution_bitcast_fusion
  530.0 11.6 all-gather.7.cloned.1.call-done
  541.6 13.3 convert_bitcast_fusion
  555.7 6.6 copy.18
  562.2 7.0 copy.24
  569.3 6.6 copy.25
  575.8 383.7 %reduce-scatter.8.cloned.1.call-done = bf16[512,3072]{0,1:T(8,128)(2,1)} async-done(((bf16[4096,3072]{0,1:T(8,128)(2,1)}), bf16[512,3072]{0,1:T(8,128)(2,1)}) %reduce-scatter.8.cloned.1.call-update) | async-done | bytes 3145744 | tf_op jit(solution)/shard_map/reduce_scatter | solution.py:73
  959.5 4.1 broadcast_in_dim.4
  963.6 1.0 copy-done.2
  964.6 15.1 multiply_subtract_fusion
  980.0 479.4 %all-gather.5.cloned.1.call-done = bf16[4096,3072]{0,1:T(8,128)(2,1)} async-done(((bf16[512,3072]{0,1:T(8,128)(2,1)}), bf16[4096,3072]{0,1:T(8,128)(2,1)}) %all-gather.5.cloned.1.call-update) | async-done | bytes 25165840 | tf_op jit(solution)/shard_map/all_gather | solution.py:64
  1459.4 13.6 fusion.5
  1473.1 13.3 convert_bitcast_fusion.1
  1486.7 14.3 convolution_convert_fusion
  1501.1 6.6 copy.21
  1507.7 6.6 copy.22
  1514.3 6.6 copy.30
  1520.8 6.6 copy.31
  1527.4 6.6 copy.32
  1534.0 356.8 %reduce-scatter.6.cloned.1.call-done = bf16[512,3072]{0,1:T(8,128)(2,1)} async-done(((bf16[4096,3072]{0,1:T(8,128)(2,1)}), bf16[512,3072]{0,1:T(8,128)(2,1)}) %reduce-scatter.6.cloned.1.call-update) | async-done | bytes 3145744 | tf_op jit(solution)/shard_map/reduce_scatter | solution.py:79
  1890.8 18.3 multiply_subtract_fusion.1
  1909.1 6.9 copy.27
  1916.0 6.6 copy.28
  1922.6 6.6 copy.29
  (25 shorter events, 3.0 us)
Async XLA Ops:
  7.2 27.7 %all-gather.11.cloned.1.call-start = ((), (), s32[]{:S(2)}) async-start(), calls=%async_computation.6 | async-start | bytes 2621440 | tf_op jit(solution)/shard_map/all_gather | solution.py:57
  7.9 509.6 %all-gather.9.cloned.1.call-start = ((), (), s32[]{:S(2)}) async-start(), calls=%async_computation.5 | async-start | bytes 28311552 | tf_op jit(solution)/shard_map/all_gather | solution.py:60
  15.3 5.1 copy-start
  16.2 3.2 copy-start.1
  23.2 518.4 %all-gather.7.cloned.1.call-start = ((), (), s32[]{:S(2)}) async-start(), calls=%async_computation.4 | async-start | bytes 2621440 | tf_op jit(solution)/shard_map/all_gather | solution.py:58
  24.0 935.5 %reduce-scatter.8.cloned.1.call-start = ((), (), s32[]{:S(2)}) async-start(), calls=%async_computation.9 | async-start | bytes 28311552 | tf_op jit(solution)/shard_map/reduce_scatter | solution.py:73
  530.0 24.9 %copy-start.3 = (f32[256,3072]{0,1:T(8,128)}, f32[256,3072]{0,1:T(8,128)S(1)}, u32[]{:S(2)}) copy-start(f32[256,3072]{0,1:T(8,128)S(1)} %convolution_bitcast_fusion) | copy-start | bytes 9437188
  554.9 0.7 copy-start.4
  554.9 904.5 %all-gather.5.cloned.1.call-start = ((), (), s32[]{:S(2)}) async-start(), calls=%async_computation.3 | async-start | bytes 28311552 | tf_op jit(solution)/shard_map/all_gather | solution.py:64
  959.5 5.1 copy-start.2
  979.8 911.0 %reduce-scatter.6.cloned.1.call-start = ((), (), s32[]{:S(2)}) async-start(), calls=%async_computation.8 | async-start | bytes 28311552 | tf_op jit(solution)/shard_map/reduce_scatter | solution.py:79
  1486.4 442.7 %reduce-scatter.4.cloned.1.call-start = ((), (), s32[]{:S(2)}) async-start(), calls=%async_computation.7 | async-start | bytes 2621440 | tf_op jit(solution)/shard_map/reduce_scatter | solution.py:85
Sparse Core Ops, SparseCore 0:
  9.6 25.2 all-gather.10
  37.0 480.4 all-gather.8
  519.0 22.5 all-gather.6
  555.1 404.4 reduce-scatter.7
  979.9 479.5 all-gather.4
  1486.5 404.2 reduce-scatter.5
  1893.9 30.5 reduce-scatter.3
where the time goes:
time: 1940 us
  waiting for transfers between devices  1730 us (89%)
  local copies, waits for them, and re-layouts  90.5 us (5%)
  matrix products  67.1 us (3%)
  other arithmetic  37 us (2%)
    all_gather x1, waiting for transfers between devices, shards(): up_whole = lax.all_gather(up_used, 'row', axis=0, tiled=True)  483 us
    all_gather x1, waiting for transfers between devices, shards(): lax.all_gather(down_used, 'row', axis=0, tiled=True)  479 us
    reduce_scatter x1, waiting for transfers between devices, shards(): lax.psum_scatter(token_product(cot_rows, activation).astype(jnp.bfloat16)...  384 us
    reduce_scatter x1, waiting for transfers between devices, shards(): lax.psum_scatter(token_product(features, pre_grad).astype(jnp.bfloat16),...  357 us
    unnamed x22, local copies, waits for them, and re-layouts  85.3 us
  transfers between devices with their start and end apart: 7, of which 6 were waited for; matrix products, arithmetic and copies ran while one was open for 7% of the time, Pallas kernels for 0%

commit v1 on v0

v1 whole, which is shorter than its diff:
```python
import jax
import jax.numpy as jnp
from jax import lax
from jax.sharding import PartitionSpec as P

inv_root_two = 0.7071067811865476
inv_root_two_pi = 0.3989422804014327
learn_rate = 0.001
bias_first = 1.0 - 0.9**10
bias_second = 1.0 - 0.95**10


def expand_mask(mask, block):
    blocks_r, blocks_c = mask.shape
    values = mask.astype(jnp.float32)[:, None, :, None]
    values = jnp.broadcast_to(values, (blocks_r, block, blocks_c, block))
    return values.reshape(blocks_r * block, blocks_c * block)


def gelu_parts(preact):
    normal_cdf = 0.5 * (1.0 + lax.erf(preact * inv_root_two))
    density = jnp.exp(-0.5 * preact * preact) * inv_root_two_pi
    return (preact * normal_cdf, normal_cdf + preact * density)


def adam_update(weight, moment, second, grad):
    moment_new = 0.9 * moment + 0.1 * grad
    second_new = 0.95 * second + 0.05 * grad * grad
    step_size = moment_new / bias_first / (jnp.sqrt(second_new / bias_second) + 1e-08)
    return (weight - learn_rate * step_size, moment_new, second_new)


def token_product(rows_full, other):
    return lax.dot_general(
        rows_full, other, (((0,), (0,)), ((), ())), preferred_element_type=jnp.float32
    )


def to_blocks(dense, block):
    rows, cols = dense.shape[-2:]
    lead = dense.shape[:-2]
    nr, nc = rows // block, cols // block
    x = dense.reshape(lead + (nr, block, nc, block))
    k = len(lead)
    x = jnp.moveaxis(x, k + 2, k + 1)
    return x.reshape(lead + (nr * nc, block, block))


def from_blocks(blocks, nr, nc):
    lead = blocks.shape[:-3]
    block = blocks.shape[-1]
    x = blocks.reshape(lead + (nr, nc, block, block))
    k = len(lead)
    x = jnp.moveaxis(x, k + 1, k + 2)
    return x.reshape(lead + (nr * block, nc * block))


def kept_index(flat_mask, slots):
    n = flat_mask.shape[-1]
    upto = jnp.cumsum(flat_mask, axis=-1)
    k = jnp.arange(slots, dtype=jnp.int32)
    idx = jnp.sum((upto[..., None, :] <= k[:, None]).astype(jnp.int32), axis=-1)
    return jnp.minimum(idx, n - 1)


def slot_of(flat_mask):
    return jnp.cumsum(flat_mask, axis=-1) - flat_mask


def compact(blocks, idx):
    return jnp.take(blocks, idx, axis=-3)


def shards(
    tokens,
    cotangent,
    w_up,
    w_down,
    mask_up,
    mask_down,
    moment_up,
    second_up,
    moment_down,
    second_down,
):
    nr, nc = mask_up.shape
    block = w_up.shape[0] // nr
    slots = (nr * nc) // 2
    n_row = lax.axis_size("row")

    flat_up = mask_up.reshape(nr * nc)
    flat_down = mask_down.reshape(nr * nc)
    masks_up = lax.all_gather(flat_up, "row", axis=0)
    masks_down = lax.all_gather(flat_down, "row", axis=0)

    up_blocks = to_blocks(w_up.astype(jnp.bfloat16), block)
    down_blocks = to_blocks(w_down.astype(jnp.bfloat16), block)
    up_sent = compact(up_blocks, kept_index(flat_up, slots))
    down_sent = compact(down_blocks, kept_index(flat_down, slots))

    features, cot_rows = (
        lax.all_gather(tokens, "col", axis=1, tiled=True),
        lax.all_gather(cotangent, "col", axis=1, tiled=True),
    )

    def rebuild(sent, masks):
        got = lax.all_gather(sent, "row", axis=0)
        flat = got.reshape((n_row * slots, block, block))
        where = slot_of(masks) + (jnp.arange(n_row, dtype=jnp.int32) * slots)[:, None]
        dense = jnp.take(flat, where.reshape(-1), axis=0)
        keep = masks.reshape(-1)[:, None, None] > 0
        dense = jnp.where(keep, dense, jnp.zeros_like(dense))
        dense = dense.reshape((n_row, nr * nc, block, block))
        dense = from_blocks(dense, nr, nc)
        return dense.reshape((n_row * nr * block, nc * block))

    up_whole = rebuild(up_sent, masks_up)
    down_whole = rebuild(down_sent, masks_down)

    preact = jnp.dot(features, up_whole, preferred_element_type=jnp.float32)
    act_grad = jnp.dot(cot_rows, down_whole, preferred_element_type=jnp.float32)
    gelu_value, gelu_slope = gelu_parts(preact)
    activation = gelu_value.astype(jnp.bfloat16)
    pre_grad = (act_grad * gelu_slope).astype(jnp.bfloat16)
    partial_tokens = lax.dot_general(
        pre_grad, up_whole, (((1,), (1,)), ((), ())), preferred_element_type=jnp.float32
    )

    def reduce_kept(partial, masks, own):
        blocks = to_blocks(
            partial.astype(jnp.bfloat16).reshape((n_row, nr * block, nc * block)), block
        )
        idx = kept_index(masks, slots)
        sent = jnp.take_along_axis(blocks, idx[:, :, None, None], axis=1)
        summed = lax.psum_scatter(sent, "row", scatter_dimension=0, tiled=True)[0]
        dense = jnp.take(summed, slot_of(own), axis=0)
        keep = own[:, None, None] > 0
        dense = jnp.where(keep, dense.astype(jnp.float32), jnp.zeros(dense.shape, jnp.float32))
        return from_blocks(dense, nr, nc)

    grad_down = reduce_kept(token_product(cot_rows, activation), masks_down, flat_down)
    grad_up = reduce_kept(token_product(features, pre_grad), masks_up, flat_up)
    token_grad = lax.psum_scatter(
        partial_tokens.astype(jnp.bfloat16), "col", scatter_dimension=1, tiled=True
    )
    new_up, new_moment_up, new_second_up = adam_update(w_up, moment_up, second_up, grad_up)
    new_down, new_moment_down, new_second_down = adam_update(
        w_down, moment_down, second_down, grad_down
    )
    return (
        token_grad,
        new_up,
        new_moment_up,
        new_second_up,
        new_down,
        new_moment_down,
        new_second_down,
    )


def solution(mesh):
    spec = P("row", "col")
    return jax.shard_map(
        shards,
        mesh=mesh,
        in_specs=(spec,) * 10,
        out_specs=(spec,) * 7,
        check_vma=False,
    )
```

time: 1940 us -> 1260 us (0.65)
  waiting for transfers between devices: 1730 us -> 723 us
  local copies, waits for them, and re-layouts: 90.5 us -> 315 us
  other arithmetic: 37 us -> 92 us
  blocking collectives: 0 us -> 39 us
    all_gather x2, waiting for transfers between devices: 962 us -> 313 us  [rebuild(): got = lax.all_gather(sent, 'row', axis=0)]
    reduce_scatter x2, waiting for transfers between devices: 740 us -> 395 us  [reduce_kept(): summed = lax.psum_scatter(sent, 'row', scatter_dimension=0, tiled=True)[0]]
    another operation x0 -> x10, local copies, waits for them, and re-layouts: none -> 195 us  [the longest x4 158 us: to_blocks(): x = dense.reshape(lead + (nr, block, nc, block))]
    gather x0 -> x10, local copies, waits for them, and re-layouts: none -> 107 us  [the longest x4 49.8 us: reduce_kept(): sent = jnp.take_along_axis(blocks, idx[:, :, None, None], axis=1)]
    unnamed x22 -> x28, local copies, waits for them, and re-layouts: 85.3 us -> 3.24 us
    select_n x0 -> x10, other arithmetic: none -> 57.9 us  [the longest x2 28.3 us: rebuild(): dense = jnp.where(keep, dense, jnp.zeros_like(dense))]
    all_gather x0 -> x2, blocking collectives: none -> 39 us  [the longest x1 22.3 us: shards(): masks_down = lax.all_gather(flat_down, 'row', axis=0)]
  transfers between devices with their start and end apart: 7 -> 7, of which waited for: 6 -> 5; matrix products, arithmetic and copies ran while one was open for 7% -> 8% of each run, Pallas kernels for 0% -> 0%
where the time goes in v1:
time: 1260 us; the launch traced here: 1250 us
  waiting for transfers between devices  723 us (57%)
  local copies, waits for them, and re-layouts  315 us (25%)
  other arithmetic  92 us (7%)
  matrix products  67.1 us (5%)
  blocking collectives  39 us (3%)
  between operations  14.8 us (1%)
    reduce_scatter x2, waiting for transfers between devices, reduce_kept(): summed = lax.psum_scatter(sent, 'row', scatter_dimension=0, tiled=True)[0]  395 us
    all_gather x2, waiting for transfers between devices, rebuild(): got = lax.all_gather(sent, 'row', axis=0)  313 us
    another operation x4, local copies, waits for them, and re-layouts, to_blocks(): x = dense.reshape(lead + (nr, block, nc, block))  158 us
    gather x4, local copies, waits for them, and re-layouts, reduce_kept(): sent = jnp.take_along_axis(blocks, idx[:, :, None, None], axis=1)  49.8 us
    gather x2, local copies, waits for them, and re-layouts, rebuild(): dense = jnp.take(flat, where.reshape(-1), axis=0)  47.7 us
    another operation x2, local copies, waits for them, and re-layouts, from_blocks(): x = blocks.reshape(lead + (nr, nc, block, block))  36.1 us
    sub x2, other arithmetic, adam_update(): return (weight - learn_rate * step_size, moment_new, second_new)  29 us
    select_n x2, other arithmetic, rebuild(): dense = jnp.where(keep, dense, jnp.zeros_like(dense))  28.3 us
  transfers between devices with their start and end apart: 7, of which 5 were waited for; matrix products, arithmetic and copies ran while one was open for 8% of the time, Pallas kernels for 0%

profile of v1, /device:TPU:0, one launch (start us, length us, event | category | flops | bytes accessed | tf_op | source)
XLA Modules:
  0.0 1251.7 jit_solution(9688611325964872924)
XLA Ops:
  8.4 3.3 convert_bitcast_fusion.2
  15.9 2.8 broadcast_select_fusion.2
  20.4 22.3 %all-gather.2 = s32[8,1,96]{2,1,0:T(1,128)S(1)} all-gather(s32[1,1,96]{2,1,0:T(1,128)S(1)} %reshape.294), channel_id=1, replica_groups=mesh['row'=8,'col'=4] {'row'}, dimensions={0}, use_global_device_ids=true | all-gather | bytes 3456 | tf_op jit(solution)/shard_map/all_gather | solution.py:94
  43.0 16.6 %all-gather.3 = s32[8,1,96]{2,1,0:T(1,128)S(1)} all-gather(s32[1,1,96]{2,1,0:T(1,128)S(1)} %reshape.296), channel_id=1, replica_groups=mesh['row'=8,'col'=4] {'row'}, dimensions={0}, use_global_device_ids=true | all-gather | bytes 3456 | tf_op jit(solution)/shard_map/all_gather | solution.py:93
  60.5 137.5 %all-gather.15.cloned.1.call-done = bf16[384,128,128]{2,1,0:T(8,128)(2,1)} async-done(((bf16[48,128,128]{2,1,0:T(8,128)(2,1)}), bf16[384,128,128]{2,1,0:T(8,128)(2,1)}) %all-gather.15.cloned.1.call-update) | async-done | bytes 12582928 | tf_op jit(solution)/shard_map/all_gather | solution.py:107
  198.0 23.8 %gather_fusion.3 = bf16[768,128,128]{2,1,0:T(8,128)(2,1)} fusion(bf16[384,128,128]{2,1,0:T(8,128)(2,1)} %all-gather.15.cloned.1.call-done, s32[1024]{0:T(1024)S(1)} %pad_clamp_fusion.2), kind=kCustom, calls=%fused_computation.5.clone | custom fusion | bytes 50334720 | tf_op jit(solution)/shard_map/jit(_take)/gather | solution.py:110
  221.8 14.4 %select_select_fusion = bf16[768,128,128]{2,1,0:T(8,128)(2,1)S(1)} fusion(bf16[768,128,128]{2,1,0:T(8,128)(2,1)} %gather_fusion.3, pred[768]{0:T(1024)(128)(4,1)S(1)} %compare_and_fusion, pred[768]{0:T(1024)(128)(4,1)S(1)} %gt.41), kind=kLoop, calls=%fused_computation.15 | loop fusion | flops 25165824 | bytes 50333184 | tf_op jit(solution)/shard_map/jit(_where)/select_n | solution.py:112
  236.2 18.0 %copy.56 = bf16[8,4,24,128,128]{4,2,3,1,0:T(8,128)(2,1)} copy(bf16[8,4,24,128,128]{4,3,2,1,0:T(8,128)(2,1)S(1)} %bitcast.126) | data formatting | bytes 50331648 | tf_op jit(solution)/shard_map/reshape;reshape | solution.py:52
  254.2 12.3 fusion.19
  266.5 14.4 %convert_bitcast_fusion = bf16[4096,3072]{0,1:T(8,128)(2,1)} fusion(bf16[256,4096]{1,0:T(8,128)(2,1)} %all-gather.9.cloned.1.call-done, f32[256,3072]{0,1:T(8,128)S(1)} %fusion.19), kind=kOutput, calls=%fused_computation.17 | convolution fusion | flops 6458966016 | bytes 30408704 | tf_op jit(solution)/shard_map/dot_general | solution.py:34
  280.9 40.5 %reshape_reshape.23 = bf16[8,4,128,24,128]{2,1,0,4,3:T(4,128)(2,1)} reshape(bf16[4096,3072]{0,1:T(8,128)(2,1)} %convert_bitcast_fusion) | data formatting | bytes 50331648 | tf_op jit(solution)/shard_map/reshape;reshape | solution.py:43
  321.5 38.6 %copy.59 = bf16[8,4,128,24,128]{4,2,3,1,0:T(8,128)(2,1)} copy(bf16[8,4,128,24,128]{2,1,0,4,3:T(4,128)(2,1)} %reshape_reshape.23) | data formatting | bytes 50331648 | tf_op jit(solution)/shard_map/reshape;reshape | solution.py:43
  360.1 25.0 %gather_fusion.6 = bf16[384,128,128]{2,1,0:T(8,128)(2,1)} fusion(bf16[8,96,128,128]{3,2,1,0:T(8,128)(2,1)} %bitcast.128, s32[384]{0:T(512)S(1)} %reshape.316), kind=kCustom, calls=%fused_computation.6.clone | custom fusion | bytes 25168896 | tf_op jit(solution)/shard_map/jit(take_along_axis)/gather | solution.py:134
  385.0 10.7 broadcast_select_fusion
  396.4 205.1 %reduce-scatter.8.cloned.1.call-done = bf16[1,48,128,128]{3,2,1,0:T(8,128)(2,1)} async-done(((bf16[8,48,128,128]{3,2,1,0:T(8,128)(2,1)}), bf16[1,48,128,128]{3,2,1,0:T(8,128)(2,1)}) %reduce-scatter.8.cloned.1.call-update) | async-done | bytes 1572880 | tf_op jit(solution)/shard_map/reduce_scatter | solution.py:135
  605.4 3.6 copy.60
  609.0 16.7 %multiply_subtract_fusion = (f32[512,3072]{1,0:T(8,128)}, f32[512,3072]{1,0:T(8,128)}, f32[512,3072]{1,0:T(8,128)}, bf16[64,8,24,128]{3,1,2,0:T(8,128)(2,1)S(1)}) fusion(f32[512,3072]{1,0:T(8,128)} %param.21, f32[64,8,24,128]{3,2,1,0:T(8,128)S(1)} %bitcast.139, f32[512,3072]{1,0:T(8,128)} %param.26, f32[512,3072]{1,0:T(8,128)} %param.27), kind=kLoop, calls=%fused_computation.31 | loop fusion | flops 22020096 | bytes 47185920 | tf_op jit(solution)/shard_map/sub | solution.py:30
  633.2 175.1 %all-gather.13.cloned.1.call-done = bf16[384,128,128]{2,1,0:T(8,128)(2,1)} async-done(((bf16[48,128,128]{2,1,0:T(8,128)(2,1)}), bf16[384,128,128]{2,1,0:T(8,128)(2,1)}) %all-gather.13.cloned.1.call-update) | async-done | bytes 12582928 | tf_op jit(solution)/shard_map/all_gather | solution.py:107
  808.3 23.9 %gather_fusion.1 = bf16[768,128,128]{2,1,0:T(8,128)(2,1)} fusion(bf16[384,128,128]{2,1,0:T(8,128)(2,1)} %all-gather.13.cloned.1.call-done, s32[1024]{0:T(1024)S(1)} %pad_clamp_fusion.4), kind=kCustom, calls=%fused_computation.1.clone | custom fusion | bytes 50334720 | tf_op jit(solution)/shard_map/jit(_take)/gather | solution.py:110
  832.3 14.0 %select_select_fusion.1 = bf16[768,128,128]{2,1,0:T(8,128)(2,1)S(1)} fusion(bf16[768,128,128]{2,1,0:T(8,128)(2,1)} %gather_fusion.1, pred[768]{0:T(1024)(128)(4,1)S(1)} %compare_and_fusion.1, pred[768]{0:T(1024)(128)(4,1)S(1)} %gt.39), kind=kLoop, calls=%fused_computation.16 | loop fusion | flops 25165824 | bytes 50333184 | tf_op jit(solution)/shard_map/jit(_where)/select_n | solution.py:112
  846.3 18.1 %copy.53 = bf16[8,4,24,128,128]{4,2,3,1,0:T(8,128)(2,1)} copy(bf16[8,4,24,128,128]{4,3,2,1,0:T(8,128)(2,1)S(1)} %bitcast.127) | data formatting | bytes 50331648 | tf_op jit(solution)/shard_map/reshape;reshape | solution.py:52
  864.4 13.3 %fusion.25 = bf16[256,3072]{0,1:T(8,128)(2,1)} fusion(bf16[256,4096]{1,0:T(8,128)(2,1)S(1)} %copy-done.2, bf16[512,8,24,128]{3,2,1,0:T(8,128)(2,1)} %bitcast.134, f32[256,3072]{0,1:T(8,128)S(1)} %copy-done.1), kind=kOutput, calls=%fused_computation.40 | convolution fusion | flops 6450315264 | bytes 31981568 | tf_op jit(solution)/shard_map/dot_general | solution.py:121
  877.6 13.1 %convert_bitcast_fusion.1 = bf16[4096,3072]{0,1:T(8,128)(2,1)} fusion(bf16[256,3072]{0,1:T(8,128)(2,1)} %fusion.25, bf16[256,4096]{1,0:T(8,128)(2,1)S(1)} %copy-done.3), kind=kOutput, calls=%fused_computation.18 | convolution fusion | flops 6455033856 | bytes 28835840 | tf_op jit(solution)/shard_map/dot_general | solution.py:34
  890.7 40.5 %reshape_reshape.22 = bf16[8,4,128,24,128]{2,1,0,4,3:T(4,128)(2,1)} reshape(bf16[4096,3072]{0,1:T(8,128)(2,1)} %convert_bitcast_fusion.1) | data formatting | bytes 50331648 | tf_op jit(solution)/shard_map/reshape;reshape | solution.py:43
  931.2 38.6 %copy.57 = bf16[8,4,128,24,128]{4,2,3,1,0:T(8,128)(2,1)} copy(bf16[8,4,128,24,128]{2,1,0,4,3:T(4,128)(2,1)} %reshape_reshape.22) | data formatting | bytes 50331648 | tf_op jit(solution)/shard_map/reshape;reshape | solution.py:43
  969.8 24.7 %gather_fusion.4 = bf16[384,128,128]{2,1,0:T(8,128)(2,1)} fusion(bf16[8,96,128,128]{3,2,1,0:T(8,128)(2,1)} %bitcast.129, s32[384]{0:T(512)S(1)} %reshape.309), kind=kCustom, calls=%fused_computation.2.clone | custom fusion | bytes 25168896 | tf_op jit(solution)/shard_map/jit(take_along_axis)/gather | solution.py:134
  994.5 10.7 broadcast_select_fusion.1
  1006.6 14.1 %fusion.13 = bf16[256,4096]{1,0:T(8,128)(2,1)} fusion(bf16[256,3072]{0,1:T(8,128)(2,1)S(1)} %copy-done.4, bf16[512,8,24,128]{3,2,1,0:T(8,128)(2,1)} %bitcast.133), kind=kOutput, calls=%fused_computation.35 | convolution fusion | flops 6443499520 | bytes 28835840 | tf_op jit(solution)/shard_map/dot_general | solution.py:125
  1020.9 190.1 %reduce-scatter.6.cloned.1.call-done = bf16[1,48,128,128]{3,2,1,0:T(8,128)(2,1)} async-done(((bf16[8,48,128,128]{3,2,1,0:T(8,128)(2,1)}), bf16[1,48,128,128]{3,2,1,0:T(8,128)(2,1)}) %reduce-scatter.6.cloned.1.call-update) | async-done | bytes 1572880 | tf_op jit(solution)/shard_map/reduce_scatter | solution.py:135
  1214.8 3.6 copy.58
  1218.5 12.3 multiply_subtract_fusion.1
  1230.8 13.8 %reduce-scatter.4.cloned.1.call-done = bf16[256,1024]{1,0:T(8,128)(2,1)} async-done(((bf16[256,4096]{1,0:T(8,128)(2,1)}), bf16[256,1024]{1,0:T(8,128)(2,1)}) %reduce-scatter.4.cloned.1.call-update) | async-done | bytes 524304 | tf_op jit(solution)/shard_map/reduce_scatter | solution.py:143
  (98 shorter events, 25.4 us)
Async XLA Ops:
  7.2 190.8 %all-gather.15.cloned.1.call-start = ((), (), s32[]{:S(2)}) async-start(), calls=%async_computation.9 | async-start | bytes 14155776 | tf_op jit(solution)/shard_map/all_gather | solution.py:107
  8.2 4.4 copy-start.8
  13.2 7.1 copy-start.6
  13.2 7.2 copy-start.5
  18.7 235.5 %all-gather.11.cloned.1.call-start = ((), (), s32[]{:S(2)}) async-start(), calls=%async_computation.4 | async-start | bytes 2621440 | tf_op jit(solution)/shard_map/all_gather | solution.py:102
  19.5 247.1 %all-gather.9.cloned.1.call-start = ((), (), s32[]{:S(2)}) async-start(), calls=%async_computation.3 | async-start | bytes 2621440 | tf_op jit(solution)/shard_map/all_gather | solution.py:103
  20.2 581.3 %reduce-scatter.8.cloned.1.call-start = ((), (), s32[]{:S(2)}) async-start(), calls=%async_computation.7 | async-start | bytes 14155776 | tf_op jit(solution)/shard_map/reduce_scatter | solution.py:135
  266.5 14.4 %copy-start = (f32[256,3072]{0,1:T(8,128)}, f32[256,3072]{0,1:T(8,128)S(1)}, u32[]{:S(2)}) copy-start(f32[256,3072]{0,1:T(8,128)S(1)} %fusion.19) | copy-start | bytes 9437188
  395.8 412.6 %all-gather.13.cloned.1.call-start = ((), (), s32[]{:S(2)}) async-start(), calls=%async_computation.8 | async-start | bytes 14155776 | tf_op jit(solution)/shard_map/all_gather | solution.py:107
  632.7 578.3 %reduce-scatter.6.cloned.1.call-start = ((), (), s32[]{:S(2)}) async-start(), calls=%async_computation.6 | async-start | bytes 14155776 | tf_op jit(solution)/shard_map/reduce_scatter | solution.py:135
  846.2 18.1 %copy-start.1 = (f32[256,3072]{0,1:T(8,128)S(1)}, f32[256,3072]{0,1:T(8,128)}, u32[]{:S(2)}) copy-start(f32[256,3072]{0,1:T(8,128)} %copy-done) | copy-start | bytes 9437188
  846.3 18.1 %copy-start.2 = (bf16[256,4096]{1,0:T(8,128)(2,1)S(1)}, bf16[256,4096]{1,0:T(8,128)(2,1)}, u32[]{:S(2)}) copy-start(bf16[256,4096]{1,0:T(8,128)(2,1)} %all-gather.9.cloned.1.call-done) | copy-start | bytes 6291460
  864.3 13.3 %copy-start.3 = (bf16[256,4096]{1,0:T(8,128)(2,1)S(1)}, bf16[256,4096]{1,0:T(8,128)(2,1)}, u32[]{:S(2)}) copy-start(bf16[256,4096]{1,0:T(8,128)(2,1)} %all-gather.11.cloned.1.call-done) | copy-start | bytes 6291460
  1005.2 1.4 copy-start.4
  1005.2 15.5 %copy-start.7 = (s32[4,24]{1,0:T(4,128)S(1)}, s32[4,24]{1,0:T(4,128)}, u32[]{:S(2)}) copy-start(s32[4,24]{1,0:T(4,128)} %param.22) | copy-start | bytes 1156
  1005.3 15.6 %copy-start.9 = (s32[96]{0:T(128)S(1)}, s32[96]{0:T(128)}, u32[]{:S(2)}) copy-start(s32[96]{0:T(128)} %copy-done.8) | copy-start | bytes 1156
  1005.3 239.3 %reduce-scatter.4.cloned.1.call-start = ((), (), s32[]{:S(2)}) async-start(), calls=%async_computation.5 | async-start | bytes 2621440 | tf_op jit(solution)/shard_map/reduce_scatter | solution.py:143
  1213.5 5.0 slice-start
  1214.8 3.7 slice-start.1
Sparse Core Ops, SparseCore 0:
  18.8 179.0 all-gather.14
  199.5 20.7 all-gather.10
  221.9 22.5 all-gather.8
  395.9 205.5 reduce-scatter.7
  632.8 175.5 all-gather.12
  1005.4 205.5 reduce-scatter.5
  1214.0 30.5 reduce-scatter.3

commit v2 on v1

--- a/solution.py
+++ b/solution.py
@@ -67,10 +67,6 @@
     return jnp.cumsum(flat_mask, axis=-1) - flat_mask
 
 
-def compact(blocks, idx):
-    return jnp.take(blocks, idx, axis=-3)
-
-
 def shards(
     tokens,
     cotangent,
@@ -84,38 +80,53 @@
     second_down,
 ):
     nr, nc = mask_up.shape
+    nb = nr * nc
     block = w_up.shape[0] // nr
-    slots = (nr * nc) // 2
+    slots = nb // 2
     n_row = lax.axis_size("row")
+    width = 2 * slots + 2
+    zero_slot = 2 * slots
+    mask_slot = 2 * slots + 1
 
-    flat_up = mask_up.reshape(nr * nc)
-    flat_down = mask_down.reshape(nr * nc)
-    masks_up = lax.all_gather(flat_up, "row", axis=0)
-    masks_down = lax.all_gather(flat_down, "row", axis=0)
+    flat_up = mask_up.reshape(nb)
+    flat_down = mask_down.reshape(nb)
 
-    up_blocks = to_blocks(w_up.astype(jnp.bfloat16), block)
-    down_blocks = to_blocks(w_down.astype(jnp.bfloat16), block)
-    up_sent = compact(up_blocks, kept_index(flat_up, slots))
-    down_sent = compact(down_blocks, kept_index(flat_down, slots))
+    def pick(w, flat):
+        blocks = to_blocks(w.astype(jnp.bfloat16), block)
+        return blocks.at[kept_index(flat, slots)].get(mode="promise_in_bounds")
+
+    mask_rows = jnp.zeros((block, block), jnp.bfloat16)
+    mask_rows = mask_rows.at[0, :nb].set(flat_up.astype(jnp.bfloat16))
+    mask_rows = mask_rows.at[1, :nb].set(flat_down.astype(jnp.bfloat16))
+    sent = jnp.concatenate(
+        [
+            pick(w_up, flat_up),
+            pick(w_down, flat_down),
+            jnp.zeros((1, block, block), jnp.bfloat16),
+            mask_rows[None],
+        ],
+        axis=0,
+    )
+    got = lax.all_gather(sent, "row", axis=0)
+    masks_up = got[:, mask_slot, 0, :nb].astype(jnp.int32)
+    masks_down = got[:, mask_slot, 1, :nb].astype(jnp.int32)
+    flat_got = got.reshape((n_row * width, block, block))
 
     features, cot_rows = (
         lax.all_gather(tokens, "col", axis=1, tiled=True),
         lax.all_gather(cotangent, "col", axis=1, tiled=True),
     )
 
-    def rebuild(sent, masks):
-        got = lax.all_gather(sent, "row", axis=0)
-        flat = got.reshape((n_row * slots, block, block))
-        where = slot_of(masks) + (jnp.arange(n_row, dtype=jnp.int32) * slots)[:, None]
-        dense = jnp.take(flat, where.reshape(-1), axis=0)
-        keep = masks.reshape(-1)[:, None, None] > 0
-        dense = jnp.where(keep, dense, jnp.zeros_like(dense))
-        dense = dense.reshape((n_row, nr * nc, block, block))
+    def rebuild(masks, offset):
+        base = (jnp.arange(n_row, dtype=jnp.int32) * width)[:, None]
+        where = jnp.where(masks > 0, base + offset + slot_of(masks), base + zero_slot)
+        dense = flat_got.at[where.reshape(-1)].get(mode="promise_in_bounds")
+        dense = dense.reshape((n_row, nb, block, block))
         dense = from_blocks(dense, nr, nc)
         return dense.reshape((n_row * nr * block, nc * block))
 
-    up_whole = rebuild(up_sent, masks_up)
-    down_whole = rebuild(down_sent, masks_down)
+    up_whole = rebuild(masks_up, 0)
+    down_whole = rebuild(masks_down, slots)
 
     preact = jnp.dot(features, up_whole, preferred_element_type=jnp.float32)
     act_grad = jnp.dot(cot_rows, down_whole, preferred_element_type=jnp.float32)
@@ -127,13 +138,13 @@
     )
 
     def reduce_kept(partial, masks, own):
-        blocks = to_blocks(
-            partial.astype(jnp.bfloat16).reshape((n_row, nr * block, nc * block)), block
-        )
+        view = partial.astype(jnp.bfloat16).reshape((n_row * nr, block, nc, block))
         idx = kept_index(masks, slots)
-        sent = jnp.take_along_axis(blocks, idx[:, :, None, None], axis=1)
+        rows = (jnp.arange(n_row, dtype=jnp.int32) * nr)[:, None] + idx // nc
+        cols = idx % nc
+        sent = view.at[rows, :, cols, :].get(mode="promise_in_bounds")
         summed = lax.psum_scatter(sent, "row", scatter_dimension=0, tiled=True)[0]
-        dense = jnp.take(summed, slot_of(own), axis=0)
+        dense = summed.at[slot_of(own)].get(mode="promise_in_bounds")
         keep = own[:, None, None] > 0
         dense = jnp.where(keep, dense.astype(jnp.float32), jnp.zeros(dense.shape, jnp.float32))
         return from_blocks(dense, nr, nc)

time: 1260 us -> 1230 us (0.976)
  waiting for transfers between devices: 723 us -> 791 us
  other arithmetic: 92 us -> 43.4 us
  blocking collectives: 39 us -> 0 us
    all_gather x2 -> x1, waiting for transfers between devices: 313 us -> 491 us  [shards(): got = lax.all_gather(sent, 'row', axis=0)]
    another operation x8 -> x4, local copies, waits for them, and re-layouts: 159 us -> 1.71 us  [the longest x4 158 us: to_blocks(): x = dense.reshape(lead + (nr, block, nc, block))]
    reduce_scatter x2, waiting for transfers between devices: 395 us -> 298 us  [reduce_kept(): summed = lax.psum_scatter(sent, 'row', scatter_dimension=0, tiled=True)[0]]
    reshape x2, local copies, waits for them, and re-layouts: 0.15 us -> 67.4 us  [reduce_kept(): view = partial.astype(jnp.bfloat16).reshape((n_row * nr, block, nc, block))]
    select_n x10 -> x4, other arithmetic: 57.9 us -> 0.68 us  [the longest x1 0.64 us: reduce_kept(): dense = summed.at[slot_of(own)].get(mode='promise_in_bounds')]
    unnamed x28 -> x22, local copies, waits for them, and re-layouts: 3.24 us -> 47.9 us
    all_gather x2 -> x0, blocking collectives: 39 us -> none  [the longest x1 22.3 us: shards(): masks_down = lax.all_gather(flat_down, 'row', axis=0)]
    another operation x2, local copies, waits for them, and re-layouts: 36.1 us -> 56.8 us  [from_blocks(): x = blocks.reshape(lead + (nr, nc, block, block))]
  transfers between devices with their start and end apart: 7 -> 6, of which waited for: 5 -> 3; matrix products, arithmetic and copies ran while one was open for 8% -> 23% of each run, Pallas kernels for 0% -> 0%
where the time goes in v2:
time: 1230 us; the launch traced here: 1220 us
  waiting for transfers between devices  791 us (64%)
  local copies, waits for them, and re-layouts  307 us (25%)
  matrix products  67.6 us (5%)
  other arithmetic  43.4 us (4%)
  between operations  14.9 us (1%)
    all_gather x1, waiting for transfers between devices, shards(): got = lax.all_gather(sent, 'row', axis=0)  491 us
    reduce_scatter x2, waiting for transfers between devices, reduce_kept(): summed = lax.psum_scatter(sent, 'row', scatter_dimension=0, tiled=True)[0]  298 us
    reshape x2, local copies, waits for them, and re-layouts, reduce_kept(): view = partial.astype(jnp.bfloat16).reshape((n_row * nr, block, nc, block))  67.4 us
    another operation x2, local copies, waits for them, and re-layouts, from_blocks(): x = blocks.reshape(lead + (nr, nc, block, block))  56.8 us
    gather x2, local copies, waits for them, and re-layouts, rebuild(): dense = flat_got.at[where.reshape(-1)].get(mode='promise_in_bounds')  56 us
    gather x2, local copies, waits for them, and re-layouts, reduce_kept(): sent = view.at[rows, :, cols, :].get(mode='promise_in_bounds')  49.2 us
    unnamed x22, local copies, waits for them, and re-layouts  47.9 us
    dot_general x2, matrix products, token_product(): lax.dot_general(rows_full, other, (((0,), (0,)), ((), ())), preferred_ele...  27.7 us
  transfers between devices with their start and end apart: 6, of which 3 were waited for; matrix products, arithmetic and copies ran while one was open for 23% of the time, Pallas kernels for 0%

profile of v2, /device:TPU:0, one launch (start us, length us, event | category | flops | bytes accessed | tf_op | source)
XLA Modules:
  0.0 1224.1 jit_solution(4170883365792418980)
XLA Ops:
  10.3 3.3 convert_bitcast_fusion.2
  13.7 0.9 copy.78
  16.9 3.3 convert_bitcast_fusion.3
  20.3 0.9 copy.77
  21.7 2.5 copy.65
  24.3 1.9 gather_fusion.1
  26.2 2.7 gather_fusion
  29.2 4.0 pad_maximum_fusion
  35.2 491.1 %all-gather.9.cloned.1.call-done = bf16[784,128,128]{2,1,0:T(8,128)(2,1)} async-done(((bf16[98,128,128]{2,1,0:T(8,128)(2,1)}), bf16[784,128,128]{2,1,0:T(8,128)(2,1)}) %all-gather.9.cloned.1.call-update) | async-done | bytes 25690128 | tf_op jit(solution)/shard_map/all_gather | solution.py:110
  528.8 28.5 %gather_fusion.2 = bf16[768,128,128]{2,1,0:T(8,128)(2,1)} fusion(bf16[784,128,128]{2,1,0:T(8,128)(2,1)} %all-gather.9.cloned.1.call-done, s32[1024]{0:T(1024)S(1)} %pad_clamp_fusion.3), kind=kCustom, calls=%fused_computation.2 | custom fusion | bytes 50334720 | tf_op jit(solution)/shard_map/gather | solution.py:123
  557.3 28.5 %copy.69 = bf16[8,4,24,128,128]{4,2,3,1,0:T(8,128)(2,1)} copy(bf16[8,4,24,128,128]{4,3,2,1,0:T(8,128)(2,1)} %bitcast.157) | data formatting | bytes 50331648 | tf_op jit(solution)/shard_map/reshape;reshape | solution.py:52
  585.8 27.5 %gather_fusion.3 = bf16[768,128,128]{2,1,0:T(8,128)(2,1)} fusion(bf16[784,128,128]{2,1,0:T(8,128)(2,1)} %all-gather.9.cloned.1.call-done, s32[1024]{0:T(1024)S(1)} %pad_clamp_fusion.2), kind=kCustom, calls=%fused_computation.3 | custom fusion | bytes 50334720 | tf_op jit(solution)/shard_map/gather | solution.py:123
  613.3 28.3 %copy.70 = bf16[8,4,24,128,128]{4,2,3,1,0:T(8,128)(2,1)} copy(bf16[8,4,24,128,128]{4,3,2,1,0:T(8,128)(2,1)} %bitcast.156) | data formatting | bytes 50331648 | tf_op jit(solution)/shard_map/reshape;reshape | solution.py:52
  642.1 12.2 fusion.21
  654.4 14.1 %fusion.27 = bf16[256,3072]{0,1:T(8,128)(2,1)} fusion(bf16[256,4096]{1,0:T(8,128)(2,1)} %all-gather.5.cloned.1.call-done, bf16[512,8,24,128]{3,2,1,0:T(8,128)(2,1)} %bitcast.166, f32[256,3072]{0,1:T(8,128)S(1)} %fusion.21), kind=kOutput, calls=%fused_computation.38 | convolution fusion | flops 6450315264 | bytes 31981568 | tf_op jit(solution)/shard_map/dot_general | solution.py:132
  668.5 13.4 %convert_bitcast_fusion.1 = bf16[384,8,32,128]{3,1,2,0:T(8,128)(2,1)} fusion(bf16[256,3072]{0,1:T(8,128)(2,1)} %fusion.27, bf16[256,4096]{1,0:T(8,128)(2,1)} %all-gather.7.cloned.1.call-done), kind=kOutput, calls=%fused_computation.16 | convolution fusion | flops 6455033856 | bytes 28835840 | tf_op jit(solution)/shard_map/dot_general | solution.py:34
  681.9 22.4 %copy.81 = bf16[384,8,32,128]{3,2,1,0:T(8,128)(2,1)} copy(bf16[384,8,32,128]{3,1,2,0:T(8,128)(2,1)} %convert_bitcast_fusion.1) | data formatting | bytes 50331648
  704.3 34.4 %copy.71 = bf16[32,128,24,128]{3,1,2,0:T(8,128)(2,1)} copy(bf16[32,128,24,128]{1,0,3,2:T(8,128)(2,1)} %bitcast.158) | data formatting | bytes 50331648 | tf_op jit(solution)/shard_map/reshape | solution.py:141
  738.9 24.6 %gather_fusion.4 = bf16[384,128,128]{2,1,0:T(8,128)(2,1)} fusion(bf16[32,128,24,128]{3,1,2,0:T(8,128)(2,1)} %copy.71, s32[384]{0:T(512)S(1)} %reshape.620), kind=kCustom, calls=%fused_computation.4 | custom fusion | bytes 25168896 | tf_op jit(solution)/shard_map/gather | solution.py:145
  763.5 14.3 %convert_bitcast_fusion = bf16[384,8,32,128]{3,1,2,0:T(8,128)(2,1)} fusion(bf16[256,4096]{1,0:T(8,128)(2,1)} %all-gather.5.cloned.1.call-done, f32[256,3072]{0,1:T(8,128)S(1)} %fusion.21), kind=kOutput, calls=%fused_computation.15 | convolution fusion | flops 6458966016 | bytes 30408704 | tf_op jit(solution)/shard_map/dot_general | solution.py:34
  777.8 22.5 %copy.83 = bf16[384,8,32,128]{3,2,1,0:T(8,128)(2,1)} copy(bf16[384,8,32,128]{3,1,2,0:T(8,128)(2,1)} %convert_bitcast_fusion) | data formatting | bytes 50331648
  800.3 33.0 %copy.74 = bf16[32,128,24,128]{3,1,2,0:T(8,128)(2,1)} copy(bf16[32,128,24,128]{1,0,3,2:T(8,128)(2,1)} %bitcast.159) | data formatting | bytes 50331648 | tf_op jit(solution)/shard_map/reshape | solution.py:141
  833.3 24.6 %gather_fusion.6 = bf16[384,128,128]{2,1,0:T(8,128)(2,1)} fusion(bf16[32,128,24,128]{3,1,2,0:T(8,128)(2,1)} %copy.74, s32[384]{0:T(512)S(1)} %reshape.634), kind=kCustom, calls=%fused_computation.6 | custom fusion | bytes 25168896 | tf_op jit(solution)/shard_map/gather | solution.py:145
  859.4 13.6 %fusion.15 = bf16[256,4096]{1,0:T(8,128)(2,1)} fusion(bf16[256,3072]{0,1:T(8,128)(2,1)S(1)} %copy-done, bf16[512,8,24,128]{3,2,1,0:T(8,128)(2,1)} %bitcast.165), kind=kOutput, calls=%fused_computation.33 | convolution fusion | flops 6443499520 | bytes 28835840 | tf_op jit(solution)/shard_map/dot_general | solution.py:136
  873.0 97.9 %reduce-scatter.6.cloned.1.call-done = bf16[1,48,128,128]{3,2,1,0:T(8,128)(2,1)} async-done(((bf16[8,48,128,128]{3,2,1,0:T(8,128)(2,1)}), bf16[1,48,128,128]{3,2,1,0:T(8,128)(2,1)}) %reduce-scatter.6.cloned.1.call-update) | async-done | bytes 1572880 | tf_op jit(solution)/shard_map/reduce_scatter | solution.py:146
  970.9 2.6 gather_fusion.5
  974.0 6.3 copy.73
  980.3 200.4 %reduce-scatter.8.cloned.1.call-done = bf16[1,48,128,128]{3,2,1,0:T(8,128)(2,1)} async-done(((bf16[8,48,128,128]{3,2,1,0:T(8,128)(2,1)}), bf16[1,48,128,128]{3,2,1,0:T(8,128)(2,1)}) %reduce-scatter.8.cloned.1.call-update) | async-done | bytes 1572880 | tf_op jit(solution)/shard_map/reduce_scatter | solution.py:146
  1180.8 2.6 gather_fusion.7
  1183.9 6.3 copy.76
  1190.2 13.6 %multiply_subtract_fusion.1 = (f32[512,3072]{1,0:T(8,128)}, f32[512,3072]{1,0:T(8,128)}, f32[512,3072]{1,0:T(8,128)}) fusion(f32[512,3072]{1,0:T(8,128)S(1)} %bitcast.168, f32[64,8,24,128]{3,2,1,0:T(8,128)} %bitcast.171, f32[512,3072]{1,0:T(8,128)} %param.20, f32[512,3072]{1,0:T(8,128)} %param.21), kind=kLoop, calls=%fused_computation.32 | loop fusion | flops 20447232 | bytes 44040192 | tf_op jit(solution)/shard_map/sub | solution.py:30
  1203.8 13.0 %multiply_subtract_fusion = (f32[512,3072]{1,0:T(8,128)}, f32[512,3072]{1,0:T(8,128)}, f32[512,3072]{1,0:T(8,128)}) fusion(f32[512,3072]{1,0:T(8,128)S(1)} %bitcast.170, f32[64,8,24,128]{3,2,1,0:T(8,128)} %bitcast.172, f32[512,3072]{1,0:T(8,128)} %param.22, f32[512,3072]{1,0:T(8,128)} %param.23), kind=kLoop, calls=%fused_computation.31 | loop fusion | flops 20447232 | bytes 44040192 | tf_op jit(solution)/shard_map/sub | solution.py:30
  (88 shorter events, 14.0 us)
Async XLA Ops:
  7.2 519.1 %all-gather.9.cloned.1.call-start = ((), (), s32[]{:S(2)}) async-start(), calls=%async_computation.8 | async-start | bytes 28901376 | tf_op jit(solution)/shard_map/all_gather | solution.py:110
  33.2 608.9 %all-gather.7.cloned.1.call-start = ((), (), s32[]{:S(2)}) async-start(), calls=%async_computation.4 | async-start | bytes 2621440 | tf_op jit(solution)/shard_map/all_gather | solution.py:116
  33.9 620.4 %all-gather.5.cloned.1.call-start = ((), (), s32[]{:S(2)}) async-start(), calls=%async_computation.3 | async-start | bytes 2621440 | tf_op jit(solution)/shard_map/all_gather | solution.py:117
  34.7 936.3 %reduce-scatter.6.cloned.1.call-start = ((), (), s32[]{:S(2)}) async-start(), calls=%async_computation.6 | async-start | bytes 14155776 | tf_op jit(solution)/shard_map/reduce_scatter | solution.py:146
  763.5 417.3 %reduce-scatter.8.cloned.1.call-start = ((), (), s32[]{:S(2)}) async-start(), calls=%async_computation.7 | async-start | bytes 14155776 | tf_op jit(solution)/shard_map/reduce_scatter | solution.py:146
  857.9 0.7 copy-start.4
  857.9 0.7 copy-start.3
  858.0 0.7 copy-start.1
  858.0 0.7 copy-start.2
  858.0 1.5 copy-start
  858.0 358.8 %reduce-scatter.4.cloned.1.call-start = ((), (), s32[]{:S(2)}) async-start(), calls=%async_computation.5 | async-start | bytes 2621440 | tf_op jit(solution)/shard_map/reduce_scatter | solution.py:154
  1183.3 6.8 slice-start
  1183.9 6.3 slice-start.1
  1183.9 19.9 %slice-start.2 = ((s8[6291456]{0:T(1024)(128)(4,1)}), s8[4194304]{0:T(1024)(128)(4,1)S(1)}, s32[]{:S(2)}) async-start(s8[6291456]{0:T(1024)(128)(4,1)} %bitcast.169), calls=%async_computation.11 | async-start | bytes 8388608
  1190.2 13.6 %slice-start.3 = ((s8[6291456]{0:T(1024)(128)(4,1)}), s8[2097152]{0:T(1024)(128)(4,1)S(1)}, s32[]{:S(2)}) async-start(s8[6291456]{0:T(1024)(128)(4,1)} %bitcast.169), calls=%async_computation.12 | async-start | bytes 4194304
Sparse Core Ops, SparseCore 0:
  33.3 492.9 all-gather.8
  527.9 22.5 all-gather.6
  552.0 22.5 all-gather.4
  763.6 207.2 reduce-scatter.5
  974.4 206.3 reduce-scatter.7
  1183.7 30.5 reduce-scatter.3

commit v3 on v2

--- a/solution.py
+++ b/solution.py
@@ -84,49 +84,53 @@
     block = w_up.shape[0] // nr
     slots = nb // 2
     n_row = lax.axis_size("row")
-    width = 2 * slots + 2
-    zero_slot = 2 * slots
-    mask_slot = 2 * slots + 1
+    me = lax.axis_index("row")
+    width = slots + 2
+    zero_slot = slots
+    mask_slot = slots + 1
+    rows_n = jnp.arange(n_row, dtype=jnp.int32)
 
     flat_up = mask_up.reshape(nb)
     flat_down = mask_down.reshape(nb)
 
-    def pick(w, flat):
+    def package(w, flat):
         blocks = to_blocks(w.astype(jnp.bfloat16), block)
-        return blocks.at[kept_index(flat, slots)].get(mode="promise_in_bounds")
+        kept = blocks.at[kept_index(flat, slots)].get(mode="promise_in_bounds")
+        mask_rows = jnp.zeros((block, block), jnp.bfloat16)
+        mask_rows = mask_rows.at[0, :nb].set(flat.astype(jnp.bfloat16))
+        return jnp.concatenate(
+            [kept, jnp.zeros((1, block, block), jnp.bfloat16), mask_rows[None]], axis=0
+        )
 
-    mask_rows = jnp.zeros((block, block), jnp.bfloat16)
-    mask_rows = mask_rows.at[0, :nb].set(flat_up.astype(jnp.bfloat16))
-    mask_rows = mask_rows.at[1, :nb].set(flat_down.astype(jnp.bfloat16))
-    sent = jnp.concatenate(
-        [
-            pick(w_up, flat_up),
-            pick(w_down, flat_down),
-            jnp.zeros((1, block, block), jnp.bfloat16),
-            mask_rows[None],
-        ],
-        axis=0,
+    def shift_perm(s):
+        return [(i, (i + s) % n_row) for i in range(n_row)]
+
+    got_up = lax.all_gather(package(w_up, flat_up), "row", axis=0)
+    sent_down = package(w_down, flat_down)
+    got_down = jnp.stack(
+        [sent_down]
+        + [lax.ppermute(sent_down, "row", shift_perm(s)) for s in range(1, n_row)]
     )
-    got = lax.all_gather(sent, "row", axis=0)
-    masks_up = got[:, mask_slot, 0, :nb].astype(jnp.int32)
-    masks_down = got[:, mask_slot, 1, :nb].astype(jnp.int32)
-    flat_got = got.reshape((n_row * width, block, block))
+    pos_down = (me - rows_n) % n_row
+    masks_up = got_up[:, mask_slot, 0, :nb].astype(jnp.int32)
+    masks_down = got_down[pos_down, mask_slot, 0, :nb].astype(jnp.int32)
 
     features, cot_rows = (
         lax.all_gather(tokens, "col", axis=1, tiled=True),
         lax.all_gather(cotangent, "col", axis=1, tiled=True),
     )
 
-    def rebuild(masks, offset):
-        base = (jnp.arange(n_row, dtype=jnp.int32) * width)[:, None]
-        where = jnp.where(masks > 0, base + offset + slot_of(masks), base + zero_slot)
+    def rebuild(got, masks, pos):
+        flat_got = got.reshape((n_row * width, block, block))
+        base = (pos * width)[:, None]
+        where = jnp.where(masks > 0, base + slot_of(masks), base + zero_slot)
         dense = flat_got.at[where.reshape(-1)].get(mode="promise_in_bounds")
         dense = dense.reshape((n_row, nb, block, block))
         dense = from_blocks(dense, nr, nc)
         return dense.reshape((n_row * nr * block, nc * block))
 
-    up_whole = rebuild(masks_up, 0)
-    down_whole = rebuild(masks_down, slots)
+    up_whole = rebuild(got_up, masks_up, rows_n)
+    down_whole = rebuild(got_down, masks_down, pos_down)
 
     preact = jnp.dot(features, up_whole, preferred_element_type=jnp.float32)
     act_grad = jnp.dot(cot_rows, down_whole, preferred_element_type=jnp.float32)
@@ -137,20 +141,28 @@
         pre_grad, up_whole, (((1,), (1,)), ((), ())), preferred_element_type=jnp.float32
     )
 
-    def reduce_kept(partial, masks, own):
+    def kept_blocks(partial, masks, dest):
         view = partial.astype(jnp.bfloat16).reshape((n_row * nr, block, nc, block))
         idx = kept_index(masks, slots)
-        rows = (jnp.arange(n_row, dtype=jnp.int32) * nr)[:, None] + idx // nc
+        rows = (dest * nr)[:, None] + idx // nc
         cols = idx % nc
-        sent = view.at[rows, :, cols, :].get(mode="promise_in_bounds")
-        summed = lax.psum_scatter(sent, "row", scatter_dimension=0, tiled=True)[0]
+        return view.at[rows, :, cols, :].get(mode="promise_in_bounds")
+
+    def unpack(summed, own):
         dense = summed.at[slot_of(own)].get(mode="promise_in_bounds")
         keep = own[:, None, None] > 0
         dense = jnp.where(keep, dense.astype(jnp.float32), jnp.zeros(dense.shape, jnp.float32))
         return from_blocks(dense, nr, nc)
 
-    grad_down = reduce_kept(token_product(cot_rows, activation), masks_down, flat_down)
-    grad_up = reduce_kept(token_product(features, pre_grad), masks_up, flat_up)
+    sent = kept_blocks(token_product(cot_rows, activation), masks_down, rows_n)
+    grad_down = unpack(lax.psum_scatter(sent, "row", scatter_dimension=0, tiled=True)[0], flat_down)
+    dest = (me + rows_n) % n_row
+    sent = kept_blocks(token_product(features, pre_grad), masks_up[dest], dest)
+    total = sent[0].astype(jnp.float32)
+    for s in range(1, n_row):
+        total = total + lax.ppermute(sent[s], "row", shift_perm(s)).astype(jnp.float32)
+    grad_up = unpack(total, flat_up)
+
     token_grad = lax.psum_scatter(
         partial_tokens.astype(jnp.bfloat16), "col", scatter_dimension=1, tiled=True
     )

time: 1230 us -> 1240 us (level)
  waiting for transfers between devices: 791 us -> 600 us
  starting transfers between devices: 0.24 us -> 135 us
  local copies, waits for them, and re-layouts: 307 us -> 360 us
    ppermute x0 -> x14, waiting for transfers between devices: none -> 515 us  [the longest x7 292 us: shards(): lax.ppermute(sent[s], 'row', shift_perm(s)).astype(jnp.float32)]
    all_gather x1, waiting for transfers between devices: 491 us -> 46.7 us  [shards(): got_up = lax.all_gather(package(w_up, flat_up), 'row', axis=0)]
    reduce_scatter x2 -> x1, waiting for transfers between devices: 298 us -> 0.01 us  [shards(): lax.psum_scatter(sent, 'row', scatter_dimension=0, tiled=True)[0]]
    ppermute x0 -> x14, starting transfers between devices: none -> 135 us  [the longest x7 73.7 us: shards(): lax.ppermute(sent_down, 'row', shift_perm(s))]
    gather x6 -> x39, local copies, waits for them, and re-layouts: 59 us -> 93.8 us  [the longest x2 49.8 us: kept_blocks(): return view.at[rows, :, cols, :].get(mode='promise_in_bounds')]
    another operation x2 -> x1, local copies, waits for them, and re-layouts: 56.8 us -> 28.3 us  [from_blocks(): x = blocks.reshape(lead + (nr, nc, block, block))]
    all_gather x1, waiting for transfers between devices: 0.02 us -> 25.9 us  [shards(): lax.all_gather(tokens, 'col', axis=1, tiled=True)]
    transpose x2 -> x3, local copies, waits for them, and re-layouts: 12.6 us -> 35.7 us  [from_blocks(): x = jnp.moveaxis(x, k + 1, k + 2)]
  transfers between devices with their start and end apart: 6 -> 19, of which waited for: 3 -> 12; matrix products, arithmetic and copies ran while one was open for 23% -> 29% of each run, Pallas kernels for 0% -> 0%
where the time goes in v3:
time: 1240 us; the launch traced here: 1230 us
  waiting for transfers between devices  600 us (48%)
  local copies, waits for them, and re-layouts  360 us (29%)
  starting transfers between devices  135 us (11%)
  matrix products  67 us (5%)
  other arithmetic  48.4 us (4%)
  between operations  14.5 us (1%)
    ppermute x7, waiting for transfers between devices, shards(): lax.ppermute(sent[s], 'row', shift_perm(s)).astype(jnp.float32)  292 us
    ppermute x7, waiting for transfers between devices, shards(): lax.ppermute(sent_down, 'row', shift_perm(s))  224 us
    ppermute x7, starting transfers between devices, shards(): lax.ppermute(sent_down, 'row', shift_perm(s))  73.7 us
    reshape x2, local copies, waits for them, and re-layouts, kept_blocks(): view = partial.astype(jnp.bfloat16).reshape((n_row * nr, block, nc, block))  66.9 us
    unnamed x40, local copies, waits for them, and re-layouts  61.5 us
    ppermute x7, starting transfers between devices, shards(): lax.ppermute(sent[s], 'row', shift_perm(s)).astype(jnp.float32)  61.1 us
    gather x2, local copies, waits for them, and re-layouts, rebuild(): dense = flat_got.at[where.reshape(-1)].get(mode='promise_in_bounds')  56.6 us
    gather x2, local copies, waits for them, and re-layouts, kept_blocks(): return view.at[rows, :, cols, :].get(mode='promise_in_bounds')  49.8 us
  transfers between devices with their start and end apart: 19, of which 12 were waited for; matrix products, arithmetic and copies ran while one was open for 29% of the time, Pallas kernels for 0%

profile of v3, /device:TPU:0, one launch (start us, length us, event | category | flops | bytes accessed | tf_op | source)
XLA Modules:
  0.0 1225.1 jit_solution(1312161481749535863)
XLA Ops:
  47.1 56.8 %collective-permute-done = bf16[50,128,128]{2,1,0:T(8,128)(2,1)} collective-permute-done((bf16[50,128,128]{2,1,0:T(8,128)(2,1)}, bf16[50,128,128]{2,1,0:T(8,128)(2,1)}, u32[]{:S(2)}, u32[]{:S(2)}) %collective-permute-start) | collective-permute-done | bytes 1638432 | tf_op jit(solution)/shard_map/ppermute | solution.py:112
  103.9 24.4 %collective-permute-start.5 = (bf16[50,128,128]{2,1,0:T(8,128)(2,1)S(1)}, bf16[50,128,128]{2,1,0:T(8,128)(2,1)S(1)}, u32[]{:S(2)}, u32[]{:S(2)}) collective-permute-start(bf16[50,128,128]{2,1,0:T(8,128)(2,1)S(1)} %copy-done.3), channel_id=1, source_target_pairs={{0,24},{4,28},{8,0},{12,4},{16,8},{20,12},{24,16},{28,20},{1,25},{... | collective-permute-start | bytes 4915208 | tf_op jit(solution)/shard_map/ppermute | solution.py:112
  128.3 38.3 %collective-permute-start.6 = (bf16[50,128,128]{2,1,0:T(8,128)(2,1)S(1)}, bf16[50,128,128]{2,1,0:T(8,128)(2,1)S(1)}, u32[]{:S(2)}, u32[]{:S(2)}) collective-permute-start(bf16[50,128,128]{2,1,0:T(8,128)(2,1)S(1)} %copy-done.3), channel_id=1, source_target_pairs={{0,28},{4,0},{8,4},{12,8},{16,12},{20,16},{24,20},{28,24},{1,29},{... | collective-permute-start | bytes 4915208 | tf_op jit(solution)/shard_map/ppermute | solution.py:112
  170.1 103.9 %collective-permute-done.2 = bf16[50,128,128]{2,1,0:T(8,128)(2,1)} collective-permute-done((bf16[50,128,128]{2,1,0:T(8,128)(2,1)}, bf16[50,128,128]{2,1,0:T(8,128)(2,1)}, u32[]{:S(2)}, u32[]{:S(2)}) %collective-permute-start.2) | collective-permute-done | bytes 1638432 | tf_op jit(solution)/shard_map/ppermute | solution.py:112
  281.6 60.6 %collective-permute-done.6 = bf16[50,128,128]{2,1,0:T(8,128)(2,1)S(1)} collective-permute-done((bf16[50,128,128]{2,1,0:T(8,128)(2,1)S(1)}, bf16[50,128,128]{2,1,0:T(8,128)(2,1)S(1)}, u32[]{:S(2)}, u32[]{:S(2)}) %collective-permute-start.6) | collective-permute-done | bytes 1638432 | tf_op jit(solution)/shard_map/ppermute | solution.py:112
  347.1 32.0 %while.3 = (s32[]{:T(128)}, bf16[8,50,128,128]{3,2,1,0:T(8,128)(2,1)}, s32[8,4]{0,1:T(4,128)S(1)}, bf16[8,96]{1,0:T(8,128)(2,1)S(1)}, s32[]{:T(128)}, /*index=5*/s32[]{:T(128)}) while((s32[]{:T(128)}, bf16[8,50,128,128]{3,2,1,0:T(8,128)(2,1)}, s32[8,4]{0,1:T(4,128)S(1)}, bf16[8,96]{1,0:T(8,128)(2,1)S(1)}, s32[]{:T(128)}, /*index=5*/s32[]{:T(128)}) %tuple.63), condition=%wide.while_cond.2, body=%wide.while_body.2.sunk | while | flops 2 | bytes 933 | solution.py:116
  379.8 46.7 %all-gather.9.cloned.1.call-done = bf16[400,128,128]{2,1,0:T(8,128)(2,1)} async-done(((bf16[50,128,128]{2,1,0:T(8,128)(2,1)}), bf16[400,128,128]{2,1,0:T(8,128)(2,1)}) %all-gather.9.cloned.1.call-update) | async-done | bytes 13107216 | tf_op jit(solution)/shard_map/all_gather | solution.py:108
  427.7 23.9 %gather_fusion.3 = bf16[768,128,128]{2,1,0:T(8,128)(2,1)} fusion(bf16[400,128,128]{2,1,0:T(8,128)(2,1)} %all-gather.9.cloned.1.call-done, s32[1024]{0:T(1024)S(1)} %pad_clamp_fusion.3), kind=kCustom, calls=%fused_computation.3 | custom fusion | bytes 50334720 | tf_op jit(solution)/shard_map/gather | solution.py:127
  451.6 28.3 %copy.74 = bf16[8,4,24,128,128]{4,2,3,1,0:T(8,128)(2,1)} copy(bf16[8,4,24,128,128]{4,3,2,1,0:T(8,128)(2,1)} %bitcast.192) | data formatting | bytes 50331648 | tf_op jit(solution)/shard_map/reshape;reshape | solution.py:52
  479.9 25.9 %all-gather.7.cloned.1.call-done = bf16[256,4096]{1,0:T(8,128)(2,1)} async-done(((bf16[256,1024]{1,0:T(8,128)(2,1)}), bf16[256,4096]{1,0:T(8,128)(2,1)}) %all-gather.7.cloned.1.call-update) | async-done | bytes 2097168 | tf_op jit(solution)/shard_map/all_gather | solution.py:119
  505.8 12.9 %fusion.20 = f32[256,3072]{0,1:T(8,128)S(1)} fusion(bf16[256,4096]{1,0:T(8,128)(2,1)} %all-gather.7.cloned.1.call-done, bf16[512,8,24,128]{3,2,1,0:T(8,128)(2,1)} %bitcast.199), kind=kOutput, calls=%fused_computation.38 | convolution fusion | flops 6442450944 | bytes 30408704 | tf_op jit(solution)/shard_map/dot_general | solution.py:135
  518.7 11.3 all-gather.5.cloned.1.call-done
  529.9 13.3 %convert_bitcast_fusion = bf16[384,8,32,128]{3,1,2,0:T(8,128)(2,1)} fusion(bf16[256,4096]{1,0:T(8,128)(2,1)} %all-gather.5.cloned.1.call-done, f32[256,3072]{0,1:T(8,128)S(1)} %fusion.20), kind=kOutput, calls=%fused_computation.18 | convolution fusion | flops 6458966016 | bytes 30408704 | tf_op jit(solution)/shard_map/dot_general | solution.py:34
  543.2 22.4 %copy.88 = bf16[384,8,32,128]{3,2,1,0:T(8,128)(2,1)} copy(bf16[384,8,32,128]{3,1,2,0:T(8,128)(2,1)} %convert_bitcast_fusion) | data formatting | bytes 50331648
  565.6 32.4 %copy.78 = bf16[32,128,24,128]{3,1,2,0:T(8,128)(2,1)} copy(bf16[32,128,24,128]{1,0,3,2:T(8,128)(2,1)} %bitcast.194) | data formatting | bytes 50331648 | tf_op jit(solution)/shard_map/reshape | solution.py:145
  598.0 24.6 %gather_fusion.7 = bf16[384,128,128]{2,1,0:T(8,128)(2,1)} fusion(bf16[32,128,24,128]{3,1,2,0:T(8,128)(2,1)} %copy.78, s32[384]{0:T(512)S(1)} %reshape.777), kind=kCustom, calls=%fused_computation.7 | custom fusion | bytes 25168896 | tf_op jit(solution)/shard_map/gather | solution.py:149
  622.9 32.6 %gather_fusion.1 = bf16[768,128,128]{2,1,0:T(8,128)(2,1)} fusion(bf16[400,128,128]{2,1,0:T(8,128)(2,1)} %bitcast.196, s32[1024]{0:T(1024)S(1)} %pad_clamp_fusion.5), kind=kCustom, calls=%fused_computation.1 | custom fusion | bytes 50334720 | tf_op jit(solution)/shard_map/gather | solution.py:127
  655.6 28.4 %copy.70 = bf16[8,4,128,24,128]{4,3,2,1,0:T(8,128)(2,1)} copy(bf16[8,4,128,24,128]{4,2,3,1,0:T(8,128)(2,1)} %bitcast.193) | data formatting | bytes 50331648 | tf_op jit(solution)/shard_map/transpose | solution.py:54
  684.0 13.9 %fusion.26 = bf16[256,3072]{0,1:T(8,128)(2,1)} fusion(bf16[256,4096]{1,0:T(8,128)(2,1)S(1)} %copy-done.1, bf16[512,8,24,128]{3,2,1,0:T(8,128)(2,1)} %bitcast.201, f32[256,3072]{0,1:T(8,128)S(1)} %fusion.20), kind=kOutput, calls=%fused_computation.40 | convolution fusion | flops 6450315264 | bytes 31981568 | tf_op jit(solution)/shard_map/dot_general | solution.py:136
  697.9 13.6 %convert_bitcast_fusion.1 = bf16[384,8,32,128]{3,1,2,0:T(8,128)(2,1)} fusion(bf16[256,3072]{0,1:T(8,128)(2,1)} %fusion.26, bf16[256,4096]{1,0:T(8,128)(2,1)} %all-gather.7.cloned.1.call-done), kind=kOutput, calls=%fused_computation.19 | convolution fusion | flops 6455033856 | bytes 28835840 | tf_op jit(solution)/shard_map/dot_general | solution.py:34
  711.5 22.7 %copy.86 = bf16[384,8,32,128]{3,2,1,0:T(8,128)(2,1)} copy(bf16[384,8,32,128]{3,1,2,0:T(8,128)(2,1)} %convert_bitcast_fusion.1) | data formatting | bytes 50331648
  734.2 34.6 %copy.75 = bf16[32,128,24,128]{3,1,2,0:T(8,128)(2,1)} copy(bf16[32,128,24,128]{1,0,3,2:T(8,128)(2,1)} %bitcast.195) | data formatting | bytes 50331648 | tf_op jit(solution)/shard_map/reshape | solution.py:145
  769.9 25.1 %gather_fusion.5 = bf16[384,128,128]{2,1,0:T(8,128)(2,1)} fusion(bf16[32,128,24,128]{3,1,2,0:T(8,128)(2,1)} %copy.75, s32[384]{0:T(512)S(1)} %reshape.763), kind=kCustom, calls=%fused_computation.5 | custom fusion | bytes 25168896 | tf_op jit(solution)/shard_map/gather | solution.py:149
  795.1 7.4 fusion.80
  802.5 58.0 %collective-permute-start.13 = (bf16[48,128,128]{2,1,0:T(8,128)(2,1)S(1)}, bf16[48,128,128]{2,1,0:T(8,128)(2,1)}, u32[]{:S(2)}, u32[]{:S(2)}) collective-permute-start(bf16[48,128,128]{2,1,0:T(8,128)(2,1)S(1)} %get-tuple-element.67), channel_id=1, source_target_pairs={{0,28},{4,0},{8,4},{12,8},{16,12},{20,16},{24,20},{28,24},{1,29},{... | collective-permute-start | bytes 4718600 | tf_op jit(solution)/shard_map/ppermute | solution.py:163
  863.7 65.3 %collective-permute-done.13 = bf16[48,128,128]{2,1,0:T(8,128)(2,1)} collective-permute-done((bf16[48,128,128]{2,1,0:T(8,128)(2,1)S(1)}, bf16[48,128,128]{2,1,0:T(8,128)(2,1)}, u32[]{:S(2)}, u32[]{:S(2)}) %collective-permute-start.13) | collective-permute-done | bytes 1572896 | tf_op jit(solution)/shard_map/ppermute | solution.py:163
  929.0 35.6 %collective-permute-done.12 = bf16[48,128,128]{2,1,0:T(8,128)(2,1)S(1)} collective-permute-done((bf16[48,128,128]{2,1,0:T(8,128)(2,1)S(1)}, bf16[48,128,128]{2,1,0:T(8,128)(2,1)S(1)}, u32[]{:S(2)}, u32[]{:S(2)}) %collective-permute-start.12) | collective-permute-done | bytes 1572896 | tf_op jit(solution)/shard_map/ppermute | solution.py:163
  965.8 13.4 %fusion.14 = bf16[256,4096]{1,0:T(8,128)(2,1)} fusion(bf16[256,3072]{0,1:T(8,128)(2,1)S(1)} %copy-done.2, bf16[512,8,24,128]{3,2,1,0:T(8,128)(2,1)} %bitcast.200), kind=kOutput, calls=%fused_computation.35 | convolution fusion | flops 6443499520 | bytes 28835840 | tf_op jit(solution)/shard_map/dot_general | solution.py:140
  979.2 19.3 %collective-permute-done.11 = bf16[48,128,128]{2,1,0:T(8,128)(2,1)} collective-permute-done((bf16[48,128,128]{2,1,0:T(8,128)(2,1)}, bf16[48,128,128]{2,1,0:T(8,128)(2,1)}, u32[]{:S(2)}, u32[]{:S(2)}) %collective-permute-start.11) | collective-permute-done | bytes 1572896 | tf_op jit(solution)/shard_map/ppermute | solution.py:163
  998.5 170.8 %collective-permute-done.10 = bf16[48,128,128]{2,1,0:T(8,128)(2,1)} collective-permute-done((bf16[48,128,128]{2,1,0:T(8,128)(2,1)}, bf16[48,128,128]{2,1,0:T(8,128)(2,1)}, u32[]{:S(2)}, u32[]{:S(2)}) %collective-permute-start.10) | collective-permute-done | bytes 1572896 | tf_op jit(solution)/shard_map/ppermute | solution.py:163
  1188.4 11.7 multiply_subtract_fusion.1
  1206.8 11.5 multiply_subtract_fusion
  (178 shorter events, 120.6 us)
Async XLA Ops:
  7.2 419.3 %all-gather.9.cloned.1.call-start = ((), (), s32[]{:S(2)}) async-start(), calls=%async_computation.6 | async-start | bytes 14745600 | tf_op jit(solution)/shard_map/all_gather | solution.py:108
  34.2 69.7 %copy-start.3 = (bf16[50,128,128]{2,1,0:T(8,128)(2,1)S(1)}, bf16[50,128,128]{2,1,0:T(8,128)(2,1)}, u32[]{:S(2)}) copy-start(bf16[50,128,128]{2,1,0:T(8,128)(2,1)} %get-tuple-element.71) | copy-start | bytes 4915204
  34.2 471.5 %all-gather.7.cloned.1.call-start = ((), (), s32[]{:S(2)}) async-start(), calls=%async_computation.3 | async-start | bytes 2621440 | tf_op jit(solution)/shard_map/all_gather | solution.py:119
  35.0 494.9 %all-gather.5.cloned.1.call-start = ((), (), s32[]{:S(2)}) async-start(), calls=%async_computation.2 | async-start | bytes 2621440 | tf_op jit(solution)/shard_map/all_gather | solution.py:120
  35.0 68.9 %collective-permute-start = (bf16[50,128,128]{2,1,0:T(8,128)(2,1)}, bf16[50,128,128]{2,1,0:T(8,128)(2,1)}, u32[]{:S(2)}, u32[]{:S(2)}) collective-permute-start(bf16[50,128,128]{2,1,0:T(8,128)(2,1)} %get-tuple-element.71), channel_id=1, source_target_pairs={{0,4},{4,8},{8,12},{12,16},{16,20},{20,24},{24,28},{28,0},{1,5},{5... | collective-permute-start | bytes 4915208 | tf_op jit(solution)/shard_map/ppermute | solution.py:112
  38.1 90.3 %collective-permute-start.1 = (bf16[50,128,128]{2,1,0:T(8,128)(2,1)}, bf16[50,128,128]{2,1,0:T(8,128)(2,1)}, u32[]{:S(2)}, u32[]{:S(2)}) collective-permute-start(bf16[50,128,128]{2,1,0:T(8,128)(2,1)} %get-tuple-element.71), channel_id=1, source_target_pairs={{0,8},{4,12},{8,16},{12,20},{16,24},{20,28},{24,0},{28,4},{1,9},{5... | collective-permute-start | bytes 4915208 | tf_op jit(solution)/shard_map/ppermute | solution.py:112
  39.6 234.4 %collective-permute-start.2 = (bf16[50,128,128]{2,1,0:T(8,128)(2,1)}, bf16[50,128,128]{2,1,0:T(8,128)(2,1)}, u32[]{:S(2)}, u32[]{:S(2)}) collective-permute-start(bf16[50,128,128]{2,1,0:T(8,128)(2,1)} %get-tuple-element.71), channel_id=1, source_target_pairs={{0,12},{4,16},{8,20},{12,24},{16,28},{20,0},{24,4},{28,8},{1,13},{... | collective-permute-start | bytes 4915208 | tf_op jit(solution)/shard_map/ppermute | solution.py:112
  42.2 235.7 %collective-permute-start.3 = (bf16[50,128,128]{2,1,0:T(8,128)(2,1)}, bf16[50,128,128]{2,1,0:T(8,128)(2,1)}, u32[]{:S(2)}, u32[]{:S(2)}) collective-permute-start(bf16[50,128,128]{2,1,0:T(8,128)(2,1)} %get-tuple-element.71), channel_id=1, source_target_pairs={{0,16},{4,20},{8,24},{12,28},{16,0},{20,4},{24,8},{28,12},{1,17},{... | collective-permute-start | bytes 4915208 | tf_op jit(solution)/shard_map/ppermute | solution.py:112
  43.4 236.2 %collective-permute-start.4 = (bf16[50,128,128]{2,1,0:T(8,128)(2,1)}, bf16[50,128,128]{2,1,0:T(8,128)(2,1)}, u32[]{:S(2)}, u32[]{:S(2)}) collective-permute-start(bf16[50,128,128]{2,1,0:T(8,128)(2,1)} %get-tuple-element.71), channel_id=1, source_target_pairs={{0,20},{4,24},{8,28},{12,0},{16,4},{20,8},{24,12},{28,16},{1,21},{... | collective-permute-start | bytes 4915208 | tf_op jit(solution)/shard_map/ppermute | solution.py:112
  46.1 1154.0 %reduce-scatter.5.cloned.1.call-start = ((), (), s32[]{:S(2)}) async-start(), calls=%async_computation.5 | async-start | bytes 14155776 | tf_op jit(solution)/shard_map/reduce_scatter | solution.py:158
  103.9 177.5 %collective-permute-start.5 = (bf16[50,128,128]{2,1,0:T(8,128)(2,1)S(1)}, bf16[50,128,128]{2,1,0:T(8,128)(2,1)S(1)}, u32[]{:S(2)}, u32[]{:S(2)}) collective-permute-start(bf16[50,128,128]{2,1,0:T(8,128)(2,1)S(1)} %copy-done.3), channel_id=1, source_target_pairs={{0,24},{4,28},{8,0},{12,4},{16,8},{20,12},{24,16},{28,20},{1,25},{... | collective-permute-start | bytes 4915208 | tf_op jit(solution)/shard_map/ppermute | solution.py:112
  128.3 213.9 %collective-permute-start.6 = (bf16[50,128,128]{2,1,0:T(8,128)(2,1)S(1)}, bf16[50,128,128]{2,1,0:T(8,128)(2,1)S(1)}, u32[]{:S(2)}, u32[]{:S(2)}) collective-permute-start(bf16[50,128,128]{2,1,0:T(8,128)(2,1)S(1)} %copy-done.3), channel_id=1, source_target_pairs={{0,28},{4,0},{8,4},{12,8},{16,12},{20,16},{24,20},{28,24},{1,29},{... | collective-permute-start | bytes 4915208 | tf_op jit(solution)/shard_map/ppermute | solution.py:112
  342.5 4.7 copy-start
  427.2 24.4 %copy-start.5 = (s32[8,96]{1,0:T(8,128)}, s32[8,96]{1,0:T(8,128)S(1)}, u32[]{:S(2)}) copy-start(s32[8,96]{1,0:T(8,128)S(1)} %get-tuple-element.68) | copy-start | bytes 9220
  622.6 595.7 %reduce-scatter.3.cloned.1.call-start = ((), (), s32[]{:S(2)}) async-start(), calls=%async_computation.4 | async-start | bytes 2621440 | tf_op jit(solution)/shard_map/reduce_scatter | solution.py:166
  655.6 28.4 %copy-start.1 = (bf16[256,4096]{1,0:T(8,128)(2,1)S(1)}, bf16[256,4096]{1,0:T(8,128)(2,1)}, u32[]{:S(2)}) copy-start(bf16[256,4096]{1,0:T(8,128)(2,1)} %all-gather.5.cloned.1.call-done) | copy-start | bytes 6291460
  734.2 34.6 %copy-start.6 = (s32[8,96]{1,0:T(8,128)S(1)}, s32[8,96]{1,0:T(8,128)}, u32[]{:S(2)}) copy-start(s32[8,96]{1,0:T(8,128)} %copy-done.5) | copy-start | bytes 9220
  795.1 65.5 %copy-start.10 = (s32[96]{0:T(128)S(1)}, s32[96]{0:T(128)}, u32[]{:S(2)}) copy-start(s32[96]{0:T(128)} %get-tuple-element.41) | copy-start | bytes 1156
  795.1 65.5 %copy-start.9 = (s32[96]{0:T(128)S(1)}, s32[96]{0:T(128)}, u32[]{:S(2)}) copy-start(s32[96]{0:T(128)} %get-tuple-element.73) | copy-start | bytes 1156
  795.1 65.5 %copy-start.7 = (s32[4,24]{1,0:T(4,128)S(1)}, s32[4,24]{1,0:T(4,128)}, u32[]{:S(2)}) copy-start(s32[4,24]{1,0:T(4,128)} %param.18) | copy-start | bytes 1156
  795.1 65.5 %copy-start.8 = (s32[4,24]{1,0:T(4,128)S(1)}, s32[4,24]{1,0:T(4,128)}, u32[]{:S(2)}) copy-start(s32[4,24]{1,0:T(4,128)} %param.19) | copy-start | bytes 1156
  795.1 170.7 %copy-start.2 = (bf16[256,3072]{0,1:T(8,128)(2,1)S(1)}, bf16[256,3072]{0,1:T(8,128)(2,1)}, u32[]{:S(2)}) copy-start(bf16[256,3072]{0,1:T(8,128)(2,1)} %fusion.26) | copy-start | bytes 4718596
  802.5 126.5 %collective-permute-start.13 = (bf16[48,128,128]{2,1,0:T(8,128)(2,1)S(1)}, bf16[48,128,128]{2,1,0:T(8,128)(2,1)}, u32[]{:S(2)}, u32[]{:S(2)}) collective-permute-start(bf16[48,128,128]{2,1,0:T(8,128)(2,1)S(1)} %get-tuple-element.67), channel_id=1, source_target_pairs={{0,28},{4,0},{8,4},{12,8},{16,12},{20,16},{24,20},{28,24},{1,29},{... | collective-permute-start | bytes 4718600 | tf_op jit(solution)/shard_map/ppermute | solution.py:163
  860.5 104.1 %collective-permute-start.12 = (bf16[48,128,128]{2,1,0:T(8,128)(2,1)S(1)}, bf16[48,128,128]{2,1,0:T(8,128)(2,1)S(1)}, u32[]{:S(2)}, u32[]{:S(2)}) collective-permute-start(bf16[48,128,128]{2,1,0:T(8,128)(2,1)S(1)} %get-tuple-element.62), channel_id=1, source_target_pairs={{0,24},{4,28},{8,0},{12,4},{16,8},{20,12},{24,16},{28,20},{1,25},{... | collective-permute-start | bytes 4718600 | tf_op jit(solution)/shard_map/ppermute | solution.py:163
  860.6 137.8 %collective-permute-start.11 = (bf16[48,128,128]{2,1,0:T(8,128)(2,1)}, bf16[48,128,128]{2,1,0:T(8,128)(2,1)}, u32[]{:S(2)}, u32[]{:S(2)}) collective-permute-start(bf16[48,128,128]{2,1,0:T(8,128)(2,1)} %get-tuple-element.63), channel_id=1, source_target_pairs={{0,20},{4,24},{8,28},{12,0},{16,4},{20,8},{24,12},{28,16},{1,21},{... | collective-permute-start | bytes 4718600 | tf_op jit(solution)/shard_map/ppermute | solution.py:163
  860.7 308.6 %collective-permute-start.10 = (bf16[48,128,128]{2,1,0:T(8,128)(2,1)}, bf16[48,128,128]{2,1,0:T(8,128)(2,1)}, u32[]{:S(2)}, u32[]{:S(2)}) collective-permute-start(bf16[48,128,128]{2,1,0:T(8,128)(2,1)} %get-tuple-element.64), channel_id=1, source_target_pairs={{0,16},{4,20},{8,24},{12,28},{16,0},{20,4},{24,8},{28,12},{1,17},{... | collective-permute-start | bytes 4718600 | tf_op jit(solution)/shard_map/ppermute | solution.py:163
  863.7 306.5 %collective-permute-start.9 = (bf16[48,128,128]{2,1,0:T(8,128)(2,1)}, bf16[48,128,128]{2,1,0:T(8,128)(2,1)}, u32[]{:S(2)}, u32[]{:S(2)}) collective-permute-start(bf16[48,128,128]{2,1,0:T(8,128)(2,1)} %get-tuple-element.65), channel_id=1, source_target_pairs={{0,12},{4,16},{8,20},{12,24},{16,28},{20,0},{24,4},{28,8},{1,13},{... | collective-permute-start | bytes 4718600 | tf_op jit(solution)/shard_map/ppermute | solution.py:163
  929.0 241.2 %collective-permute-start.8 = (bf16[48,128,128]{2,1,0:T(8,128)(2,1)}, bf16[48,128,128]{2,1,0:T(8,128)(2,1)}, u32[]{:S(2)}, u32[]{:S(2)}) collective-permute-start(bf16[48,128,128]{2,1,0:T(8,128)(2,1)} %get-tuple-element.66), channel_id=1, source_target_pairs={{0,8},{4,12},{8,16},{12,20},{16,24},{20,28},{24,0},{28,4},{1,9},{5... | collective-permute-start | bytes 4718600 | tf_op jit(solution)/shard_map/ppermute | solution.py:163
  965.8 204.4 %collective-permute-start.7 = (bf16[48,128,128]{2,1,0:T(8,128)(2,1)S(1)}, bf16[48,128,128]{2,1,0:T(8,128)(2,1)}, u32[]{:S(2)}, u32[]{:S(2)}) collective-permute-start(bf16[48,128,128]{2,1,0:T(8,128)(2,1)S(1)} %get-tuple-element.61), channel_id=1, source_target_pairs={{0,4},{4,8},{8,12},{12,16},{16,20},{20,24},{24,28},{28,0},{1,5},{5... | collective-permute-start | bytes 4718600 | tf_op jit(solution)/shard_map/ppermute | solution.py:163
  1181.3 7.1 slice-start
  1184.7 3.7 slice-start.1
  1202.6 4.2 slice-start.2
  (2 other events, 4.8 us)
Sparse Core Ops, SparseCore 0:
  34.4 392.0 all-gather.8
  428.0 77.6 all-gather.6
  507.3 22.5 all-gather.4
  622.7 421.9 reduce-scatter.4
  1047.7 43.1 reduce-scatter.2

commit v4 on v3

--- a/solution.py
+++ b/solution.py
@@ -84,7 +84,6 @@
     block = w_up.shape[0] // nr
     slots = nb // 2
     n_row = lax.axis_size("row")
-    me = lax.axis_index("row")
     width = slots + 2
     zero_slot = slots
     mask_slot = slots + 1
@@ -102,18 +101,10 @@
             [kept, jnp.zeros((1, block, block), jnp.bfloat16), mask_rows[None]], axis=0
         )
 
-    def shift_perm(s):
-        return [(i, (i + s) % n_row) for i in range(n_row)]
-
     got_up = lax.all_gather(package(w_up, flat_up), "row", axis=0)
-    sent_down = package(w_down, flat_down)
-    got_down = jnp.stack(
-        [sent_down]
-        + [lax.ppermute(sent_down, "row", shift_perm(s)) for s in range(1, n_row)]
-    )
-    pos_down = (me - rows_n) % n_row
+    got_down = lax.all_gather(package(w_down, flat_down), "row", axis=0)
     masks_up = got_up[:, mask_slot, 0, :nb].astype(jnp.int32)
-    masks_down = got_down[pos_down, mask_slot, 0, :nb].astype(jnp.int32)
+    masks_down = got_down[:, mask_slot, 0, :nb].astype(jnp.int32)
 
     features, cot_rows = (
         lax.all_gather(tokens, "col", axis=1, tiled=True),
@@ -130,7 +121,7 @@
         return dense.reshape((n_row * nr * block, nc * block))
 
     up_whole = rebuild(got_up, masks_up, rows_n)
-    down_whole = rebuild(got_down, masks_down, pos_down)
+    down_whole = rebuild(got_down, masks_down, rows_n)
 
     preact = jnp.dot(features, up_whole, preferred_element_type=jnp.float32)
     act_grad = jnp.dot(cot_rows, down_whole, preferred_element_type=jnp.float32)
@@ -154,14 +145,12 @@
         dense = jnp.where(keep, dense.astype(jnp.float32), jnp.zeros(dense.shape, jnp.float32))
         return from_blocks(dense, nr, nc)
 
-    sent = kept_blocks(token_product(cot_rows, activation), masks_down, rows_n)
-    grad_down = unpack(lax.psum_scatter(sent, "row", scatter_dimension=0, tiled=True)[0], flat_down)
-    dest = (me + rows_n) % n_row
-    sent = kept_blocks(token_product(features, pre_grad), masks_up[dest], dest)
-    total = sent[0].astype(jnp.float32)
-    for s in range(1, n_row):
-        total = total + lax.ppermute(sent[s], "row", shift_perm(s)).astype(jnp.float32)
-    grad_up = unpack(total, flat_up)
+    def reduce_kept(partial, masks, own):
+        sent = kept_blocks(partial, masks, rows_n)
+        return unpack(lax.psum_scatter(sent, "row", scatter_dimension=0, tiled=True)[0], own)
+
+    grad_down = reduce_kept(token_product(cot_rows, activation), masks_down, flat_down)
+    grad_up = reduce_kept(token_product(features, pre_grad), masks_up, flat_up)
 
     token_grad = lax.psum_scatter(
         partial_tokens.astype(jnp.bfloat16), "col", scatter_dimension=1, tiled=True

time: 1240 us -> 1100 us (0.89)
  starting transfers between devices: 135 us -> 0.28 us
  waiting for transfers between devices: 600 us -> 662 us
  local copies, waits for them, and re-layouts: 360 us -> 301 us
    ppermute x14 -> x0, waiting for transfers between devices: 515 us -> none  [the longest x7 292 us: shards(): lax.ppermute(sent[s], 'row', shift_perm(s)).astype(jnp.float32)]
    reduce_scatter x1 -> x2, waiting for transfers between devices: 0.01 us -> 295 us  [reduce_kept(): lax.psum_scatter(sent, 'row', scatter_dimension=0, tiled=True)[0]]
    all_gather x0 -> x1, waiting for transfers between devices: none -> 182 us  [shards(): got_down = lax.all_gather(package(w_down, flat_down), 'row', axis=0)]
    all_gather x1, waiting for transfers between devices: 46.7 us -> 183 us  [shards(): got_up = lax.all_gather(package(w_up, flat_up), 'row', axis=0)]
    ppermute x14 -> x0, starting transfers between devices: 135 us -> none  [the longest x7 73.7 us: shards(): lax.ppermute(sent_down, 'row', shift_perm(s))]
    gather x33 -> x0, local copies, waits for them, and re-layouts: 32.3 us -> none
    another operation x1 -> x2, local copies, waits for them, and re-layouts: 28.3 us -> 56.9 us  [from_blocks(): x = blocks.reshape(lead + (nr, nc, block, block))]
    all_gather x1, waiting for transfers between devices: 25.9 us -> 0.02 us  [shards(): lax.all_gather(tokens, 'col', axis=1, tiled=True)]
  transfers between devices with their start and end apart: 19 -> 7, of which waited for: 12 -> 4; matrix products, arithmetic and copies ran while one was open for 29% -> 25% of each run, Pallas kernels for 0% -> 0%
where the time goes in v4:
time: 1100 us; the launch traced here: 1090 us
  waiting for transfers between devices  662 us (60%)
  local copies, waits for them, and re-layouts  301 us (27%)
  matrix products  67.2 us (6%)
  other arithmetic  44.9 us (4%)
  between operations  14.6 us (1%)
    reduce_scatter x2, waiting for transfers between devices, reduce_kept(): lax.psum_scatter(sent, 'row', scatter_dimension=0, tiled=True)[0]  295 us
    all_gather x1, waiting for transfers between devices, shards(): got_up = lax.all_gather(package(w_up, flat_up), 'row', axis=0)  183 us
    all_gather x1, waiting for transfers between devices, shards(): got_down = lax.all_gather(package(w_down, flat_down), 'row', axis=0)  182 us
    reshape x2, local copies, waits for them, and re-layouts, kept_blocks(): view = partial.astype(jnp.bfloat16).reshape((n_row * nr, block, nc, block))  69 us
    another operation x2, local copies, waits for them, and re-layouts, from_blocks(): x = blocks.reshape(lead + (nr, nc, block, block))  56.9 us
    gather x2, local copies, waits for them, and re-layouts, kept_blocks(): return view.at[rows, :, cols, :].get(mode='promise_in_bounds')  49.2 us
    gather x2, local copies, waits for them, and re-layouts, rebuild(): dense = flat_got.at[where.reshape(-1)].get(mode='promise_in_bounds')  48.6 us
    unnamed x22, local copies, waits for them, and re-layouts  48 us
  transfers between devices with their start and end apart: 7, of which 4 were waited for; matrix products, arithmetic and copies ran while one was open for 25% of the time, Pallas kernels for 0%

profile of v4, /device:TPU:0, one launch (start us, length us, event | category | flops | bytes accessed | tf_op | source)
XLA Modules:
  0.0 1090.0 jit_solution(2186076261053792976)
XLA Ops:
  10.2 3.3 convert_bitcast_fusion.2
  16.9 3.3 convert_bitcast_fusion.3
  20.3 0.9 copy.77
  21.7 2.5 copy.65
  24.3 1.9 gather_fusion.2
  26.3 2.7 gather_fusion
  29.0 4.2 fusion.37
  35.7 183.2 %all-gather.13.cloned.1.call-done = bf16[400,128,128]{2,1,0:T(8,128)(2,1)} async-done(((bf16[50,128,128]{2,1,0:T(8,128)(2,1)}), bf16[400,128,128]{2,1,0:T(8,128)(2,1)}) %all-gather.13.cloned.1.call-update) | async-done | bytes 13107216 | tf_op jit(solution)/shard_map/all_gather | solution.py:104
  220.9 181.9 %all-gather.11.cloned.1.call-done = bf16[400,128,128]{2,1,0:T(8,128)(2,1)} async-done(((bf16[50,128,128]{2,1,0:T(8,128)(2,1)}), bf16[400,128,128]{2,1,0:T(8,128)(2,1)}) %all-gather.11.cloned.1.call-update) | async-done | bytes 13107216 | tf_op jit(solution)/shard_map/all_gather | solution.py:105
  404.7 24.7 %gather_fusion.1 = bf16[768,128,128]{2,1,0:T(8,128)(2,1)} fusion(bf16[400,128,128]{2,1,0:T(8,128)(2,1)} %all-gather.11.cloned.1.call-done, s32[1024]{0:T(1024)S(1)} %pad_clamp_fusion.4), kind=kCustom, calls=%fused_computation.1 | custom fusion | bytes 50334720 | tf_op jit(solution)/shard_map/gather | solution.py:118
  429.4 28.6 %copy.67 = bf16[8,4,24,128,128]{4,2,3,1,0:T(8,128)(2,1)} copy(bf16[8,4,24,128,128]{4,3,2,1,0:T(8,128)(2,1)} %bitcast.155) | data formatting | bytes 50331648 | tf_op jit(solution)/shard_map/reshape;reshape | solution.py:52
  457.9 23.9 %gather_fusion.3 = bf16[768,128,128]{2,1,0:T(8,128)(2,1)} fusion(bf16[400,128,128]{2,1,0:T(8,128)(2,1)} %all-gather.13.cloned.1.call-done, s32[1024]{0:T(1024)S(1)} %pad_clamp_fusion.2), kind=kCustom, calls=%fused_computation.3 | custom fusion | bytes 50334720 | tf_op jit(solution)/shard_map/gather | solution.py:118
  481.8 28.3 %copy.70 = bf16[8,4,24,128,128]{4,2,3,1,0:T(8,128)(2,1)} copy(bf16[8,4,24,128,128]{4,3,2,1,0:T(8,128)(2,1)} %bitcast.156) | data formatting | bytes 50331648 | tf_op jit(solution)/shard_map/reshape;reshape | solution.py:52
  510.6 12.3 %fusion.21 = f32[256,3072]{0,1:T(8,128)S(1)} fusion(bf16[256,4096]{1,0:T(8,128)(2,1)} %all-gather.9.cloned.1.call-done, bf16[512,8,24,128]{3,2,1,0:T(8,128)(2,1)} %bitcast.165), kind=kOutput, calls=%fused_computation.36 | convolution fusion | flops 6442450944 | bytes 30408704 | tf_op jit(solution)/shard_map/dot_general | solution.py:126
  523.0 14.1 %fusion.27 = bf16[256,3072]{0,1:T(8,128)(2,1)} fusion(bf16[256,4096]{1,0:T(8,128)(2,1)} %all-gather.7.cloned.1.call-done, bf16[512,8,24,128]{3,2,1,0:T(8,128)(2,1)} %bitcast.167, f32[256,3072]{0,1:T(8,128)S(1)} %fusion.21), kind=kOutput, calls=%fused_computation.38 | convolution fusion | flops 6450315264 | bytes 31981568 | tf_op jit(solution)/shard_map/dot_general | solution.py:127
  537.1 13.4 %convert_bitcast_fusion.1 = bf16[384,8,32,128]{3,1,2,0:T(8,128)(2,1)} fusion(bf16[256,3072]{0,1:T(8,128)(2,1)} %fusion.27, bf16[256,4096]{1,0:T(8,128)(2,1)} %all-gather.9.cloned.1.call-done), kind=kOutput, calls=%fused_computation.16 | convolution fusion | flops 6455033856 | bytes 28835840 | tf_op jit(solution)/shard_map/dot_general | solution.py:34
  550.4 22.4 %copy.81 = bf16[384,8,32,128]{3,2,1,0:T(8,128)(2,1)} copy(bf16[384,8,32,128]{3,1,2,0:T(8,128)(2,1)} %convert_bitcast_fusion.1) | data formatting | bytes 50331648
  572.8 34.4 %copy.71 = bf16[32,128,24,128]{3,1,2,0:T(8,128)(2,1)} copy(bf16[32,128,24,128]{1,0,3,2:T(8,128)(2,1)} %bitcast.157) | data formatting | bytes 50331648 | tf_op jit(solution)/shard_map/reshape | solution.py:136
  607.4 24.6 %gather_fusion.4 = bf16[384,128,128]{2,1,0:T(8,128)(2,1)} fusion(bf16[32,128,24,128]{3,1,2,0:T(8,128)(2,1)} %copy.71, s32[384]{0:T(512)S(1)} %reshape.620), kind=kCustom, calls=%fused_computation.4 | custom fusion | bytes 25168896 | tf_op jit(solution)/shard_map/gather | solution.py:140
  632.1 13.5 %convert_bitcast_fusion = bf16[384,8,32,128]{3,1,2,0:T(8,128)(2,1)} fusion(bf16[256,4096]{1,0:T(8,128)(2,1)} %all-gather.7.cloned.1.call-done, f32[256,3072]{0,1:T(8,128)S(1)} %fusion.21), kind=kOutput, calls=%fused_computation.15 | convolution fusion | flops 6458966016 | bytes 30408704 | tf_op jit(solution)/shard_map/dot_general | solution.py:34
  645.5 22.5 %copy.83 = bf16[384,8,32,128]{3,2,1,0:T(8,128)(2,1)} copy(bf16[384,8,32,128]{3,1,2,0:T(8,128)(2,1)} %convert_bitcast_fusion) | data formatting | bytes 50331648
  668.1 34.5 %copy.74 = bf16[32,128,24,128]{3,1,2,0:T(8,128)(2,1)} copy(bf16[32,128,24,128]{1,0,3,2:T(8,128)(2,1)} %bitcast.158) | data formatting | bytes 50331648 | tf_op jit(solution)/shard_map/reshape | solution.py:136
  702.7 24.6 %gather_fusion.6 = bf16[384,128,128]{2,1,0:T(8,128)(2,1)} fusion(bf16[32,128,24,128]{3,1,2,0:T(8,128)(2,1)} %copy.74, s32[384]{0:T(512)S(1)} %reshape.634), kind=kCustom, calls=%fused_computation.6 | custom fusion | bytes 25168896 | tf_op jit(solution)/shard_map/gather | solution.py:140
  728.8 13.9 %fusion.15 = bf16[256,4096]{1,0:T(8,128)(2,1)} fusion(bf16[256,3072]{0,1:T(8,128)(2,1)S(1)} %copy-done, bf16[512,8,24,128]{3,2,1,0:T(8,128)(2,1)} %bitcast.166), kind=kOutput, calls=%fused_computation.33 | convolution fusion | flops 6443499520 | bytes 28835840 | tf_op jit(solution)/shard_map/dot_general | solution.py:131
  742.7 94.5 %reduce-scatter.6.cloned.1.call-done = bf16[1,48,128,128]{3,2,1,0:T(8,128)(2,1)} async-done(((bf16[8,48,128,128]{3,2,1,0:T(8,128)(2,1)}), bf16[1,48,128,128]{3,2,1,0:T(8,128)(2,1)}) %reduce-scatter.6.cloned.1.call-update) | async-done | bytes 1572880 | tf_op jit(solution)/shard_map/reduce_scatter | solution.py:150
  837.3 2.6 gather_fusion.5
  840.3 6.3 copy.73
  846.7 200.4 %reduce-scatter.8.cloned.1.call-done = bf16[1,48,128,128]{3,2,1,0:T(8,128)(2,1)} async-done(((bf16[8,48,128,128]{3,2,1,0:T(8,128)(2,1)}), bf16[1,48,128,128]{3,2,1,0:T(8,128)(2,1)}) %reduce-scatter.8.cloned.1.call-update) | async-done | bytes 1572880 | tf_op jit(solution)/shard_map/reduce_scatter | solution.py:150
  1047.1 2.6 gather_fusion.7
  1050.2 6.3 copy.76
  1056.5 13.5 %multiply_subtract_fusion.1 = (f32[512,3072]{1,0:T(8,128)}, f32[512,3072]{1,0:T(8,128)}, f32[512,3072]{1,0:T(8,128)}) fusion(f32[512,3072]{1,0:T(8,128)S(1)} %bitcast.169, f32[64,8,24,128]{3,2,1,0:T(8,128)} %bitcast.172, f32[512,3072]{1,0:T(8,128)} %param.20, f32[512,3072]{1,0:T(8,128)} %param.21), kind=kLoop, calls=%fused_computation.32 | loop fusion | flops 20447232 | bytes 44040192 | tf_op jit(solution)/shard_map/sub | solution.py:30
  1070.0 13.0 %multiply_subtract_fusion = (f32[512,3072]{1,0:T(8,128)}, f32[512,3072]{1,0:T(8,128)}, f32[512,3072]{1,0:T(8,128)}) fusion(f32[512,3072]{1,0:T(8,128)S(1)} %bitcast.171, f32[64,8,24,128]{3,2,1,0:T(8,128)} %bitcast.173, f32[512,3072]{1,0:T(8,128)} %param.22, f32[512,3072]{1,0:T(8,128)} %param.23), kind=kLoop, calls=%fused_computation.31 | loop fusion | flops 20447232 | bytes 44040192 | tf_op jit(solution)/shard_map/sub | solution.py:30
  (88 shorter events, 16.5 us)
Async XLA Ops:
  7.2 211.8 %all-gather.13.cloned.1.call-start = ((), (), s32[]{:S(2)}) async-start(), calls=%async_computation.9 | async-start | bytes 14745600 | tf_op jit(solution)/shard_map/all_gather | solution.py:104
  33.3 369.5 %all-gather.11.cloned.1.call-start = ((), (), s32[]{:S(2)}) async-start(), calls=%async_computation.8 | async-start | bytes 14745600 | tf_op jit(solution)/shard_map/all_gather | solution.py:105
  34.1 476.6 %all-gather.9.cloned.1.call-start = ((), (), s32[]{:S(2)}) async-start(), calls=%async_computation.4 | async-start | bytes 2621440 | tf_op jit(solution)/shard_map/all_gather | solution.py:110
  34.8 488.2 %all-gather.7.cloned.1.call-start = ((), (), s32[]{:S(2)}) async-start(), calls=%async_computation.3 | async-start | bytes 2621440 | tf_op jit(solution)/shard_map/all_gather | solution.py:111
  35.4 801.9 %reduce-scatter.6.cloned.1.call-start = ((), (), s32[]{:S(2)}) async-start(), calls=%async_computation.6 | async-start | bytes 14155776 | tf_op jit(solution)/shard_map/reduce_scatter | solution.py:150
  632.0 415.1 %reduce-scatter.8.cloned.1.call-start = ((), (), s32[]{:S(2)}) async-start(), calls=%async_computation.7 | async-start | bytes 14155776 | tf_op jit(solution)/shard_map/reduce_scatter | solution.py:150
  727.3 0.7 copy-start.4
  727.3 0.7 copy-start.3
  727.3 0.7 copy-start.1
  727.3 0.7 copy-start.2
  727.3 1.5 copy-start
  727.4 355.6 %reduce-scatter.4.cloned.1.call-start = ((), (), s32[]{:S(2)}) async-start(), calls=%async_computation.5 | async-start | bytes 2621440 | tf_op jit(solution)/shard_map/reduce_scatter | solution.py:155
  1049.6 6.8 slice-start
  1050.1 6.3 slice-start.1
  1050.2 19.8 %slice-start.2 = ((s8[6291456]{0:T(1024)(128)(4,1)}), s8[4194304]{0:T(1024)(128)(4,1)S(1)}, s32[]{:S(2)}) async-start(s8[6291456]{0:T(1024)(128)(4,1)} %bitcast.170), calls=%async_computation.12 | async-start | bytes 8388608
  1056.5 13.5 %slice-start.3 = ((s8[6291456]{0:T(1024)(128)(4,1)}), s8[2097152]{0:T(1024)(128)(4,1)S(1)}, s32[]{:S(2)}) async-start(s8[6291456]{0:T(1024)(128)(4,1)} %bitcast.170), calls=%async_computation.13 | async-start | bytes 4194304
Sparse Core Ops, SparseCore 0:
  33.4 185.5 all-gather.12
  221.7 180.9 all-gather.10
  404.4 20.7 all-gather.8
  426.6 22.5 all-gather.6
  632.1 205.0 reduce-scatter.5
  840.7 206.3 reduce-scatter.7
  1050.2 30.4 reduce-scatter.3

commit v5 on v4

--- a/solution.py
+++ b/solution.py
@@ -96,7 +96,8 @@
         blocks = to_blocks(w.astype(jnp.bfloat16), block)
         kept = blocks.at[kept_index(flat, slots)].get(mode="promise_in_bounds")
         mask_rows = jnp.zeros((block, block), jnp.bfloat16)
-        mask_rows = mask_rows.at[0, :nb].set(flat.astype(jnp.bfloat16))
+        mask_rows = mask_rows.at[0, :nb].set(flat_up.astype(jnp.bfloat16))
+        mask_rows = mask_rows.at[1, :nb].set(flat_down.astype(jnp.bfloat16))
         return jnp.concatenate(
             [kept, jnp.zeros((1, block, block), jnp.bfloat16), mask_rows[None]], axis=0
         )
@@ -104,7 +105,7 @@
     got_up = lax.all_gather(package(w_up, flat_up), "row", axis=0)
     got_down = lax.all_gather(package(w_down, flat_down), "row", axis=0)
     masks_up = got_up[:, mask_slot, 0, :nb].astype(jnp.int32)
-    masks_down = got_down[:, mask_slot, 0, :nb].astype(jnp.int32)
+    masks_down = got_up[:, mask_slot, 1, :nb].astype(jnp.int32)
 
     features, cot_rows = (
         lax.all_gather(tokens, "col", axis=1, tiled=True),
@@ -121,16 +122,9 @@
         return dense.reshape((n_row * nr * block, nc * block))
 
     up_whole = rebuild(got_up, masks_up, rows_n)
-    down_whole = rebuild(got_down, masks_down, rows_n)
-
     preact = jnp.dot(features, up_whole, preferred_element_type=jnp.float32)
-    act_grad = jnp.dot(cot_rows, down_whole, preferred_element_type=jnp.float32)
     gelu_value, gelu_slope = gelu_parts(preact)
     activation = gelu_value.astype(jnp.bfloat16)
-    pre_grad = (act_grad * gelu_slope).astype(jnp.bfloat16)
-    partial_tokens = lax.dot_general(
-        pre_grad, up_whole, (((1,), (1,)), ((), ())), preferred_element_type=jnp.float32
-    )
 
     def kept_blocks(partial, masks, dest):
         view = partial.astype(jnp.bfloat16).reshape((n_row * nr, block, nc, block))
@@ -145,12 +139,23 @@
         dense = jnp.where(keep, dense.astype(jnp.float32), jnp.zeros(dense.shape, jnp.float32))
         return from_blocks(dense, nr, nc)
 
-    def reduce_kept(partial, masks, own):
-        sent = kept_blocks(partial, masks, rows_n)
+    def reduce_kept(sent, own):
         return unpack(lax.psum_scatter(sent, "row", scatter_dimension=0, tiled=True)[0], own)
 
-    grad_down = reduce_kept(token_product(cot_rows, activation), masks_down, flat_down)
-    grad_up = reduce_kept(token_product(features, pre_grad), masks_up, flat_up)
+    sent_down = kept_blocks(token_product(cot_rows, activation), masks_down, rows_n)
+    got_down, sent_down = lax.optimization_barrier((got_down, sent_down))
+    summed_down = lax.psum_scatter(sent_down, "row", scatter_dimension=0, tiled=True)[0]
+
+    down_whole = rebuild(got_down, masks_down, rows_n)
+    act_grad = jnp.dot(cot_rows, down_whole, preferred_element_type=jnp.float32)
+    pre_grad = (act_grad * gelu_slope).astype(jnp.bfloat16)
+    partial_tokens = lax.dot_general(
+        pre_grad, up_whole, (((1,), (1,)), ((), ())), preferred_element_type=jnp.float32
+    )
+    sent_up = kept_blocks(token_product(features, pre_grad), masks_up, rows_n)
+    summed_down, sent_up = lax.optimization_barrier((summed_down, sent_up))
+    grad_down = unpack(summed_down, flat_down)
+    grad_up = reduce_kept(sent_up, flat_up)
 
     token_grad = lax.psum_scatter(
         partial_tokens.astype(jnp.bfloat16), "col", scatter_dimension=1, tiled=True

time: 1100 us -> 917 us (0.83)
  waiting for transfers between devices: 662 us -> 492 us
    reduce_scatter x2 -> x1, waiting for transfers between devices: 295 us -> 176 us  [reduce_kept(): lax.psum_scatter(sent, 'row', scatter_dimension=0, tiled=True)[0]]
    all_gather x1, waiting for transfers between devices: 182 us -> 68.1 us  [shards(): got_down = lax.all_gather(package(w_down, flat_down), 'row', axis=0)]
    reduce_scatter x0 -> x1, waiting for transfers between devices: none -> 47.2 us  [shards(): lax.psum_scatter(sent_down, 'row', scatter_dimension=0, tiled=True)[0]]
    another operation x2 -> x1, local copies, waits for them, and re-layouts: 56.9 us -> 28.5 us  [from_blocks(): x = blocks.reshape(lead + (nr, nc, block, block))]
    transpose x2 -> x3, local copies, waits for them, and re-layouts: 12.7 us -> 35.8 us  [from_blocks(): x = jnp.moveaxis(x, k + 1, k + 2)]
    reduce_scatter x1, waiting for transfers between devices: 0.01 us -> 14.9 us  [shards(): lax.psum_scatter(partial_tokens.astype(jnp.bfloat16), 'col', scatter_dime...]
    unnamed x22 -> x28, local copies, waits for them, and re-layouts: 48 us -> 48.7 us
  transfers between devices with their start and end apart: 7 -> 7, of which waited for: 4 -> 5; matrix products, arithmetic and copies ran while one was open for 25% -> 41% of each run, Pallas kernels for 0% -> 0%
where the time goes in v5:
time: 917 us; the launch traced here: 908 us
  waiting for transfers between devices  492 us (54%)
  local copies, waits for them, and re-layouts  296 us (32%)
  matrix products  67.3 us (7%)
  other arithmetic  37.3 us (4%)
  between operations  14.7 us (2%)
    all_gather x1, waiting for transfers between devices, shards(): got_up = lax.all_gather(package(w_up, flat_up), 'row', axis=0)  183 us
    reduce_scatter x1, waiting for transfers between devices, reduce_kept(): lax.psum_scatter(sent, 'row', scatter_dimension=0, tiled=True)[0]  176 us
    all_gather x1, waiting for transfers between devices, shards(): got_down = lax.all_gather(package(w_down, flat_down), 'row', axis=0)  68.1 us
    reshape x2, local copies, waits for them, and re-layouts, kept_blocks(): view = partial.astype(jnp.bfloat16).reshape((n_row * nr, block, nc, block))  68 us
    gather x2, local copies, waits for them, and re-layouts, kept_blocks(): return view.at[rows, :, cols, :].get(mode='promise_in_bounds')  50.2 us
    unnamed x28, local copies, waits for them, and re-layouts  48.7 us
    gather x2, local copies, waits for them, and re-layouts, rebuild(): dense = flat_got.at[where.reshape(-1)].get(mode='promise_in_bounds')  48.4 us
    reduce_scatter x1, waiting for transfers between devices, shards(): lax.psum_scatter(sent_down, 'row', scatter_dimension=0, tiled=True)[0]  47.2 us
  transfers between devices with their start and end apart: 7, of which 5 were waited for; matrix products, arithmetic and copies ran while one was open for 41% of the time, Pallas kernels for 0%

profile of v5, /device:TPU:0, one launch (start us, length us, event | category | flops | bytes accessed | tf_op | source)
XLA Modules:
  0.0 907.9 jit_solution(12035091577683687742)
XLA Ops:
  11.2 3.3 convert_bitcast_fusion.3
  18.2 0.9 copy.77
  19.6 2.5 copy.66
  22.2 1.9 gather_fusion
  24.2 2.7 gather_fusion.1
  27.1 3.5 pad_maximum_fusion
  33.0 183.2 %all-gather.13.cloned.1.call-done = bf16[400,128,128]{2,1,0:T(8,128)(2,1)} async-done(((bf16[50,128,128]{2,1,0:T(8,128)(2,1)}), bf16[400,128,128]{2,1,0:T(8,128)(2,1)}) %all-gather.13.cloned.1.call-update) | async-done | bytes 13107216 | tf_op jit(solution)/shard_map/all_gather | solution.py:105
  218.8 24.4 %gather_fusion.2 = bf16[768,128,128]{2,1,0:T(8,128)(2,1)} fusion(bf16[400,128,128]{2,1,0:T(8,128)(2,1)} %all-gather.13.cloned.1.call-done, s32[1024]{0:T(1024)S(1)} %pad_clamp_fusion.3), kind=kCustom, calls=%fused_computation.2 | custom fusion | bytes 50334720 | tf_op jit(solution)/shard_map/gather | solution.py:119
  243.2 28.5 %copy.68 = bf16[8,4,24,128,128]{4,2,3,1,0:T(8,128)(2,1)} copy(bf16[8,4,24,128,128]{4,3,2,1,0:T(8,128)(2,1)} %bitcast.159) | data formatting | bytes 50331648 | tf_op jit(solution)/shard_map/reshape;reshape | solution.py:52
  271.7 13.6 %fusion.18 = f32[256,3072]{0,1:T(8,128)S(1)} fusion(bf16[256,4096]{1,0:T(8,128)(2,1)} %all-gather.7.cloned.1.call-done, bf16[512,8,24,128]{3,2,1,0:T(8,128)(2,1)} %bitcast.167), kind=kOutput, calls=%fused_computation.35 | convolution fusion | flops 6442450944 | bytes 30408704 | tf_op jit(solution)/shard_map/dot_general | solution.py:125
  285.3 13.3 %convert_bitcast_fusion.1 = bf16[384,8,32,128]{3,1,2,0:T(8,128)(2,1)} fusion(bf16[256,4096]{1,0:T(8,128)(2,1)} %all-gather.9.cloned.1.call-done, f32[256,3072]{0,1:T(8,128)S(1)} %fusion.18), kind=kOutput, calls=%fused_computation.16 | convolution fusion | flops 6458966016 | bytes 30408704 | tf_op jit(solution)/shard_map/dot_general | solution.py:34
  298.7 22.5 %copy.79 = bf16[384,8,32,128]{3,2,1,0:T(8,128)(2,1)} copy(bf16[384,8,32,128]{3,1,2,0:T(8,128)(2,1)} %convert_bitcast_fusion.1) | data formatting | bytes 50331648
  321.1 33.4 %copy.69 = bf16[32,128,24,128]{3,1,2,0:T(8,128)(2,1)} copy(bf16[32,128,24,128]{1,0,3,2:T(8,128)(2,1)} %bitcast.161) | data formatting | bytes 50331648 | tf_op jit(solution)/shard_map/reshape | solution.py:130
  355.1 25.1 %gather_fusion.3 = bf16[384,128,128]{2,1,0:T(8,128)(2,1)} fusion(bf16[32,128,24,128]{3,1,2,0:T(8,128)(2,1)} %copy.69, s32[384]{0:T(512)S(1)} %reshape.638), kind=kCustom, calls=%fused_computation.3 | custom fusion | bytes 25168896 | tf_op jit(solution)/shard_map/gather | solution.py:134
  380.2 68.1 %all-gather.11.cloned.1.call-done = bf16[400,128,128]{2,1,0:T(8,128)(2,1)} async-done(((bf16[50,128,128]{2,1,0:T(8,128)(2,1)}), bf16[400,128,128]{2,1,0:T(8,128)(2,1)}) %all-gather.11.cloned.1.call-update) | async-done | bytes 13107216 | tf_op jit(solution)/shard_map/all_gather | solution.py:106
  448.4 23.9 %gather_fusion.4 = bf16[768,128,128]{2,1,0:T(8,128)(2,1)} fusion(bf16[400,128,128]{2,1,0:T(8,128)(2,1)} %all-gather.11.cloned.1.call-done, s32[1024]{0:T(1024)S(1)} %pad_clamp_fusion.2), kind=kCustom, calls=%fused_computation.4 | custom fusion | bytes 50334720 | tf_op jit(solution)/shard_map/gather | solution.py:119
  472.3 28.5 %copy.70 = bf16[8,4,128,24,128]{4,3,2,1,0:T(8,128)(2,1)} copy(bf16[8,4,128,24,128]{4,2,3,1,0:T(8,128)(2,1)} %bitcast.160) | data formatting | bytes 50331648 | tf_op jit(solution)/shard_map/transpose | solution.py:54
  500.9 13.6 %fusion.27 = bf16[256,3072]{0,1:T(8,128)(2,1)} fusion(bf16[256,4096]{1,0:T(8,128)(2,1)S(1)} %copy-done, bf16[512,8,24,128]{3,2,1,0:T(8,128)(2,1)} %bitcast.169, f32[256,3072]{0,1:T(8,128)S(1)} %fusion.18), kind=kOutput, calls=%fused_computation.38 | convolution fusion | flops 6450315264 | bytes 31981568 | tf_op jit(solution)/shard_map/dot_general | solution.py:150
  514.5 13.5 %convert_bitcast_fusion = bf16[384,8,32,128]{3,1,2,0:T(8,128)(2,1)} fusion(bf16[256,3072]{0,1:T(8,128)(2,1)} %fusion.27, bf16[256,4096]{1,0:T(8,128)(2,1)} %all-gather.7.cloned.1.call-done), kind=kOutput, calls=%fused_computation.15 | convolution fusion | flops 6455033856 | bytes 28835840 | tf_op jit(solution)/shard_map/dot_general | solution.py:34
  527.9 22.5 %copy.81 = bf16[384,8,32,128]{3,2,1,0:T(8,128)(2,1)} copy(bf16[384,8,32,128]{3,1,2,0:T(8,128)(2,1)} %convert_bitcast_fusion) | data formatting | bytes 50331648
  550.4 34.6 %copy.71 = bf16[32,128,24,128]{3,1,2,0:T(8,128)(2,1)} copy(bf16[32,128,24,128]{1,0,3,2:T(8,128)(2,1)} %bitcast.162) | data formatting | bytes 50331648 | tf_op jit(solution)/shard_map/reshape | solution.py:130
  585.1 25.0 %gather_fusion.5 = bf16[384,128,128]{2,1,0:T(8,128)(2,1)} fusion(bf16[32,128,24,128]{3,1,2,0:T(8,128)(2,1)} %copy.71, s32[384]{0:T(512)S(1)} %reshape.652), kind=kCustom, calls=%fused_computation.5 | custom fusion | bytes 25168896 | tf_op jit(solution)/shard_map/gather | solution.py:134
  610.1 47.2 %reduce-scatter.6.cloned.1.call-done = bf16[1,48,128,128]{3,2,1,0:T(8,128)(2,1)} async-done(((bf16[8,48,128,128]{3,2,1,0:T(8,128)(2,1)}), bf16[1,48,128,128]{3,2,1,0:T(8,128)(2,1)}) %reduce-scatter.6.cloned.1.call-update) | async-done | bytes 1572880 | tf_op jit(solution)/shard_map/reduce_scatter | solution.py:147
  658.8 13.3 %fusion.15 = bf16[256,4096]{1,0:T(8,128)(2,1)} fusion(bf16[256,3072]{0,1:T(8,128)(2,1)S(1)} %copy-done.1, bf16[512,8,24,128]{3,2,1,0:T(8,128)(2,1)} %bitcast.168), kind=kOutput, calls=%fused_computation.33 | convolution fusion | flops 6443499520 | bytes 28835840 | tf_op jit(solution)/shard_map/dot_general | solution.py:152
  672.2 2.6 gather_fusion.7
  675.3 3.6 copy.75
  679.0 11.8 %multiply_subtract_fusion = (f32[512,3072]{1,0:T(8,128)}, f32[512,3072]{1,0:T(8,128)}, f32[512,3072]{1,0:T(8,128)}) fusion(f32[512,3072]{1,0:T(8,128)S(1)} %bitcast.171, f32[64,8,24,128]{3,2,1,0:T(8,128)S(1)} %bitcast.176, f32[512,3072]{1,0:T(8,128)} %param.26, f32[512,3072]{1,0:T(8,128)} %param.27), kind=kLoop, calls=%fused_computation.31 | loop fusion | flops 20447232 | bytes 44040192 | tf_op jit(solution)/shard_map/sub | solution.py:30
  690.7 176.5 %reduce-scatter.8.cloned.1.call-done = bf16[1,48,128,128]{3,2,1,0:T(8,128)(2,1)} async-done(((bf16[8,48,128,128]{3,2,1,0:T(8,128)(2,1)}), bf16[1,48,128,128]{3,2,1,0:T(8,128)(2,1)}) %reduce-scatter.8.cloned.1.call-update) | async-done | bytes 1572880 | tf_op jit(solution)/shard_map/reduce_scatter | solution.py:143
  867.2 2.6 gather_fusion.6
  870.3 3.6 copy.73
  874.0 11.9 %multiply_subtract_fusion.1 = (f32[512,3072]{1,0:T(8,128)}, f32[512,3072]{1,0:T(8,128)}, f32[512,3072]{1,0:T(8,128)}) fusion(f32[512,3072]{1,0:T(8,128)S(1)} %bitcast.175, f32[64,8,24,128]{3,2,1,0:T(8,128)S(1)} %bitcast.177, f32[512,3072]{1,0:T(8,128)} %param.24, f32[512,3072]{1,0:T(8,128)} %param.25), kind=kLoop, calls=%fused_computation.32 | loop fusion | flops 20447232 | bytes 44040192 | tf_op jit(solution)/shard_map/sub | solution.py:30
  885.9 14.9 %reduce-scatter.4.cloned.1.call-done = bf16[256,1024]{1,0:T(8,128)(2,1)} async-done(((bf16[256,4096]{1,0:T(8,128)(2,1)}), bf16[256,1024]{1,0:T(8,128)(2,1)}) %reduce-scatter.4.cloned.1.call-update) | async-done | bytes 524304 | tf_op jit(solution)/shard_map/reduce_scatter | solution.py:160
  (95 shorter events, 16.5 us)
Async XLA Ops:
  7.2 209.1 %all-gather.13.cloned.1.call-start = ((), (), s32[]{:S(2)}) async-start(), calls=%async_computation.9 | async-start | bytes 14745600 | tf_op jit(solution)/shard_map/all_gather | solution.py:105
  14.5 2.4 slice-start.2
  15.4 2.2 slice-start.3
  30.6 241.1 %all-gather.7.cloned.1.call-start = ((), (), s32[]{:S(2)}) async-start(), calls=%async_computation.3 | async-start | bytes 2621440 | tf_op jit(solution)/shard_map/all_gather | solution.py:111
  31.3 254.0 %all-gather.9.cloned.1.call-start = ((), (), s32[]{:S(2)}) async-start(), calls=%async_computation.4 | async-start | bytes 2621440 | tf_op jit(solution)/shard_map/all_gather | solution.py:112
  32.1 416.2 %all-gather.11.cloned.1.call-start = ((), (), s32[]{:S(2)}) async-start(), calls=%async_computation.8 | async-start | bytes 14745600 | tf_op jit(solution)/shard_map/all_gather | solution.py:106
  32.7 624.7 %reduce-scatter.6.cloned.1.call-start = ((), (), s32[]{:S(2)}) async-start(), calls=%async_computation.6 | async-start | bytes 14155776 | tf_op jit(solution)/shard_map/reduce_scatter | solution.py:147
  448.3 418.9 %reduce-scatter.8.cloned.1.call-start = ((), (), s32[]{:S(2)}) async-start(), calls=%async_computation.7 | async-start | bytes 14155776 | tf_op jit(solution)/shard_map/reduce_scatter | solution.py:143
  472.3 28.5 %copy-start = (bf16[256,4096]{1,0:T(8,128)(2,1)S(1)}, bf16[256,4096]{1,0:T(8,128)(2,1)}, u32[]{:S(2)}) copy-start(bf16[256,4096]{1,0:T(8,128)(2,1)} %all-gather.9.cloned.1.call-done) | copy-start | bytes 6291460
  657.4 0.7 copy-start.5
  657.4 0.7 copy-start.4
  657.4 0.7 copy-start.2
  657.4 0.7 copy-start.3
  657.4 1.5 copy-start.1
  657.4 243.5 %reduce-scatter.4.cloned.1.call-start = ((), (), s32[]{:S(2)}) async-start(), calls=%async_computation.5 | async-start | bytes 2621440 | tf_op jit(solution)/shard_map/reduce_scatter | solution.py:160
  674.8 4.2 slice-start
  675.3 3.7 slice-start.1
  869.8 4.2 slice-start.4
  870.3 3.7 slice-start.5
Sparse Core Ops, SparseCore 0:
  30.7 185.5 all-gather.12
  217.8 20.7 all-gather.6
  240.2 22.5 all-gather.8
  265.5 182.8 all-gather.10
  451.7 205.5 reduce-scatter.5
  660.8 206.3 reduce-scatter.7
  870.3 30.5 reduce-scatter.3

commit v6 on v5

--- a/solution.py
+++ b/solution.py
@@ -1,3 +1,5 @@
+import functools
+
 import jax
 import jax.numpy as jnp
 from jax import lax
@@ -67,7 +69,43 @@
     return jnp.cumsum(flat_mask, axis=-1) - flat_mask
 
 
+def row_ring(mesh):
+    devices = mesh.devices
+    n = devices.shape[0]
+    try:
+        pts = [tuple(devices[r, 0].coords) for r in range(n)]
+    except AttributeError:
+        return list(range(n))
+
+    def near(a, b):
+        return sum(abs(i - j) for i, j in zip(pts[a], pts[b])) == 1
+
+    path, used, budget = [0], {0}, [20000]
+
+    def search():
+        budget[0] -= 1
+        if budget[0] < 0:
+            return False
+        if len(path) == n:
+            return near(path[-1], 0)
+        options = [j for j in range(n) if j not in used and near(path[-1], j)]
+        options.sort(key=lambda j: sum(1 for k in range(n) if k not in used and near(j, k)))
+        for j in options:
+            path.append(j)
+            used.add(j)
+            if search():
+                return True
+            path.pop()
+            used.discard(j)
+        return False
+
+    if n > 2 and search():
+        return path
+    return list(range(n))
+
+
 def shards(
+    ring,
     tokens,
     cotangent,
     w_up,
@@ -85,9 +123,21 @@
     slots = nb // 2
     n_row = lax.axis_size("row")
     width = slots + 2
+    width += width % 2
     zero_slot = slots
     mask_slot = slots + 1
+    half = width // 2
     rows_n = jnp.arange(n_row, dtype=jnp.int32)
+
+    place = [0] * n_row
+    for i, r in enumerate(ring):
+        place[r] = i
+    right = [(ring[i], ring[(i + 1) % n_row]) for i in range(n_row)]
+    left = [(ring[i], ring[(i - 1) % n_row]) for i in range(n_row)]
+    me = lax.axis_index("row")
+    place_of = jnp.array(place, jnp.int32)
+    ring_of = jnp.array(ring, jnp.int32)
+    p = place_of[me]
 
     flat_up = mask_up.reshape(nb)
     flat_down = mask_down.reshape(nb)
@@ -95,67 +145,100 @@
     def package(w, flat):
         blocks = to_blocks(w.astype(jnp.bfloat16), block)
         kept = blocks.at[kept_index(flat, slots)].get(mode="promise_in_bounds")
-        mask_rows = jnp.zeros((block, block), jnp.bfloat16)
-        mask_rows = mask_rows.at[0, :nb].set(flat_up.astype(jnp.bfloat16))
-        mask_rows = mask_rows.at[1, :nb].set(flat_down.astype(jnp.bfloat16))
+        extra = jnp.zeros((width - slots, block, block), jnp.bfloat16)
+        extra = extra.at[mask_slot - slots, 0, :nb].set(flat_up.astype(jnp.bfloat16))
+        extra = extra.at[mask_slot - slots, 1, :nb].set(flat_down.astype(jnp.bfloat16))
+        return jnp.concatenate([kept, extra], axis=0)
+
+    def ring_gather(pk):
+        a, b = pk[:half], pk[half:]
+        got_a, got_b = [a], [b]
+        for _ in range(1, n_row):
+            a = lax.ppermute(a, "row", right)
+            b = lax.ppermute(b, "row", left)
+            got_a.append(a)
+            got_b.append(b)
         return jnp.concatenate(
-            [kept, jnp.zeros((1, block, block), jnp.bfloat16), mask_rows[None]], axis=0
+            [jnp.stack(got_a).reshape((n_row * half, block, block)),
+             jnp.stack(got_b).reshape((n_row * half, block, block))],
+            axis=0,
         )
 
-    got_up = lax.all_gather(package(w_up, flat_up), "row", axis=0)
-    got_down = lax.all_gather(package(w_down, flat_down), "row", axis=0)
-    masks_up = got_up[:, mask_slot, 0, :nb].astype(jnp.int32)
-    masks_down = got_up[:, mask_slot, 1, :nb].astype(jnp.int32)
+    q = place_of
+    step_a = (p - q) % n_row
+    step_b = (q - p) % n_row
+
+    def where_is(k):
+        in_a = k < half
+        return jnp.where(
+            in_a,
+            step_a[:, None] * half + k,
+            n_row * half + step_b[:, None] * half + (k - half),
+        )
+
+    got_up = ring_gather(package(w_up, flat_up))
+    got_down = ring_gather(package(w_down, flat_down))
+    mask_blocks = got_up.at[where_is(jnp.full((n_row, 1), mask_slot, jnp.int32))[:, 0]].get(
+        mode="promise_in_bounds"
+    )
+    masks_up = mask_blocks[:, 0, :nb].astype(jnp.int32)
+    masks_down = mask_blocks[:, 1, :nb].astype(jnp.int32)
 
     features, cot_rows = (
         lax.all_gather(tokens, "col", axis=1, tiled=True),
         lax.all_gather(cotangent, "col", axis=1, tiled=True),
     )
 
-    def rebuild(got, masks, pos):
-        flat_got = got.reshape((n_row * width, block, block))
-        base = (pos * width)[:, None]
-        where = jnp.where(masks > 0, base + slot_of(masks), base + zero_slot)
-        dense = flat_got.at[where.reshape(-1)].get(mode="promise_in_bounds")
+    def rebuild(got, masks):
+        k = jnp.where(masks > 0, slot_of(masks), zero_slot)
+        dense = got.at[where_is(k).reshape(-1)].get(mode="promise_in_bounds")
         dense = dense.reshape((n_row, nb, block, block))
         dense = from_blocks(dense, nr, nc)
         return dense.reshape((n_row * nr * block, nc * block))
 
-    up_whole = rebuild(got_up, masks_up, rows_n)
+    def kept_blocks(partial, masks, dest, lo, hi):
+        view = partial.astype(jnp.bfloat16).reshape((n_row * nr, block, nc, block))
+        idx = kept_index(masks[dest], slots)[:, lo:hi]
+        rows = (dest * nr)[:, None] + idx // nc
+        cols = idx % nc
+        return view.at[rows, :, cols, :].get(mode="promise_in_bounds")
+
+    def ring_reduce(partial, masks):
+        ha = (slots + 1) // 2
+        dest_a = ring_of[(p - rows_n) % n_row]
+        dest_b = ring_of[(p + rows_n) % n_row]
+        sent_a = kept_blocks(partial, masks, dest_a, 0, ha)
+        sent_b = kept_blocks(partial, masks, dest_b, ha, slots)
+        acc_a, acc_b = sent_a[1], sent_b[1]
+        for s in range(1, n_row):
+            in_a = lax.ppermute(acc_a, "row", right).astype(jnp.float32)
+            in_b = lax.ppermute(acc_b, "row", left).astype(jnp.float32)
+            if s < n_row - 1:
+                acc_a = (in_a + sent_a[s + 1].astype(jnp.float32)).astype(jnp.bfloat16)
+                acc_b = (in_b + sent_b[s + 1].astype(jnp.float32)).astype(jnp.bfloat16)
+        total_a = in_a + sent_a[0].astype(jnp.float32)
+        total_b = in_b + sent_b[0].astype(jnp.float32)
+        return jnp.concatenate([total_a, total_b], axis=0)
+
+    def unpack(summed, own):
+        dense = summed.at[slot_of(own)].get(mode="promise_in_bounds")
+        keep = own[:, None, None] > 0
+        dense = jnp.where(keep, dense, jnp.zeros(dense.shape, jnp.float32))
+        return from_blocks(dense, nr, nc)
+
+    up_whole = rebuild(got_up, masks_up)
     preact = jnp.dot(features, up_whole, preferred_element_type=jnp.float32)
     gelu_value, gelu_slope = gelu_parts(preact)
     activation = gelu_value.astype(jnp.bfloat16)
-
-    def kept_blocks(partial, masks, dest):
-        view = partial.astype(jnp.bfloat16).reshape((n_row * nr, block, nc, block))
-        idx = kept_index(masks, slots)
-        rows = (dest * nr)[:, None] + idx // nc
-        cols = idx % nc
-        return view.at[rows, :, cols, :].get(mode="promise_in_bounds")
-
-    def unpack(summed, own):
-        dense = summed.at[slot_of(own)].get(mode="promise_in_bounds")
-        keep = own[:, None, None] > 0
-        dense = jnp.where(keep, dense.astype(jnp.float32), jnp.zeros(dense.shape, jnp.float32))
-        return from_blocks(dense, nr, nc)
-
-    def reduce_kept(sent, own):
-        return unpack(lax.psum_scatter(sent, "row", scatter_dimension=0, tiled=True)[0], own)
-
-    sent_down = kept_blocks(token_product(cot_rows, activation), masks_down, rows_n)
-    got_down, sent_down = lax.optimization_barrier((got_down, sent_down))
-    summed_down = lax.psum_scatter(sent_down, "row", scatter_dimension=0, tiled=True)[0]
-
-    down_whole = rebuild(got_down, masks_down, rows_n)
+    grad_down = unpack(ring_reduce(token_product(cot_rows, activation), masks_down), flat_down)
+
+    down_whole = rebuild(got_down, masks_down)
     act_grad = jnp.dot(cot_rows, down_whole, preferred_element_type=jnp.float32)
     pre_grad = (act_grad * gelu_slope).astype(jnp.bfloat16)
     partial_tokens = lax.dot_general(
         pre_grad, up_whole, (((1,), (1,)), ((), ())), preferred_element_type=jnp.float32
     )
-    sent_up = kept_blocks(token_product(features, pre_grad), masks_up, rows_n)
-    summed_down, sent_up = lax.optimization_barrier((summed_down, sent_up))
-    grad_down = unpack(summed_down, flat_down)
-    grad_up = reduce_kept(sent_up, flat_up)
+    grad_up = unpack(ring_reduce(token_product(features, pre_grad), masks_up), flat_up)
 
     token_grad = lax.psum_scatter(
         partial_tokens.astype(jnp.bfloat16), "col", scatter_dimension=1, tiled=True
@@ -178,7 +261,7 @@
 def solution(mesh):
     spec = P("row", "col")
     return jax.shard_map(
-        shards,
+        functools.partial(shards, row_ring(mesh)),
         mesh=mesh,
         in_specs=(spec,) * 10,
         out_specs=(spec,) * 7,

time: 917 us -> 993 us (1.083)
  waiting for transfers between devices: 492 us -> 376 us
  local copies, waits for them, and re-layouts: 296 us -> 365 us
  other arithmetic: 37.3 us -> 102 us
  starting transfers between devices: 0.27 us -> 59.7 us
    ppermute x0 -> x56, waiting for transfers between devices: none -> 376 us  [the longest x14 183 us: ring_reduce(): in_a = lax.ppermute(acc_a, 'row', right).astype(jnp.float32)]
    all_gather x2 -> x0, waiting for transfers between devices: 251 us -> none  [the longest x1 183 us: shards(): got_up = lax.all_gather(package(w_up, flat_up), 'row', axis=0)]
    reduce_scatter x2 -> x0, waiting for transfers between devices: 224 us -> none  [the longest x1 176 us: reduce_kept(): lax.psum_scatter(sent, 'row', scatter_dimension=0, tiled=True)[0]]
    ppermute x0 -> x56, starting transfers between devices: none -> 59.6 us  [the longest x14 22.4 us: ring_gather(): b = lax.ppermute(b, 'row', left)]
    unnamed x28 -> x62, local copies, waits for them, and re-layouts: 48.7 us -> 79.1 us
    convert_element_type x4 -> x28, other arithmetic: 3.01 us -> 27.4 us  [the longest x12 16.9 us: ring_reduce(): acc_b = (in_b + sent_b[s + 1].astype(jnp.float32)).astype(jnp.bfloat16)]
    gather x2 -> x4, local copies, waits for them, and re-layouts: 50.2 us -> 70.3 us  [kept_blocks(): return view.at[rows, :, cols, :].get(mode='promise_in_bounds')]
    concatenate x1 -> x4, other arithmetic: 3.46 us -> 20.6 us  [the longest x2 20.2 us: ring_gather(): jnp.concatenate([jnp.stack(got_a).reshape((n_row * half, block, block)),...]
  transfers between devices with their start and end apart: 7 -> 59, of which waited for: 5 -> 35; matrix products, arithmetic and copies ran while one was open for 41% -> 25% of each run, Pallas kernels for 0% -> 0%
where the time goes in v6:
time: 993 us; the launch traced here: 984 us
  waiting for transfers between devices  376 us (38%)
  local copies, waits for them, and re-layouts  365 us (37%)
  other arithmetic  102 us (10%)
  matrix products  66.4 us (7%)
  starting transfers between devices  59.7 us (6%)
  between operations  14.8 us (1%)
    ppermute x14, waiting for transfers between devices, ring_reduce(): in_a = lax.ppermute(acc_a, 'row', right).astype(jnp.float32)  183 us
    ppermute x14, waiting for transfers between devices, ring_gather(): b = lax.ppermute(b, 'row', left)  179 us
    unnamed x62, local copies, waits for them, and re-layouts  79.1 us
    gather x4, local copies, waits for them, and re-layouts, kept_blocks(): return view.at[rows, :, cols, :].get(mode='promise_in_bounds')  70.3 us
    reshape x2, local copies, waits for them, and re-layouts, kept_blocks(): view = partial.astype(jnp.bfloat16).reshape((n_row * nr, block, nc, block))  64.4 us
    gather x2, local copies, waits for them, and re-layouts, rebuild(): dense = got.at[where_is(k).reshape(-1)].get(mode='promise_in_bounds')  47.9 us
    transpose x3, local copies, waits for them, and re-layouts, from_blocks(): x = jnp.moveaxis(x, k + 1, k + 2)  35.7 us
    sub x2, other arithmetic, adam_update(): return (weight - learn_rate * step_size, moment_new, second_new)  28.4 us
  transfers between devices with their start and end apart: 59, of which 35 were waited for; matrix products, arithmetic and copies ran while one was open for 25% of the time, Pallas kernels for 0%

profile of v6, /device:TPU:0, one launch (start us, length us, event | category | flops | bytes accessed | tf_op | source)
XLA Modules:
  0.0 984.0 jit_solution(3204564573859540680)
XLA Ops:
  26.3 18.1 %collective-permute-done.21 = bf16[25,128,128]{2,1,0:T(8,128)(2,1)S(1)} collective-permute-done((bf16[25,128,128]{2,1,0:T(8,128)(2,1)S(1)}, bf16[25,128,128]{2,1,0:T(8,128)(2,1)S(1)}, u32[]{:S(2)}, u32[]{:S(2)}) %collective-permute-start.21) | collective-permute-done | bytes 819232 | tf_op jit(solution)/shard_map/ppermute | solution.py:158
  48.5 15.5 %collective-permute-done.22 = bf16[25,128,128]{2,1,0:T(8,128)(2,1)S(1)} collective-permute-done((bf16[25,128,128]{2,1,0:T(8,128)(2,1)S(1)}, bf16[25,128,128]{2,1,0:T(8,128)(2,1)S(1)}, u32[]{:S(2)}, u32[]{:S(2)}) %collective-permute-start.22) | collective-permute-done | bytes 819232 | tf_op jit(solution)/shard_map/ppermute | solution.py:158
  69.0 13.8 %collective-permute-done.23 = bf16[25,128,128]{2,1,0:T(8,128)(2,1)} collective-permute-done((bf16[25,128,128]{2,1,0:T(8,128)(2,1)S(1)}, bf16[25,128,128]{2,1,0:T(8,128)(2,1)}, u32[]{:S(2)}, u32[]{:S(2)}) %collective-permute-start.23) | collective-permute-done | bytes 819232 | tf_op jit(solution)/shard_map/ppermute | solution.py:158
  85.4 15.9 %collective-permute-done.24 = bf16[25,128,128]{2,1,0:T(8,128)(2,1)S(1)} collective-permute-done((bf16[25,128,128]{2,1,0:T(8,128)(2,1)}, bf16[25,128,128]{2,1,0:T(8,128)(2,1)S(1)}, u32[]{:S(2)}, u32[]{:S(2)}) %collective-permute-start.24) | collective-permute-done | bytes 819232 | tf_op jit(solution)/shard_map/ppermute | solution.py:158
  176.0 23.9 %gather_fusion.4 = bf16[768,128,128]{2,1,0:T(8,128)(2,1)} fusion(bf16[400,128,128]{2,1,0:T(8,128)(2,1)} %pad_maximum_fusion.1, s32[1024]{0:T(1024)S(1)} %get-tuple-element.78), kind=kCustom, calls=%fused_computation.4 | custom fusion | bytes 50334720 | tf_op jit(solution)/shard_map/gather | solution.py:194
  199.9 28.3 %copy.55 = bf16[8,4,24,128,128]{4,2,3,1,0:T(8,128)(2,1)} copy(bf16[8,4,24,128,128]{4,3,2,1,0:T(8,128)(2,1)} %bitcast.188) | data formatting | bytes 50331648 | tf_op jit(solution)/shard_map/reshape;reshape | solution.py:54
  241.0 14.4 %convert_bitcast_fusion = bf16[384,8,32,128]{3,1,2,0:T(8,128)(2,1)} fusion(bf16[256,4096]{1,0:T(8,128)(2,1)} %all-gather.3.cloned.1.call-done, f32[256,3072]{0,1:T(8,128)S(1)} %fusion.19), kind=kOutput, calls=%fused_computation.24 | convolution fusion | flops 6458966016 | bytes 30408704 | tf_op jit(solution)/shard_map/dot_general | solution.py:36
  255.4 22.4 %copy.70 = bf16[384,8,32,128]{3,2,1,0:T(8,128)(2,1)} copy(bf16[384,8,32,128]{3,1,2,0:T(8,128)(2,1)} %convert_bitcast_fusion) | data formatting | bytes 50331648
  277.8 32.0 %copy.60 = bf16[32,128,24,128]{3,1,2,0:T(8,128)(2,1)} copy(bf16[32,128,24,128]{1,0,3,2:T(8,128)(2,1)} %bitcast.190) | data formatting | bytes 50331648 | tf_op jit(solution)/shard_map/reshape | solution.py:200
  309.8 17.6 %gather_fusion.15 = bf16[192,128,128]{2,1,0:T(8,128)(2,1)} fusion(bf16[32,128,24,128]{3,1,2,0:T(8,128)(2,1)} %copy.60, s32[192]{0:T(256)S(1)} %reshape.788), kind=kCustom, calls=%fused_computation.15 | custom fusion | bytes 12584448 | tf_op jit(solution)/shard_map/gather | solution.py:204
  330.6 17.6 %gather_fusion.13 = bf16[192,128,128]{2,1,0:T(8,128)(2,1)} fusion(bf16[32,128,24,128]{3,1,2,0:T(8,128)(2,1)} %copy.60, s32[192]{0:T(256)S(1)} %reshape.774), kind=kCustom, calls=%fused_computation.13 | custom fusion | bytes 12584448 | tf_op jit(solution)/shard_map/gather | solution.py:204
  371.1 14.3 %collective-permute-done.43 = bf16[24,128,128]{2,1,0:T(8,128)(2,1)S(1)} collective-permute-done((bf16[24,128,128]{2,1,0:T(8,128)(2,1)S(1)}, bf16[24,128,128]{2,1,0:T(8,128)(2,1)S(1)}, u32[]{:S(2)}, u32[]{:S(2)}) %collective-permute-start.43) | collective-permute-done | bytes 786464 | tf_op jit(solution)/shard_map/ppermute | solution.py:214
  389.5 15.4 %collective-permute-done.44 = bf16[24,128,128]{2,1,0:T(8,128)(2,1)S(1)} collective-permute-done((bf16[24,128,128]{2,1,0:T(8,128)(2,1)S(1)}, bf16[24,128,128]{2,1,0:T(8,128)(2,1)S(1)}, u32[]{:S(2)}, u32[]{:S(2)}) %collective-permute-start.44) | collective-permute-done | bytes 786464 | tf_op jit(solution)/shard_map/ppermute | solution.py:214
  408.7 16.8 %collective-permute-done.45 = bf16[24,128,128]{2,1,0:T(8,128)(2,1)S(1)} collective-permute-done((bf16[24,128,128]{2,1,0:T(8,128)(2,1)S(1)}, bf16[24,128,128]{2,1,0:T(8,128)(2,1)S(1)}, u32[]{:S(2)}, u32[]{:S(2)}) %collective-permute-start.45) | collective-permute-done | bytes 786464 | tf_op jit(solution)/shard_map/ppermute | solution.py:214
  429.4 16.3 %collective-permute-done.46 = bf16[24,128,128]{2,1,0:T(8,128)(2,1)S(1)} collective-permute-done((bf16[24,128,128]{2,1,0:T(8,128)(2,1)S(1)}, bf16[24,128,128]{2,1,0:T(8,128)(2,1)S(1)}, u32[]{:S(2)}, u32[]{:S(2)}) %collective-permute-start.46) | collective-permute-done | bytes 786464 | tf_op jit(solution)/shard_map/ppermute | solution.py:214
  451.1 15.0 %collective-permute-done.47 = bf16[24,128,128]{2,1,0:T(8,128)(2,1)S(1)} collective-permute-done((bf16[24,128,128]{2,1,0:T(8,128)(2,1)S(1)}, bf16[24,128,128]{2,1,0:T(8,128)(2,1)S(1)}, u32[]{:S(2)}, u32[]{:S(2)}) %collective-permute-start.47) | collective-permute-done | bytes 786464 | tf_op jit(solution)/shard_map/ppermute | solution.py:214
  491.9 16.7 %multiply_subtract_fusion = (f32[512,3072]{1,0:T(8,128)}, f32[512,3072]{1,0:T(8,128)}, f32[512,3072]{1,0:T(8,128)}, bf16[64,8,24,128]{3,1,2,0:T(8,128)(2,1)S(1)}) fusion(f32[512,3072]{1,0:T(8,128)} %param.23, f32[64,8,24,128]{3,2,1,0:T(8,128)S(1)} %bitcast.199, f32[512,3072]{1,0:T(8,128)} %param.28, f32[512,3072]{1,0:T(8,128)} %param.29), kind=kLoop, calls=%fused_computation.38 | loop fusion | flops 22020096 | bytes 47185920 | tf_op jit(solution)/shard_map/sub | solution.py:32
  519.0 16.2 %collective-permute-done.7 = bf16[25,128,128]{2,1,0:T(8,128)(2,1)S(1)} collective-permute-done((bf16[25,128,128]{2,1,0:T(8,128)(2,1)S(1)}, bf16[25,128,128]{2,1,0:T(8,128)(2,1)S(1)}, u32[]{:S(2)}, u32[]{:S(2)}) %collective-permute-start.7) | collective-permute-done | bytes 819232 | tf_op jit(solution)/shard_map/ppermute | solution.py:158
  537.2 16.2 %collective-permute-done.8 = bf16[25,128,128]{2,1,0:T(8,128)(2,1)S(1)} collective-permute-done((bf16[25,128,128]{2,1,0:T(8,128)(2,1)S(1)}, bf16[25,128,128]{2,1,0:T(8,128)(2,1)S(1)}, u32[]{:S(2)}, u32[]{:S(2)}) %collective-permute-start.8) | collective-permute-done | bytes 819232 | tf_op jit(solution)/shard_map/ppermute | solution.py:158
  555.6 16.0 %collective-permute-done.9 = bf16[25,128,128]{2,1,0:T(8,128)(2,1)} collective-permute-done((bf16[25,128,128]{2,1,0:T(8,128)(2,1)S(1)}, bf16[25,128,128]{2,1,0:T(8,128)(2,1)}, u32[]{:S(2)}, u32[]{:S(2)}) %collective-permute-start.9) | collective-permute-done | bytes 819232 | tf_op jit(solution)/shard_map/ppermute | solution.py:158
  573.7 16.5 %collective-permute-done.10 = bf16[25,128,128]{2,1,0:T(8,128)(2,1)} collective-permute-done((bf16[25,128,128]{2,1,0:T(8,128)(2,1)}, bf16[25,128,128]{2,1,0:T(8,128)(2,1)}, u32[]{:S(2)}, u32[]{:S(2)}) %collective-permute-start.10) | collective-permute-done | bytes 819232 | tf_op jit(solution)/shard_map/ppermute | solution.py:158
  648.3 23.9 %gather_fusion.3 = bf16[768,128,128]{2,1,0:T(8,128)(2,1)} fusion(bf16[400,128,128]{2,1,0:T(8,128)(2,1)} %pad_maximum_fusion, s32[1024]{0:T(1024)S(1)} %get-tuple-element.79), kind=kCustom, calls=%fused_computation.3 | custom fusion | bytes 50334720 | tf_op jit(solution)/shard_map/gather | solution.py:194
  672.3 28.4 %copy.54 = bf16[8,4,128,24,128]{4,3,2,1,0:T(8,128)(2,1)} copy(bf16[8,4,128,24,128]{4,2,3,1,0:T(8,128)(2,1)} %bitcast.189) | data formatting | bytes 50331648 | tf_op jit(solution)/shard_map/transpose | solution.py:56
  727.1 22.4 %copy.68 = bf16[384,8,32,128]{3,2,1,0:T(8,128)(2,1)} copy(bf16[384,8,32,128]{3,1,2,0:T(8,128)(2,1)} %convert_bitcast_fusion.1) | data formatting | bytes 50331648
  749.5 32.4 %copy.56 = bf16[32,128,24,128]{3,1,2,0:T(8,128)(2,1)} copy(bf16[32,128,24,128]{1,0,3,2:T(8,128)(2,1)} %bitcast.191) | data formatting | bytes 50331648 | tf_op jit(solution)/shard_map/reshape | solution.py:200
  781.9 17.6 %gather_fusion.10 = bf16[192,128,128]{2,1,0:T(8,128)(2,1)} fusion(bf16[32,128,24,128]{3,1,2,0:T(8,128)(2,1)} %copy.56, s32[192]{0:T(256)S(1)} %reshape.752), kind=kCustom, calls=%fused_computation.10 | custom fusion | bytes 12584448 | tf_op jit(solution)/shard_map/gather | solution.py:204
  800.9 17.6 %gather_fusion.7 = bf16[192,128,128]{2,1,0:T(8,128)(2,1)} fusion(bf16[32,128,24,128]{3,1,2,0:T(8,128)(2,1)} %copy.56, s32[192]{0:T(256)S(1)} %reshape.730), kind=kCustom, calls=%fused_computation.7 | custom fusion | bytes 12584448 | tf_op jit(solution)/shard_map/gather | solution.py:204
  823.3 15.2 %collective-permute-done.28 = bf16[24,128,128]{2,1,0:T(8,128)(2,1)S(1)} collective-permute-done((bf16[24,128,128]{2,1,0:T(8,128)(2,1)S(1)}, bf16[24,128,128]{2,1,0:T(8,128)(2,1)S(1)}, u32[]{:S(2)}, u32[]{:S(2)}) %collective-permute-start.28) | collective-permute-done | bytes 786464 | tf_op jit(solution)/shard_map/ppermute | solution.py:214
  843.9 15.8 %collective-permute-done.29 = bf16[24,128,128]{2,1,0:T(8,128)(2,1)S(1)} collective-permute-done((bf16[24,128,128]{2,1,0:T(8,128)(2,1)S(1)}, bf16[24,128,128]{2,1,0:T(8,128)(2,1)S(1)}, u32[]{:S(2)}, u32[]{:S(2)}) %collective-permute-start.29) | collective-permute-done | bytes 786464 | tf_op jit(solution)/shard_map/ppermute | solution.py:214
  863.8 16.3 %collective-permute-done.30 = bf16[24,128,128]{2,1,0:T(8,128)(2,1)S(1)} collective-permute-done((bf16[24,128,128]{2,1,0:T(8,128)(2,1)S(1)}, bf16[24,128,128]{2,1,0:T(8,128)(2,1)S(1)}, u32[]{:S(2)}, u32[]{:S(2)}) %collective-permute-start.30) | collective-permute-done | bytes 786464 | tf_op jit(solution)/shard_map/ppermute | solution.py:214
  883.9 16.8 %collective-permute-done.31 = bf16[24,128,128]{2,1,0:T(8,128)(2,1)S(1)} collective-permute-done((bf16[24,128,128]{2,1,0:T(8,128)(2,1)S(1)}, bf16[24,128,128]{2,1,0:T(8,128)(2,1)S(1)}, u32[]{:S(2)}, u32[]{:S(2)}) %collective-permute-start.31) | collective-permute-done | bytes 786464 | tf_op jit(solution)/shard_map/ppermute | solution.py:214
  904.5 16.6 %collective-permute-done.32 = bf16[24,128,128]{2,1,0:T(8,128)(2,1)S(1)} collective-permute-done((bf16[24,128,128]{2,1,0:T(8,128)(2,1)S(1)}, bf16[24,128,128]{2,1,0:T(8,128)(2,1)S(1)}, u32[]{:S(2)}, u32[]{:S(2)}) %collective-permute-start.32) | collective-permute-done | bytes 786464 | tf_op jit(solution)/shard_map/ppermute | solution.py:214
  (301 shorter events, 367.2 us)
Async XLA Ops:
  7.2 221.5 %all-gather.5.cloned.1.call-start = ((), (), s32[]{:S(2)}) async-start(), calls=%async_computation.2 | async-start | bytes 2621440 | tf_op jit(solution)/shard_map/all_gather | solution.py:188
  7.9 233.1 %all-gather.3.cloned.1.call-start = ((), (), s32[]{:S(2)}) async-start(), calls=%async_computation.1 | async-start | bytes 2621440 | tf_op jit(solution)/shard_map/all_gather | solution.py:189
  23.0 21.4 %collective-permute-start.21 = (bf16[25,128,128]{2,1,0:T(8,128)(2,1)S(1)}, bf16[25,128,128]{2,1,0:T(8,128)(2,1)S(1)}, u32[]{:S(2)}, u32[]{:S(2)}) collective-permute-start(bf16[25,128,128]{2,1,0:T(8,128)(2,1)S(1)} %get-tuple-element.64), channel_id=1, source_target_pairs={{0,8},{4,0},{12,4},{20,12},{28,20},{24,28},{16,24},{8,16},{1,9},{5... | collective-permute-start | bytes 2457608 | tf_op jit(solution)/shard_map/ppermute | solution.py:158
  26.2 20.0 %collective-permute-start.14 = (bf16[25,128,128]{2,1,0:T(8,128)(2,1)S(1)}, bf16[25,128,128]{2,1,0:T(8,128)(2,1)S(1)}, u32[]{:S(2)}, u32[]{:S(2)}) collective-permute-start(bf16[25,128,128]{2,1,0:T(8,128)(2,1)S(1)} %slice.310), channel_id=1, source_target_pairs={{0,4},{4,12},{12,20},{20,28},{28,24},{24,16},{16,8},{8,0},{1,5},{5... | collective-permute-start | bytes 2457608 | tf_op jit(solution)/shard_map/ppermute | solution.py:157
  44.4 19.5 %collective-permute-start.22 = (bf16[25,128,128]{2,1,0:T(8,128)(2,1)S(1)}, bf16[25,128,128]{2,1,0:T(8,128)(2,1)S(1)}, u32[]{:S(2)}, u32[]{:S(2)}) collective-permute-start(bf16[25,128,128]{2,1,0:T(8,128)(2,1)S(1)} %collective-permute-done.21), channel_id=1, source_target_pairs={{0,8},{4,0},{12,4},{20,12},{28,20},{24,28},{16,24},{8,16},{1,9},{5... | collective-permute-start | bytes 2457608 | tf_op jit(solution)/shard_map/ppermute | solution.py:158
  46.2 19.9 %collective-permute-start.15 = (bf16[25,128,128]{2,1,0:T(8,128)(2,1)S(1)}, bf16[25,128,128]{2,1,0:T(8,128)(2,1)}, u32[]{:S(2)}, u32[]{:S(2)}) collective-permute-start(bf16[25,128,128]{2,1,0:T(8,128)(2,1)S(1)} %collective-permute-done.14), channel_id=1, source_target_pairs={{0,4},{4,12},{12,20},{20,28},{28,24},{24,16},{16,8},{8,0},{1,5},{5... | collective-permute-start | bytes 2457608 | tf_op jit(solution)/shard_map/ppermute | solution.py:157
  46.5 930.8 %reduce-scatter.2.cloned.1.call-start = ((), (), s32[]{:S(2)}) async-start(), calls=%async_computation.3 | async-start | bytes 2621440 | tf_op jit(solution)/shard_map/reduce_scatter | solution.py:243
  63.9 18.8 %collective-permute-start.23 = (bf16[25,128,128]{2,1,0:T(8,128)(2,1)S(1)}, bf16[25,128,128]{2,1,0:T(8,128)(2,1)}, u32[]{:S(2)}, u32[]{:S(2)}) collective-permute-start(bf16[25,128,128]{2,1,0:T(8,128)(2,1)S(1)} %collective-permute-done.22), channel_id=1, source_target_pairs={{0,8},{4,0},{12,4},{20,12},{28,20},{24,28},{16,24},{8,16},{1,9},{5... | collective-permute-start | bytes 2457608 | tf_op jit(solution)/shard_map/ppermute | solution.py:158
  82.7 18.6 %collective-permute-start.24 = (bf16[25,128,128]{2,1,0:T(8,128)(2,1)}, bf16[25,128,128]{2,1,0:T(8,128)(2,1)S(1)}, u32[]{:S(2)}, u32[]{:S(2)}) collective-permute-start(bf16[25,128,128]{2,1,0:T(8,128)(2,1)} %collective-permute-done.23), channel_id=1, source_target_pairs={{0,8},{4,0},{12,4},{20,12},{28,20},{24,28},{16,24},{8,16},{1,9},{5... | collective-permute-start | bytes 2457608 | tf_op jit(solution)/shard_map/ppermute | solution.py:158
  84.6 18.9 %collective-permute-start.17 = (bf16[25,128,128]{2,1,0:T(8,128)(2,1)}, bf16[25,128,128]{2,1,0:T(8,128)(2,1)S(1)}, u32[]{:S(2)}, u32[]{:S(2)}) collective-permute-start(bf16[25,128,128]{2,1,0:T(8,128)(2,1)} %collective-permute-done.16), channel_id=1, source_target_pairs={{0,4},{4,12},{12,20},{20,28},{28,24},{24,16},{16,8},{8,0},{1,5},{5... | collective-permute-start | bytes 2457608 | tf_op jit(solution)/shard_map/ppermute | solution.py:157
  103.5 19.6 %collective-permute-start.18 = (bf16[25,128,128]{2,1,0:T(8,128)(2,1)S(1)}, bf16[25,128,128]{2,1,0:T(8,128)(2,1)S(1)}, u32[]{:S(2)}, u32[]{:S(2)}) collective-permute-start(bf16[25,128,128]{2,1,0:T(8,128)(2,1)S(1)} %collective-permute-done.17), channel_id=1, source_target_pairs={{0,4},{4,12},{12,20},{20,28},{28,24},{24,16},{16,8},{8,0},{1,5},{5... | collective-permute-start | bytes 2457608 | tf_op jit(solution)/shard_map/ppermute | solution.py:157
  328.6 21.2 %collective-permute-start.49 = (bf16[24,128,128]{2,1,0:T(8,128)(2,1)S(1)}, bf16[24,128,128]{2,1,0:T(8,128)(2,1)S(1)}, u32[]{:S(2)}, u32[]{:S(2)}) collective-permute-start(bf16[24,128,128]{2,1,0:T(8,128)(2,1)S(1)} %slice.337), channel_id=1, source_target_pairs={{0,8},{4,0},{12,4},{20,12},{28,20},{24,28},{16,24},{8,16},{1,9},{5... | collective-permute-start | bytes 2359304 | tf_op jit(solution)/shard_map/ppermute | solution.py:215
  385.7 19.2 %collective-permute-start.44 = (bf16[24,128,128]{2,1,0:T(8,128)(2,1)S(1)}, bf16[24,128,128]{2,1,0:T(8,128)(2,1)S(1)}, u32[]{:S(2)}, u32[]{:S(2)}) collective-permute-start(bf16[24,128,128]{2,1,0:T(8,128)(2,1)S(1)} %fusion.42), channel_id=1, source_target_pairs={{0,4},{4,12},{12,20},{20,28},{28,24},{24,16},{16,8},{8,0},{1,5},{5... | collective-permute-start | bytes 2359304 | tf_op jit(solution)/shard_map/ppermute | solution.py:214
  405.2 20.4 %collective-permute-start.45 = (bf16[24,128,128]{2,1,0:T(8,128)(2,1)S(1)}, bf16[24,128,128]{2,1,0:T(8,128)(2,1)S(1)}, u32[]{:S(2)}, u32[]{:S(2)}) collective-permute-start(bf16[24,128,128]{2,1,0:T(8,128)(2,1)S(1)} %fusion.41), channel_id=1, source_target_pairs={{0,4},{4,12},{12,20},{20,28},{28,24},{24,16},{16,8},{8,0},{1,5},{5... | collective-permute-start | bytes 2359304 | tf_op jit(solution)/shard_map/ppermute | solution.py:214
  406.6 19.3 %collective-permute-start.53 = (bf16[24,128,128]{2,1,0:T(8,128)(2,1)S(1)}, bf16[24,128,128]{2,1,0:T(8,128)(2,1)S(1)}, u32[]{:S(2)}, u32[]{:S(2)}) collective-permute-start(bf16[24,128,128]{2,1,0:T(8,128)(2,1)S(1)} %fusion.34), channel_id=1, source_target_pairs={{0,8},{4,0},{12,4},{20,12},{28,20},{24,28},{16,24},{8,16},{1,9},{5... | collective-permute-start | bytes 2359304 | tf_op jit(solution)/shard_map/ppermute | solution.py:215
  425.8 19.8 %collective-permute-start.46 = (bf16[24,128,128]{2,1,0:T(8,128)(2,1)S(1)}, bf16[24,128,128]{2,1,0:T(8,128)(2,1)S(1)}, u32[]{:S(2)}, u32[]{:S(2)}) collective-permute-start(bf16[24,128,128]{2,1,0:T(8,128)(2,1)S(1)} %fusion.40), channel_id=1, source_target_pairs={{0,4},{4,12},{12,20},{20,28},{28,24},{24,16},{16,8},{8,0},{1,5},{5... | collective-permute-start | bytes 2359304 | tf_op jit(solution)/shard_map/ppermute | solution.py:214
  427.3 20.4 %collective-permute-start.54 = (bf16[24,128,128]{2,1,0:T(8,128)(2,1)S(1)}, bf16[24,128,128]{2,1,0:T(8,128)(2,1)S(1)}, u32[]{:S(2)}, u32[]{:S(2)}) collective-permute-start(bf16[24,128,128]{2,1,0:T(8,128)(2,1)S(1)} %fusion.33), channel_id=1, source_target_pairs={{0,8},{4,0},{12,4},{20,12},{28,20},{24,28},{16,24},{8,16},{1,9},{5... | collective-permute-start | bytes 2359304 | tf_op jit(solution)/shard_map/ppermute | solution.py:215
  445.9 20.2 %collective-permute-start.47 = (bf16[24,128,128]{2,1,0:T(8,128)(2,1)S(1)}, bf16[24,128,128]{2,1,0:T(8,128)(2,1)S(1)}, u32[]{:S(2)}, u32[]{:S(2)}) collective-permute-start(bf16[24,128,128]{2,1,0:T(8,128)(2,1)S(1)} %fusion.39), channel_id=1, source_target_pairs={{0,4},{4,12},{12,20},{20,28},{28,24},{24,16},{16,8},{8,0},{1,5},{5... | collective-permute-start | bytes 2359304 | tf_op jit(solution)/shard_map/ppermute | solution.py:214
  449.1 19.1 %collective-permute-start.55 = (bf16[24,128,128]{2,1,0:T(8,128)(2,1)S(1)}, bf16[24,128,128]{2,1,0:T(8,128)(2,1)S(1)}, u32[]{:S(2)}, u32[]{:S(2)}) collective-permute-start(bf16[24,128,128]{2,1,0:T(8,128)(2,1)S(1)} %fusion.32), channel_id=1, source_target_pairs={{0,8},{4,0},{12,4},{20,12},{28,20},{24,28},{16,24},{8,16},{1,9},{5... | collective-permute-start | bytes 2359304 | tf_op jit(solution)/shard_map/ppermute | solution.py:215
  571.6 18.6 %collective-permute-start.10 = (bf16[25,128,128]{2,1,0:T(8,128)(2,1)}, bf16[25,128,128]{2,1,0:T(8,128)(2,1)}, u32[]{:S(2)}, u32[]{:S(2)}) collective-permute-start(bf16[25,128,128]{2,1,0:T(8,128)(2,1)} %collective-permute-done.9), channel_id=1, source_target_pairs={{0,8},{4,0},{12,4},{20,12},{28,20},{24,28},{16,24},{8,16},{1,9},{5... | collective-permute-start | bytes 2457608 | tf_op jit(solution)/shard_map/ppermute | solution.py:158
  573.2 19.6 %collective-permute-start.3 = (bf16[25,128,128]{2,1,0:T(8,128)(2,1)S(1)}, bf16[25,128,128]{2,1,0:T(8,128)(2,1)}, u32[]{:S(2)}, u32[]{:S(2)}) collective-permute-start(bf16[25,128,128]{2,1,0:T(8,128)(2,1)S(1)} %collective-permute-done.2), channel_id=1, source_target_pairs={{0,4},{4,12},{12,20},{20,28},{28,24},{24,16},{16,8},{8,0},{1,5},{5... | collective-permute-start | bytes 2457608 | tf_op jit(solution)/shard_map/ppermute | solution.py:157
  590.2 18.6 %collective-permute-start.11 = (bf16[25,128,128]{2,1,0:T(8,128)(2,1)}, bf16[25,128,128]{2,1,0:T(8,128)(2,1)S(1)}, u32[]{:S(2)}, u32[]{:S(2)}) collective-permute-start(bf16[25,128,128]{2,1,0:T(8,128)(2,1)} %collective-permute-done.10), channel_id=1, source_target_pairs={{0,8},{4,0},{12,4},{20,12},{28,20},{24,28},{16,24},{8,16},{1,9},{5... | collective-permute-start | bytes 2457608 | tf_op jit(solution)/shard_map/ppermute | solution.py:158
  592.8 19.8 %collective-permute-start.4 = (bf16[25,128,128]{2,1,0:T(8,128)(2,1)}, bf16[25,128,128]{2,1,0:T(8,128)(2,1)S(1)}, u32[]{:S(2)}, u32[]{:S(2)}) collective-permute-start(bf16[25,128,128]{2,1,0:T(8,128)(2,1)} %collective-permute-done.3), channel_id=1, source_target_pairs={{0,4},{4,12},{12,20},{20,28},{28,24},{24,16},{16,8},{8,0},{1,5},{5... | collective-permute-start | bytes 2457608 | tf_op jit(solution)/shard_map/ppermute | solution.py:157
  800.7 21.1 %collective-permute-start.35 = (bf16[24,128,128]{2,1,0:T(8,128)(2,1)S(1)}, bf16[24,128,128]{2,1,0:T(8,128)(2,1)S(1)}, u32[]{:S(2)}, u32[]{:S(2)}) collective-permute-start(bf16[24,128,128]{2,1,0:T(8,128)(2,1)S(1)} %slice.321), channel_id=1, source_target_pairs={{0,8},{4,0},{12,4},{20,12},{28,20},{24,28},{16,24},{8,16},{1,9},{5... | collective-permute-start | bytes 2359304 | tf_op jit(solution)/shard_map/ppermute | solution.py:215
  819.8 18.7 %collective-permute-start.28 = (bf16[24,128,128]{2,1,0:T(8,128)(2,1)S(1)}, bf16[24,128,128]{2,1,0:T(8,128)(2,1)S(1)}, u32[]{:S(2)}, u32[]{:S(2)}) collective-permute-start(bf16[24,128,128]{2,1,0:T(8,128)(2,1)S(1)} %slice.313), channel_id=1, source_target_pairs={{0,4},{4,12},{12,20},{20,28},{28,24},{24,16},{16,8},{8,0},{1,5},{5... | collective-permute-start | bytes 2359304 | tf_op jit(solution)/shard_map/ppermute | solution.py:214
  823.2 19.3 %collective-permute-start.36 = (bf16[24,128,128]{2,1,0:T(8,128)(2,1)S(1)}, bf16[24,128,128]{2,1,0:T(8,128)(2,1)S(1)}, u32[]{:S(2)}, u32[]{:S(2)}) collective-permute-start(bf16[24,128,128]{2,1,0:T(8,128)(2,1)S(1)} %fusion.49), channel_id=1, source_target_pairs={{0,8},{4,0},{12,4},{20,12},{28,20},{24,28},{16,24},{8,16},{1,9},{5... | collective-permute-start | bytes 2359304 | tf_op jit(solution)/shard_map/ppermute | solution.py:215
  839.9 19.8 %collective-permute-start.29 = (bf16[24,128,128]{2,1,0:T(8,128)(2,1)S(1)}, bf16[24,128,128]{2,1,0:T(8,128)(2,1)S(1)}, u32[]{:S(2)}, u32[]{:S(2)}) collective-permute-start(bf16[24,128,128]{2,1,0:T(8,128)(2,1)S(1)} %fusion.55), channel_id=1, source_target_pairs={{0,4},{4,12},{12,20},{20,28},{28,24},{24,16},{16,8},{8,0},{1,5},{5... | collective-permute-start | bytes 2359304 | tf_op jit(solution)/shard_map/ppermute | solution.py:214
  860.0 20.1 %collective-permute-start.30 = (bf16[24,128,128]{2,1,0:T(8,128)(2,1)S(1)}, bf16[24,128,128]{2,1,0:T(8,128)(2,1)S(1)}, u32[]{:S(2)}, u32[]{:S(2)}) collective-permute-start(bf16[24,128,128]{2,1,0:T(8,128)(2,1)S(1)} %fusion.54), channel_id=1, source_target_pairs={{0,4},{4,12},{12,20},{20,28},{28,24},{24,16},{16,8},{8,0},{1,5},{5... | collective-permute-start | bytes 2359304 | tf_op jit(solution)/shard_map/ppermute | solution.py:214
  880.4 20.3 %collective-permute-start.31 = (bf16[24,128,128]{2,1,0:T(8,128)(2,1)S(1)}, bf16[24,128,128]{2,1,0:T(8,128)(2,1)S(1)}, u32[]{:S(2)}, u32[]{:S(2)}) collective-permute-start(bf16[24,128,128]{2,1,0:T(8,128)(2,1)S(1)} %fusion.53), channel_id=1, source_target_pairs={{0,4},{4,12},{12,20},{20,28},{28,24},{24,16},{16,8},{8,0},{1,5},{5... | collective-permute-start | bytes 2359304 | tf_op jit(solution)/shard_map/ppermute | solution.py:214
  882.7 18.6 %collective-permute-start.39 = (bf16[24,128,128]{2,1,0:T(8,128)(2,1)S(1)}, bf16[24,128,128]{2,1,0:T(8,128)(2,1)S(1)}, u32[]{:S(2)}, u32[]{:S(2)}) collective-permute-start(bf16[24,128,128]{2,1,0:T(8,128)(2,1)S(1)} %fusion.46), channel_id=1, source_target_pairs={{0,8},{4,0},{12,4},{20,12},{28,20},{24,28},{16,24},{8,16},{1,9},{5... | collective-permute-start | bytes 2359304 | tf_op jit(solution)/shard_map/ppermute | solution.py:215
  901.0 20.2 %collective-permute-start.32 = (bf16[24,128,128]{2,1,0:T(8,128)(2,1)S(1)}, bf16[24,128,128]{2,1,0:T(8,128)(2,1)S(1)}, u32[]{:S(2)}, u32[]{:S(2)}) collective-permute-start(bf16[24,128,128]{2,1,0:T(8,128)(2,1)S(1)} %fusion.52), channel_id=1, source_target_pairs={{0,4},{4,12},{12,20},{20,28},{28,24},{24,16},{16,8},{8,0},{1,5},{5... | collective-permute-start | bytes 2359304 | tf_op jit(solution)/shard_map/ppermute | solution.py:214
  902.7 33.3 %collective-permute-start.40 = (bf16[24,128,128]{2,1,0:T(8,128)(2,1)S(1)}, bf16[24,128,128]{2,1,0:T(8,128)(2,1)S(1)}, u32[]{:S(2)}, u32[]{:S(2)}) collective-permute-start(bf16[24,128,128]{2,1,0:T(8,128)(2,1)S(1)} %fusion.45), channel_id=1, source_target_pairs={{0,8},{4,0},{12,4},{20,12},{28,20},{24,28},{16,24},{8,16},{1,9},{5... | collective-permute-start | bytes 2359304 | tf_op jit(solution)/shard_map/ppermute | solution.py:215
  (44 other events, 906.6 us)
Sparse Core Ops, SparseCore 0:
  9.6 25.2 all-gather.4
  46.6 23.9 all-gather.2
  936.1 29.8 reduce-scatter.1

commit v7 on v6

--- a/solution.py
+++ b/solution.py
@@ -177,7 +177,7 @@
         )
 
     got_up = ring_gather(package(w_up, flat_up))
-    got_down = ring_gather(package(w_down, flat_down))
+    got_down = lax.all_gather(package(w_down, flat_down), "row", axis=0)
     mask_blocks = got_up.at[where_is(jnp.full((n_row, 1), mask_slot, jnp.int32))[:, 0]].get(
         mode="promise_in_bounds"
     )
@@ -189,12 +189,15 @@
         lax.all_gather(cotangent, "col", axis=1, tiled=True),
     )
 
-    def rebuild(got, masks):
+    def rebuild(got, masks, at):
         k = jnp.where(masks > 0, slot_of(masks), zero_slot)
-        dense = got.at[where_is(k).reshape(-1)].get(mode="promise_in_bounds")
+        dense = got.at[at(k).reshape(-1)].get(mode="promise_in_bounds")
         dense = dense.reshape((n_row, nb, block, block))
         dense = from_blocks(dense, nr, nc)
         return dense.reshape((n_row * nr * block, nc * block))
+
+    def in_order(k):
+        return (rows_n * width)[:, None] + k
 
     def kept_blocks(partial, masks, dest, lo, hi):
         view = partial.astype(jnp.bfloat16).reshape((n_row * nr, block, nc, block))
@@ -203,12 +206,14 @@
         cols = idx % nc
         return view.at[rows, :, cols, :].get(mode="promise_in_bounds")
 
-    def ring_reduce(partial, masks):
+    def ring_reduce(partial, masks, hold=None):
         ha = (slots + 1) // 2
         dest_a = ring_of[(p - rows_n) % n_row]
         dest_b = ring_of[(p + rows_n) % n_row]
         sent_a = kept_blocks(partial, masks, dest_a, 0, ha)
         sent_b = kept_blocks(partial, masks, dest_b, ha, slots)
+        if hold is not None:
+            hold, sent_a, sent_b = lax.optimization_barrier((hold, sent_a, sent_b))
         acc_a, acc_b = sent_a[1], sent_b[1]
         for s in range(1, n_row):
             in_a = lax.ppermute(acc_a, "row", right).astype(jnp.float32)
@@ -218,7 +223,7 @@
                 acc_b = (in_b + sent_b[s + 1].astype(jnp.float32)).astype(jnp.bfloat16)
         total_a = in_a + sent_a[0].astype(jnp.float32)
         total_b = in_b + sent_b[0].astype(jnp.float32)
-        return jnp.concatenate([total_a, total_b], axis=0)
+        return jnp.concatenate([total_a, total_b], axis=0), hold
 
     def unpack(summed, own):
         dense = summed.at[slot_of(own)].get(mode="promise_in_bounds")
@@ -226,19 +231,23 @@
         dense = jnp.where(keep, dense, jnp.zeros(dense.shape, jnp.float32))
         return from_blocks(dense, nr, nc)
 
-    up_whole = rebuild(got_up, masks_up)
+    up_whole = rebuild(got_up, masks_up, where_is)
     preact = jnp.dot(features, up_whole, preferred_element_type=jnp.float32)
     gelu_value, gelu_slope = gelu_parts(preact)
     activation = gelu_value.astype(jnp.bfloat16)
-    grad_down = unpack(ring_reduce(token_product(cot_rows, activation), masks_down), flat_down)
-
-    down_whole = rebuild(got_down, masks_down)
+    sent_down = kept_blocks(token_product(cot_rows, activation), masks_down, rows_n, 0, slots)
+    got_down, sent_down = lax.optimization_barrier((got_down, sent_down))
+    summed_down = lax.psum_scatter(sent_down, "row", scatter_dimension=0, tiled=True)[0]
+
+    down_whole = rebuild(got_down.reshape((n_row * width, block, block)), masks_down, in_order)
     act_grad = jnp.dot(cot_rows, down_whole, preferred_element_type=jnp.float32)
     pre_grad = (act_grad * gelu_slope).astype(jnp.bfloat16)
     partial_tokens = lax.dot_general(
         pre_grad, up_whole, (((1,), (1,)), ((), ())), preferred_element_type=jnp.float32
     )
-    grad_up = unpack(ring_reduce(token_product(features, pre_grad), masks_up), flat_up)
+    summed_up, summed_down = ring_reduce(token_product(features, pre_grad), masks_up, summed_down)
+    grad_down = unpack(summed_down.astype(jnp.float32), flat_down)
+    grad_up = unpack(summed_up, flat_up)
 
     token_grad = lax.psum_scatter(
         partial_tokens.astype(jnp.bfloat16), "col", scatter_dimension=1, tiled=True

time: 993 us -> 890 us (0.90)
  waiting for transfers between devices: 376 us -> 287 us
  starting transfers between devices: 59.7 us -> 91.4 us
  local copies, waits for them, and re-layouts: 365 us -> 335 us
  other arithmetic: 102 us -> 85 us
    ppermute x14 -> x7, waiting for transfers between devices: 183 us -> 62.4 us  [ring_reduce(): in_a = lax.ppermute(acc_a, 'row', right).astype(jnp.float32)]
    ppermute x14 -> x7, starting transfers between devices: 22.4 us -> 76.1 us  [ring_gather(): b = lax.ppermute(b, 'row', left)]
    reduce_scatter x0 -> x1, waiting for transfers between devices: none -> 30.6 us  [shards(): lax.psum_scatter(sent_down, 'row', scatter_dimension=0, tiled=True)[0]]
    ppermute x14 -> x7, waiting for transfers between devices: 3.3 us -> 30.5 us  [ring_gather(): a = lax.ppermute(a, 'row', right)]
    ppermute x14 -> x7, waiting for transfers between devices: 179 us -> 161 us  [ring_gather(): b = lax.ppermute(b, 'row', left)]
    ppermute x14 -> x7, starting transfers between devices: 19.5 us -> 4.3 us  [ring_reduce(): in_b = lax.ppermute(acc_b, 'row', left).astype(jnp.float32)]
    unnamed x62 -> x42, local copies, waits for them, and re-layouts: 79.1 us -> 64.6 us
    gather x4 -> x3, local copies, waits for them, and re-layouts: 70.3 us -> 60.4 us  [kept_blocks(): return view.at[rows, :, cols, :].get(mode='promise_in_bounds')]
  transfers between devices with their start and end apart: 59 -> 33, of which waited for: 35 -> 19; matrix products, arithmetic and copies ran while one was open for 25% -> 55% of each run, Pallas kernels for 0% -> 0%
where the time goes in v7:
time: 890 us; the launch traced here: 879 us
  local copies, waits for them, and re-layouts  335 us (38%)
  waiting for transfers between devices  287 us (32%)
  starting transfers between devices  91.4 us (10%)
  other arithmetic  85 us (10%)
  matrix products  65.9 us (7%)
  between operations  14.6 us (2%)
    ppermute x7, waiting for transfers between devices, ring_gather(): b = lax.ppermute(b, 'row', left)  161 us
    ppermute x7, starting transfers between devices, ring_gather(): b = lax.ppermute(b, 'row', left)  76.1 us
    reshape x2, local copies, waits for them, and re-layouts, kept_blocks(): view = partial.astype(jnp.bfloat16).reshape((n_row * nr, block, nc, block))  65 us
    unnamed x42, local copies, waits for them, and re-layouts  64.6 us
    ppermute x7, waiting for transfers between devices, ring_reduce(): in_a = lax.ppermute(acc_a, 'row', right).astype(jnp.float32)  62.4 us
    gather x3, local copies, waits for them, and re-layouts, kept_blocks(): return view.at[rows, :, cols, :].get(mode='promise_in_bounds')  60.4 us
    gather x2, local copies, waits for them, and re-layouts, rebuild(): dense = got.at[at(k).reshape(-1)].get(mode='promise_in_bounds')  49 us
    transpose x3, local copies, waits for them, and re-layouts, from_blocks(): x = jnp.moveaxis(x, k + 1, k + 2)  35.9 us
  transfers between devices with their start and end apart: 33, of which 19 were waited for; matrix products, arithmetic and copies ran while one was open for 55% of the time, Pallas kernels for 0%

profile of v7, /device:TPU:0, one launch (start us, length us, event | category | flops | bytes accessed | tf_op | source)
XLA Modules:
  0.0 878.8 jit_solution(7086127715367903118)
XLA Ops:
  37.5 18.2 %collective-permute-done.7 = bf16[25,128,128]{2,1,0:T(8,128)(2,1)S(1)} collective-permute-done((bf16[25,128,128]{2,1,0:T(8,128)(2,1)S(1)}, bf16[25,128,128]{2,1,0:T(8,128)(2,1)S(1)}, u32[]{:S(2)}, u32[]{:S(2)}) %collective-permute-start.7) | collective-permute-done | bytes 819232 | tf_op jit(solution)/shard_map/ppermute | solution.py:158
  57.7 21.5 %collective-permute-done.8 = bf16[25,128,128]{2,1,0:T(8,128)(2,1)} collective-permute-done((bf16[25,128,128]{2,1,0:T(8,128)(2,1)S(1)}, bf16[25,128,128]{2,1,0:T(8,128)(2,1)}, u32[]{:S(2)}, u32[]{:S(2)}) %collective-permute-start.8) | collective-permute-done | bytes 819232 | tf_op jit(solution)/shard_map/ppermute | solution.py:158
  86.4 31.9 %collective-permute-done.9 = bf16[25,128,128]{2,1,0:T(8,128)(2,1)} collective-permute-done((bf16[25,128,128]{2,1,0:T(8,128)(2,1)}, bf16[25,128,128]{2,1,0:T(8,128)(2,1)}, u32[]{:S(2)}, u32[]{:S(2)}) %collective-permute-start.9) | collective-permute-done | bytes 819232 | tf_op jit(solution)/shard_map/ppermute | solution.py:158
  118.2 20.4 %collective-permute-start.10 = (bf16[25,128,128]{2,1,0:T(8,128)(2,1)}, bf16[25,128,128]{2,1,0:T(8,128)(2,1)}, u32[]{:S(2)}, u32[]{:S(2)}) collective-permute-start(bf16[25,128,128]{2,1,0:T(8,128)(2,1)} %collective-permute-done.9), channel_id=1, source_target_pairs={{0,8},{4,0},{12,4},{20,12},{28,20},{24,28},{16,24},{8,16},{1,9},{5... | collective-permute-start | bytes 2457608 | tf_op jit(solution)/shard_map/ppermute | solution.py:158
  143.3 19.4 %collective-permute-done.10 = bf16[25,128,128]{2,1,0:T(8,128)(2,1)} collective-permute-done((bf16[25,128,128]{2,1,0:T(8,128)(2,1)}, bf16[25,128,128]{2,1,0:T(8,128)(2,1)}, u32[]{:S(2)}, u32[]{:S(2)}) %collective-permute-start.10) | collective-permute-done | bytes 819232 | tf_op jit(solution)/shard_map/ppermute | solution.py:158
  171.6 25.5 %collective-permute-done.11 = bf16[25,128,128]{2,1,0:T(8,128)(2,1)S(1)} collective-permute-done((bf16[25,128,128]{2,1,0:T(8,128)(2,1)}, bf16[25,128,128]{2,1,0:T(8,128)(2,1)S(1)}, u32[]{:S(2)}, u32[]{:S(2)}) %collective-permute-start.11) | collective-permute-done | bytes 819232 | tf_op jit(solution)/shard_map/ppermute | solution.py:158
  197.1 18.5 %collective-permute-start.12 = (bf16[25,128,128]{2,1,0:T(8,128)(2,1)S(1)}, bf16[25,128,128]{2,1,0:T(8,128)(2,1)S(1)}, u32[]{:S(2)}, u32[]{:S(2)}) collective-permute-start(bf16[25,128,128]{2,1,0:T(8,128)(2,1)S(1)} %collective-permute-done.11), channel_id=1, source_target_pairs={{0,8},{4,0},{12,4},{20,12},{28,20},{24,28},{16,24},{8,16},{1,9},{5... | collective-permute-start | bytes 2457608 | tf_op jit(solution)/shard_map/ppermute | solution.py:158
  225.0 23.7 %collective-permute-done.12 = bf16[25,128,128]{2,1,0:T(8,128)(2,1)S(1)} collective-permute-done((bf16[25,128,128]{2,1,0:T(8,128)(2,1)S(1)}, bf16[25,128,128]{2,1,0:T(8,128)(2,1)S(1)}, u32[]{:S(2)}, u32[]{:S(2)}) %collective-permute-start.12) | collective-permute-done | bytes 819232 | tf_op jit(solution)/shard_map/ppermute | solution.py:158
  248.6 24.2 %collective-permute-start.13 = (bf16[25,128,128]{2,1,0:T(8,128)(2,1)S(1)}, bf16[25,128,128]{2,1,0:T(8,128)(2,1)S(1)}, u32[]{:S(2)}, u32[]{:S(2)}) collective-permute-start(bf16[25,128,128]{2,1,0:T(8,128)(2,1)S(1)} %collective-permute-done.12), channel_id=1, source_target_pairs={{0,8},{4,0},{12,4},{20,12},{28,20},{24,28},{16,24},{8,16},{1,9},{5... | collective-permute-start | bytes 2457608 | tf_op jit(solution)/shard_map/ppermute | solution.py:158
  279.8 21.1 %collective-permute-done.13 = bf16[25,128,128]{2,1,0:T(8,128)(2,1)S(1)} collective-permute-done((bf16[25,128,128]{2,1,0:T(8,128)(2,1)S(1)}, bf16[25,128,128]{2,1,0:T(8,128)(2,1)S(1)}, u32[]{:S(2)}, u32[]{:S(2)}) %collective-permute-start.13) | collective-permute-done | bytes 819232 | tf_op jit(solution)/shard_map/ppermute | solution.py:158
  302.0 21.7 %collective-permute-done.6 = bf16[25,128,128]{2,1,0:T(8,128)(2,1)S(1)} collective-permute-done((bf16[25,128,128]{2,1,0:T(8,128)(2,1)S(1)}, bf16[25,128,128]{2,1,0:T(8,128)(2,1)S(1)}, u32[]{:S(2)}, u32[]{:S(2)}) %collective-permute-start.6) | collective-permute-done | bytes 819232 | tf_op jit(solution)/shard_map/ppermute | solution.py:157
  342.3 23.9 %gather_fusion.3 = bf16[768,128,128]{2,1,0:T(8,128)(2,1)} fusion(bf16[400,128,128]{2,1,0:T(8,128)(2,1)} %pad_maximum_fusion, s32[1024]{0:T(1024)S(1)} %get-tuple-element.81), kind=kCustom, calls=%fused_computation.3 | custom fusion | bytes 50334720 | tf_op jit(solution)/shard_map/gather | solution.py:194
  366.2 28.3 %copy.77 = bf16[8,4,24,128,128]{4,2,3,1,0:T(8,128)(2,1)} copy(bf16[8,4,24,128,128]{4,3,2,1,0:T(8,128)(2,1)} %bitcast.226) | data formatting | bytes 50331648 | tf_op jit(solution)/shard_map/reshape;reshape | solution.py:54
  394.5 12.2 %fusion.16 = f32[256,3072]{0,1:T(8,128)S(1)} fusion(bf16[256,4096]{1,0:T(8,128)(2,1)} %all-gather.5.cloned.1.call-done, bf16[512,8,24,128]{3,2,1,0:T(8,128)(2,1)} %bitcast.231), kind=kOutput, calls=%fused_computation.41 | convolution fusion | flops 6442450944 | bytes 30408704 | tf_op jit(solution)/shard_map/dot_general | solution.py:235
  406.8 13.3 %convert_bitcast_fusion.1 = bf16[384,8,32,128]{3,1,2,0:T(8,128)(2,1)} fusion(bf16[256,4096]{1,0:T(8,128)(2,1)} %all-gather.7.cloned.1.call-done, f32[256,3072]{0,1:T(8,128)S(1)} %fusion.16), kind=kOutput, calls=%fused_computation.23 | convolution fusion | flops 6458966016 | bytes 30408704 | tf_op jit(solution)/shard_map/dot_general | solution.py:36
  420.1 22.4 %copy.89 = bf16[384,8,32,128]{3,2,1,0:T(8,128)(2,1)} copy(bf16[384,8,32,128]{3,1,2,0:T(8,128)(2,1)} %convert_bitcast_fusion.1) | data formatting | bytes 50331648
  442.5 32.8 %copy.78 = bf16[32,128,24,128]{3,1,2,0:T(8,128)(2,1)} copy(bf16[32,128,24,128]{1,0,3,2:T(8,128)(2,1)} %bitcast.228) | data formatting | bytes 50331648 | tf_op jit(solution)/shard_map/reshape | solution.py:203
  475.3 24.6 %gather_fusion.5 = bf16[384,128,128]{2,1,0:T(8,128)(2,1)} fusion(bf16[32,128,24,128]{3,1,2,0:T(8,128)(2,1)} %copy.78, s32[384]{0:T(512)S(1)} %reshape.750), kind=kCustom, calls=%fused_computation.5 | custom fusion | bytes 25168896 | tf_op jit(solution)/shard_map/gather | solution.py:207
  505.8 25.1 %gather_fusion.6 = bf16[768,128,128]{2,1,0:T(8,128)(2,1)} fusion(bf16[400,128,128]{2,1,0:T(8,128)(2,1)} %all-gather.9.cloned.1.call-done, s32[1024]{0:T(1024)S(1)} %get-tuple-element.79), kind=kCustom, calls=%fused_computation.6 | custom fusion | bytes 50334720 | tf_op jit(solution)/shard_map/gather | solution.py:194
  530.8 28.7 %copy.79 = bf16[8,4,128,24,128]{4,3,2,1,0:T(8,128)(2,1)} copy(bf16[8,4,128,24,128]{4,2,3,1,0:T(8,128)(2,1)} %bitcast.227) | data formatting | bytes 50331648 | tf_op jit(solution)/shard_map/transpose | solution.py:56
  559.5 13.2 %fusion.25 = bf16[256,3072]{0,1:T(8,128)(2,1)} fusion(bf16[256,4096]{1,0:T(8,128)(2,1)S(1)} %copy-done.1, bf16[512,8,24,128]{3,2,1,0:T(8,128)(2,1)} %bitcast.233, f32[256,3072]{0,1:T(8,128)S(1)} %fusion.16), kind=kOutput, calls=%fused_computation.44 | convolution fusion | flops 6450315264 | bytes 31981568 | tf_op jit(solution)/shard_map/dot_general | solution.py:243
  572.7 13.5 %convert_bitcast_fusion = bf16[384,8,32,128]{3,1,2,0:T(8,128)(2,1)} fusion(bf16[256,3072]{0,1:T(8,128)(2,1)} %fusion.25, bf16[256,4096]{1,0:T(8,128)(2,1)} %all-gather.5.cloned.1.call-done), kind=kOutput, calls=%fused_computation.22 | convolution fusion | flops 6455033856 | bytes 28835840 | tf_op jit(solution)/shard_map/dot_general | solution.py:36
  586.2 22.6 %copy.91 = bf16[384,8,32,128]{3,2,1,0:T(8,128)(2,1)} copy(bf16[384,8,32,128]{3,1,2,0:T(8,128)(2,1)} %convert_bitcast_fusion) | data formatting | bytes 50331648
  608.9 32.2 %copy.80 = bf16[32,128,24,128]{3,1,2,0:T(8,128)(2,1)} copy(bf16[32,128,24,128]{1,0,3,2:T(8,128)(2,1)} %bitcast.229) | data formatting | bytes 50331648 | tf_op jit(solution)/shard_map/reshape | solution.py:203
  641.0 18.1 %gather_fusion.12 = bf16[192,128,128]{2,1,0:T(8,128)(2,1)} fusion(bf16[32,128,24,128]{3,1,2,0:T(8,128)(2,1)} %copy.80, s32[192]{0:T(256)S(1)} %reshape.802), kind=kCustom, calls=%fused_computation.12 | custom fusion | bytes 12584448 | tf_op jit(solution)/shard_map/gather | solution.py:207
  659.1 17.7 %gather_fusion.9 = bf16[192,128,128]{2,1,0:T(8,128)(2,1)} fusion(bf16[32,128,24,128]{3,1,2,0:T(8,128)(2,1)} %copy.80, s32[192]{0:T(256)S(1)} %reshape.780), kind=kCustom, calls=%fused_computation.9 | custom fusion | bytes 12584448 | tf_op jit(solution)/shard_map/gather | solution.py:207
  676.8 30.6 %reduce-scatter.5.cloned.1.call-done = bf16[1,48,128,128]{3,2,1,0:T(8,128)(2,1)} async-done(((bf16[8,48,128,128]{3,2,1,0:T(8,128)(2,1)}), bf16[1,48,128,128]{3,2,1,0:T(8,128)(2,1)}) %reduce-scatter.5.cloned.1.call-update) | async-done | bytes 1572880 | tf_op jit(solution)/shard_map/reduce_scatter | solution.py:240
  712.0 16.1 %collective-permute-done.14 = bf16[24,128,128]{2,1,0:T(8,128)(2,1)S(1)} collective-permute-done((bf16[24,128,128]{2,1,0:T(8,128)(2,1)S(1)}, bf16[24,128,128]{2,1,0:T(8,128)(2,1)S(1)}, u32[]{:S(2)}, u32[]{:S(2)}) %collective-permute-start.14) | collective-permute-done | bytes 786464 | tf_op jit(solution)/shard_map/ppermute | solution.py:219
  733.0 15.0 %collective-permute-done.15 = bf16[24,128,128]{2,1,0:T(8,128)(2,1)S(1)} collective-permute-done((bf16[24,128,128]{2,1,0:T(8,128)(2,1)S(1)}, bf16[24,128,128]{2,1,0:T(8,128)(2,1)S(1)}, u32[]{:S(2)}, u32[]{:S(2)}) %collective-permute-start.15) | collective-permute-done | bytes 786464 | tf_op jit(solution)/shard_map/ppermute | solution.py:219
  752.9 14.1 %collective-permute-done.16 = bf16[24,128,128]{2,1,0:T(8,128)(2,1)S(1)} collective-permute-done((bf16[24,128,128]{2,1,0:T(8,128)(2,1)S(1)}, bf16[24,128,128]{2,1,0:T(8,128)(2,1)S(1)}, u32[]{:S(2)}, u32[]{:S(2)}) %collective-permute-start.16) | collective-permute-done | bytes 786464 | tf_op jit(solution)/shard_map/ppermute | solution.py:219
  771.9 13.1 %collective-permute-done.17 = bf16[24,128,128]{2,1,0:T(8,128)(2,1)S(1)} collective-permute-done((bf16[24,128,128]{2,1,0:T(8,128)(2,1)S(1)}, bf16[24,128,128]{2,1,0:T(8,128)(2,1)S(1)}, u32[]{:S(2)}, u32[]{:S(2)}) %collective-permute-start.17) | collective-permute-done | bytes 786464 | tf_op jit(solution)/shard_map/ppermute | solution.py:219
  791.6 13.7 %fusion.13 = bf16[256,4096]{1,0:T(8,128)(2,1)} fusion(bf16[256,3072]{0,1:T(8,128)(2,1)S(1)} %copy-done.2, bf16[512,8,24,128]{3,2,1,0:T(8,128)(2,1)} %bitcast.232), kind=kOutput, calls=%fused_computation.39 | convolution fusion | flops 6443499520 | bytes 28835840 | tf_op jit(solution)/shard_map/dot_general | solution.py:245
  (213 shorter events, 186.9 us)
Async XLA Ops:
  7.2 387.4 %all-gather.5.cloned.1.call-start = ((), (), s32[]{:S(2)}) async-start(), calls=%async_computation.2 | async-start | bytes 2621440 | tf_op jit(solution)/shard_map/all_gather | solution.py:188
  7.9 398.9 %all-gather.7.cloned.1.call-start = ((), (), s32[]{:S(2)}) async-start(), calls=%async_computation.3 | async-start | bytes 2621440 | tf_op jit(solution)/shard_map/all_gather | solution.py:189
  8.6 491.3 %all-gather.9.cloned.1.call-start = ((), (), s32[]{:S(2)}) async-start(), calls=%async_computation.6 | async-start | bytes 14745600 | tf_op jit(solution)/shard_map/all_gather | solution.py:180
  21.9 685.6 %reduce-scatter.5.cloned.1.call-start = ((), (), s32[]{:S(2)}) async-start(), calls=%async_computation.5 | async-start | bytes 14155776 | tf_op jit(solution)/shard_map/reduce_scatter | solution.py:240
  34.4 21.3 %collective-permute-start.7 = (bf16[25,128,128]{2,1,0:T(8,128)(2,1)S(1)}, bf16[25,128,128]{2,1,0:T(8,128)(2,1)S(1)}, u32[]{:S(2)}, u32[]{:S(2)}) collective-permute-start(bf16[25,128,128]{2,1,0:T(8,128)(2,1)S(1)} %get-tuple-element.72), channel_id=1, source_target_pairs={{0,8},{4,0},{12,4},{20,12},{28,20},{24,28},{16,24},{8,16},{1,9},{5... | collective-permute-start | bytes 2457608 | tf_op jit(solution)/shard_map/ppermute | solution.py:158
  37.5 20.0 %collective-permute-start = (bf16[25,128,128]{2,1,0:T(8,128)(2,1)S(1)}, bf16[25,128,128]{2,1,0:T(8,128)(2,1)S(1)}, u32[]{:S(2)}, u32[]{:S(2)}) collective-permute-start(bf16[25,128,128]{2,1,0:T(8,128)(2,1)S(1)} %slice.193), channel_id=1, source_target_pairs={{0,4},{4,12},{12,20},{20,28},{28,24},{24,16},{16,8},{8,0},{1,5},{5... | collective-permute-start | bytes 2457608 | tf_op jit(solution)/shard_map/ppermute | solution.py:157
  55.7 23.6 %collective-permute-start.8 = (bf16[25,128,128]{2,1,0:T(8,128)(2,1)S(1)}, bf16[25,128,128]{2,1,0:T(8,128)(2,1)}, u32[]{:S(2)}, u32[]{:S(2)}) collective-permute-start(bf16[25,128,128]{2,1,0:T(8,128)(2,1)S(1)} %collective-permute-done.7), channel_id=1, source_target_pairs={{0,8},{4,0},{12,4},{20,12},{28,20},{24,28},{16,24},{8,16},{1,9},{5... | collective-permute-start | bytes 2457608 | tf_op jit(solution)/shard_map/ppermute | solution.py:158
  57.5 28.3 %collective-permute-start.1 = (bf16[25,128,128]{2,1,0:T(8,128)(2,1)S(1)}, bf16[25,128,128]{2,1,0:T(8,128)(2,1)}, u32[]{:S(2)}, u32[]{:S(2)}) collective-permute-start(bf16[25,128,128]{2,1,0:T(8,128)(2,1)S(1)} %collective-permute-done), channel_id=1, source_target_pairs={{0,4},{4,12},{12,20},{20,28},{28,24},{24,16},{16,8},{8,0},{1,5},{5... | collective-permute-start | bytes 2457608 | tf_op jit(solution)/shard_map/ppermute | solution.py:157
  79.3 39.0 %collective-permute-start.9 = (bf16[25,128,128]{2,1,0:T(8,128)(2,1)}, bf16[25,128,128]{2,1,0:T(8,128)(2,1)}, u32[]{:S(2)}, u32[]{:S(2)}) collective-permute-start(bf16[25,128,128]{2,1,0:T(8,128)(2,1)} %collective-permute-done.8), channel_id=1, source_target_pairs={{0,8},{4,0},{12,4},{20,12},{28,20},{24,28},{16,24},{8,16},{1,9},{5... | collective-permute-start | bytes 2457608 | tf_op jit(solution)/shard_map/ppermute | solution.py:158
  85.8 56.5 %collective-permute-start.2 = (bf16[25,128,128]{2,1,0:T(8,128)(2,1)}, bf16[25,128,128]{2,1,0:T(8,128)(2,1)S(1)}, u32[]{:S(2)}, u32[]{:S(2)}) collective-permute-start(bf16[25,128,128]{2,1,0:T(8,128)(2,1)} %collective-permute-done.1), channel_id=1, source_target_pairs={{0,4},{4,12},{12,20},{20,28},{28,24},{24,16},{16,8},{8,0},{1,5},{5... | collective-permute-start | bytes 2457608 | tf_op jit(solution)/shard_map/ppermute | solution.py:157
  118.2 44.4 %collective-permute-start.10 = (bf16[25,128,128]{2,1,0:T(8,128)(2,1)}, bf16[25,128,128]{2,1,0:T(8,128)(2,1)}, u32[]{:S(2)}, u32[]{:S(2)}) collective-permute-start(bf16[25,128,128]{2,1,0:T(8,128)(2,1)} %collective-permute-done.9), channel_id=1, source_target_pairs={{0,8},{4,0},{12,4},{20,12},{28,20},{24,28},{16,24},{8,16},{1,9},{5... | collective-permute-start | bytes 2457608 | tf_op jit(solution)/shard_map/ppermute | solution.py:158
  142.3 23.8 %collective-permute-start.3 = (bf16[25,128,128]{2,1,0:T(8,128)(2,1)S(1)}, bf16[25,128,128]{2,1,0:T(8,128)(2,1)}, u32[]{:S(2)}, u32[]{:S(2)}) collective-permute-start(bf16[25,128,128]{2,1,0:T(8,128)(2,1)S(1)} %collective-permute-done.2), channel_id=1, source_target_pairs={{0,4},{4,12},{12,20},{20,28},{28,24},{24,16},{16,8},{8,0},{1,5},{5... | collective-permute-start | bytes 2457608 | tf_op jit(solution)/shard_map/ppermute | solution.py:157
  162.6 34.5 %collective-permute-start.11 = (bf16[25,128,128]{2,1,0:T(8,128)(2,1)}, bf16[25,128,128]{2,1,0:T(8,128)(2,1)S(1)}, u32[]{:S(2)}, u32[]{:S(2)}) collective-permute-start(bf16[25,128,128]{2,1,0:T(8,128)(2,1)} %collective-permute-done.10), channel_id=1, source_target_pairs={{0,8},{4,0},{12,4},{20,12},{28,20},{24,28},{16,24},{8,16},{1,9},{5... | collective-permute-start | bytes 2457608 | tf_op jit(solution)/shard_map/ppermute | solution.py:158
  166.1 53.7 %collective-permute-start.4 = (bf16[25,128,128]{2,1,0:T(8,128)(2,1)}, bf16[25,128,128]{2,1,0:T(8,128)(2,1)S(1)}, u32[]{:S(2)}, u32[]{:S(2)}) collective-permute-start(bf16[25,128,128]{2,1,0:T(8,128)(2,1)} %collective-permute-done.3), channel_id=1, source_target_pairs={{0,4},{4,12},{12,20},{20,28},{28,24},{24,16},{16,8},{8,0},{1,5},{5... | collective-permute-start | bytes 2457608 | tf_op jit(solution)/shard_map/ppermute | solution.py:157
  197.1 51.5 %collective-permute-start.12 = (bf16[25,128,128]{2,1,0:T(8,128)(2,1)S(1)}, bf16[25,128,128]{2,1,0:T(8,128)(2,1)S(1)}, u32[]{:S(2)}, u32[]{:S(2)}) collective-permute-start(bf16[25,128,128]{2,1,0:T(8,128)(2,1)S(1)} %collective-permute-done.11), channel_id=1, source_target_pairs={{0,8},{4,0},{12,4},{20,12},{28,20},{24,28},{16,24},{8,16},{1,9},{5... | collective-permute-start | bytes 2457608 | tf_op jit(solution)/shard_map/ppermute | solution.py:158
  219.7 57.1 %collective-permute-start.5 = (bf16[25,128,128]{2,1,0:T(8,128)(2,1)S(1)}, bf16[25,128,128]{2,1,0:T(8,128)(2,1)S(1)}, u32[]{:S(2)}, u32[]{:S(2)}) collective-permute-start(bf16[25,128,128]{2,1,0:T(8,128)(2,1)S(1)} %collective-permute-done.4), channel_id=1, source_target_pairs={{0,4},{4,12},{12,20},{20,28},{28,24},{24,16},{16,8},{8,0},{1,5},{5... | collective-permute-start | bytes 2457608 | tf_op jit(solution)/shard_map/ppermute | solution.py:157
  248.6 52.3 %collective-permute-start.13 = (bf16[25,128,128]{2,1,0:T(8,128)(2,1)S(1)}, bf16[25,128,128]{2,1,0:T(8,128)(2,1)S(1)}, u32[]{:S(2)}, u32[]{:S(2)}) collective-permute-start(bf16[25,128,128]{2,1,0:T(8,128)(2,1)S(1)} %collective-permute-done.12), channel_id=1, source_target_pairs={{0,8},{4,0},{12,4},{20,12},{28,20},{24,28},{16,24},{8,16},{1,9},{5... | collective-permute-start | bytes 2457608 | tf_op jit(solution)/shard_map/ppermute | solution.py:158
  276.8 46.9 %collective-permute-start.6 = (bf16[25,128,128]{2,1,0:T(8,128)(2,1)S(1)}, bf16[25,128,128]{2,1,0:T(8,128)(2,1)S(1)}, u32[]{:S(2)}, u32[]{:S(2)}) collective-permute-start(bf16[25,128,128]{2,1,0:T(8,128)(2,1)S(1)} %collective-permute-done.5), channel_id=1, source_target_pairs={{0,4},{4,12},{12,20},{20,28},{28,24},{24,16},{16,8},{8,0},{1,5},{5... | collective-permute-start | bytes 2457608 | tf_op jit(solution)/shard_map/ppermute | solution.py:157
  500.0 372.1 %reduce-scatter.3.cloned.1.call-start = ((), (), s32[]{:S(2)}) async-start(), calls=%async_computation.4 | async-start | bytes 2621440 | tf_op jit(solution)/shard_map/reduce_scatter | solution.py:252
  708.6 19.4 %collective-permute-start.14 = (bf16[24,128,128]{2,1,0:T(8,128)(2,1)S(1)}, bf16[24,128,128]{2,1,0:T(8,128)(2,1)S(1)}, u32[]{:S(2)}, u32[]{:S(2)}) collective-permute-start(bf16[24,128,128]{2,1,0:T(8,128)(2,1)S(1)} %slice_bitcast_fusion.1), channel_id=1, source_target_pairs={{0,4},{4,12},{12,20},{20,28},{28,24},{24,16},{16,8},{8,0},{1,5},{5... | collective-permute-start | bytes 2359304 | tf_op jit(solution)/shard_map/ppermute | solution.py:219
  711.3 19.6 %collective-permute-start.21 = (bf16[24,128,128]{2,1,0:T(8,128)(2,1)S(1)}, bf16[24,128,128]{2,1,0:T(8,128)(2,1)S(1)}, u32[]{:S(2)}, u32[]{:S(2)}) collective-permute-start(bf16[24,128,128]{2,1,0:T(8,128)(2,1)S(1)} %slice_bitcast_fusion), channel_id=1, source_target_pairs={{0,8},{4,0},{12,4},{20,12},{28,20},{24,28},{16,24},{8,16},{1,9},{5... | collective-permute-start | bytes 2359304 | tf_op jit(solution)/shard_map/ppermute | solution.py:220
  729.5 18.5 %collective-permute-start.15 = (bf16[24,128,128]{2,1,0:T(8,128)(2,1)S(1)}, bf16[24,128,128]{2,1,0:T(8,128)(2,1)S(1)}, u32[]{:S(2)}, u32[]{:S(2)}) collective-permute-start(bf16[24,128,128]{2,1,0:T(8,128)(2,1)S(1)} %fusion.43), channel_id=1, source_target_pairs={{0,4},{4,12},{12,20},{20,28},{28,24},{24,16},{16,8},{8,0},{1,5},{5... | collective-permute-start | bytes 2359304 | tf_op jit(solution)/shard_map/ppermute | solution.py:219
  732.4 18.5 %collective-permute-start.22 = (bf16[24,128,128]{2,1,0:T(8,128)(2,1)S(1)}, bf16[24,128,128]{2,1,0:T(8,128)(2,1)S(1)}, u32[]{:S(2)}, u32[]{:S(2)}) collective-permute-start(bf16[24,128,128]{2,1,0:T(8,128)(2,1)S(1)} %fusion.37), channel_id=1, source_target_pairs={{0,8},{4,0},{12,4},{20,12},{28,20},{24,28},{16,24},{8,16},{1,9},{5... | collective-permute-start | bytes 2359304 | tf_op jit(solution)/shard_map/ppermute | solution.py:220
  749.4 17.6 %collective-permute-start.16 = (bf16[24,128,128]{2,1,0:T(8,128)(2,1)S(1)}, bf16[24,128,128]{2,1,0:T(8,128)(2,1)S(1)}, u32[]{:S(2)}, u32[]{:S(2)}) collective-permute-start(bf16[24,128,128]{2,1,0:T(8,128)(2,1)S(1)} %fusion.42), channel_id=1, source_target_pairs={{0,4},{4,12},{12,20},{20,28},{28,24},{24,16},{16,8},{8,0},{1,5},{5... | collective-permute-start | bytes 2359304 | tf_op jit(solution)/shard_map/ppermute | solution.py:219
  752.3 17.6 %collective-permute-start.23 = (bf16[24,128,128]{2,1,0:T(8,128)(2,1)S(1)}, bf16[24,128,128]{2,1,0:T(8,128)(2,1)S(1)}, u32[]{:S(2)}, u32[]{:S(2)}) collective-permute-start(bf16[24,128,128]{2,1,0:T(8,128)(2,1)S(1)} %fusion.36), channel_id=1, source_target_pairs={{0,8},{4,0},{12,4},{20,12},{28,20},{24,28},{16,24},{8,16},{1,9},{5... | collective-permute-start | bytes 2359304 | tf_op jit(solution)/shard_map/ppermute | solution.py:220
  768.4 16.7 %collective-permute-start.17 = (bf16[24,128,128]{2,1,0:T(8,128)(2,1)S(1)}, bf16[24,128,128]{2,1,0:T(8,128)(2,1)S(1)}, u32[]{:S(2)}, u32[]{:S(2)}) collective-permute-start(bf16[24,128,128]{2,1,0:T(8,128)(2,1)S(1)} %fusion.41), channel_id=1, source_target_pairs={{0,4},{4,12},{12,20},{20,28},{28,24},{24,16},{16,8},{8,0},{1,5},{5... | collective-permute-start | bytes 2359304 | tf_op jit(solution)/shard_map/ppermute | solution.py:219
  771.2 17.5 %collective-permute-start.24 = (bf16[24,128,128]{2,1,0:T(8,128)(2,1)S(1)}, bf16[24,128,128]{2,1,0:T(8,128)(2,1)S(1)}, u32[]{:S(2)}, u32[]{:S(2)}) collective-permute-start(bf16[24,128,128]{2,1,0:T(8,128)(2,1)S(1)} %fusion.35), channel_id=1, source_target_pairs={{0,8},{4,0},{12,4},{20,12},{28,20},{24,28},{16,24},{8,16},{1,9},{5... | collective-permute-start | bytes 2359304 | tf_op jit(solution)/shard_map/ppermute | solution.py:220
  787.3 23.4 %collective-permute-start.18 = (bf16[24,128,128]{2,1,0:T(8,128)(2,1)}, bf16[24,128,128]{2,1,0:T(8,128)(2,1)}, u32[]{:S(2)}, u32[]{:S(2)}) collective-permute-start(bf16[24,128,128]{2,1,0:T(8,128)(2,1)} %fusion.40), channel_id=1, source_target_pairs={{0,4},{4,12},{12,20},{20,28},{28,24},{24,16},{16,8},{8,0},{1,5},{5... | collective-permute-start | bytes 2359304 | tf_op jit(solution)/shard_map/ppermute | solution.py:219
  791.0 22.9 %collective-permute-start.25 = (bf16[24,128,128]{2,1,0:T(8,128)(2,1)}, bf16[24,128,128]{2,1,0:T(8,128)(2,1)}, u32[]{:S(2)}, u32[]{:S(2)}) collective-permute-start(bf16[24,128,128]{2,1,0:T(8,128)(2,1)} %fusion.34), channel_id=1, source_target_pairs={{0,8},{4,0},{12,4},{20,12},{28,20},{24,28},{16,24},{8,16},{1,9},{5... | collective-permute-start | bytes 2359304 | tf_op jit(solution)/shard_map/ppermute | solution.py:220
  812.4 15.2 %collective-permute-start.19 = (bf16[24,128,128]{2,1,0:T(8,128)(2,1)S(1)}, bf16[24,128,128]{2,1,0:T(8,128)(2,1)S(1)}, u32[]{:S(2)}, u32[]{:S(2)}) collective-permute-start(bf16[24,128,128]{2,1,0:T(8,128)(2,1)S(1)} %fusion.39), channel_id=1, source_target_pairs={{0,4},{4,12},{12,20},{20,28},{28,24},{24,16},{16,8},{8,0},{1,5},{5... | collective-permute-start | bytes 2359304 | tf_op jit(solution)/shard_map/ppermute | solution.py:219
  815.7 15.7 %collective-permute-start.26 = (bf16[24,128,128]{2,1,0:T(8,128)(2,1)S(1)}, bf16[24,128,128]{2,1,0:T(8,128)(2,1)S(1)}, u32[]{:S(2)}, u32[]{:S(2)}) collective-permute-start(bf16[24,128,128]{2,1,0:T(8,128)(2,1)S(1)} %fusion.33), channel_id=1, source_target_pairs={{0,8},{4,0},{12,4},{20,12},{28,20},{24,28},{16,24},{8,16},{1,9},{5... | collective-permute-start | bytes 2359304 | tf_op jit(solution)/shard_map/ppermute | solution.py:220
  829.8 16.0 %collective-permute-start.20 = (bf16[24,128,128]{2,1,0:T(8,128)(2,1)}, bf16[24,128,128]{2,1,0:T(8,128)(2,1)}, u32[]{:S(2)}, u32[]{:S(2)}) collective-permute-start(bf16[24,128,128]{2,1,0:T(8,128)(2,1)} %fusion.38), channel_id=1, source_target_pairs={{0,4},{4,12},{12,20},{20,28},{28,24},{24,16},{16,8},{8,0},{1,5},{5... | collective-permute-start | bytes 2359304 | tf_op jit(solution)/shard_map/ppermute | solution.py:219
  (14 other events, 432.1 us)
Sparse Core Ops, SparseCore 0:
  9.6 25.2 all-gather.4
  36.4 22.5 all-gather.6
  61.8 261.9 all-gather.8
  500.1 207.2 reduce-scatter.4
  805.4 31.3 reduce-scatter.2

commit v8 on v7

--- a/solution.py
+++ b/solution.py
@@ -192,9 +192,7 @@
     def rebuild(got, masks, at):
         k = jnp.where(masks > 0, slot_of(masks), zero_slot)
         dense = got.at[at(k).reshape(-1)].get(mode="promise_in_bounds")
-        dense = dense.reshape((n_row, nb, block, block))
-        dense = from_blocks(dense, nr, nc)
-        return dense.reshape((n_row * nr * block, nc * block))
+        return dense.reshape((n_row * nr, nc, block, block))
 
     def in_order(k):
         return (rows_n * width)[:, None] + k
@@ -232,20 +230,39 @@
         return from_blocks(dense, nr, nc)
 
     up_whole = rebuild(got_up, masks_up, where_is)
-    preact = jnp.dot(features, up_whole, preferred_element_type=jnp.float32)
+    features3 = features.reshape((features.shape[0], n_row * nr, block))
+    cot3 = cot_rows.reshape((cot_rows.shape[0], n_row * nr, block))
+
+    def forward(rows3, w4):
+        out = lax.dot_general(
+            rows3, w4, (((1, 2), (0, 2)), ((), ())), preferred_element_type=jnp.float32
+        )
+        return out.reshape((out.shape[0], nc * block))
+
+    def grad_view(rows3, acts):
+        acts3 = acts.reshape((acts.shape[0], nc, block))
+        out = lax.dot_general(
+            rows3, acts3, (((0,), (0,)), ((), ())), preferred_element_type=jnp.float32
+        )
+        return out.reshape((n_row * nr * block, nc * block))
+
+    preact = forward(features3, up_whole)
     gelu_value, gelu_slope = gelu_parts(preact)
     activation = gelu_value.astype(jnp.bfloat16)
-    sent_down = kept_blocks(token_product(cot_rows, activation), masks_down, rows_n, 0, slots)
+    sent_down = kept_blocks(grad_view(cot3, activation), masks_down, rows_n, 0, slots)
     got_down, sent_down = lax.optimization_barrier((got_down, sent_down))
     summed_down = lax.psum_scatter(sent_down, "row", scatter_dimension=0, tiled=True)[0]
 
     down_whole = rebuild(got_down.reshape((n_row * width, block, block)), masks_down, in_order)
-    act_grad = jnp.dot(cot_rows, down_whole, preferred_element_type=jnp.float32)
+    act_grad = forward(cot3, down_whole)
     pre_grad = (act_grad * gelu_slope).astype(jnp.bfloat16)
     partial_tokens = lax.dot_general(
-        pre_grad, up_whole, (((1,), (1,)), ((), ())), preferred_element_type=jnp.float32
-    )
-    summed_up, summed_down = ring_reduce(token_product(features, pre_grad), masks_up, summed_down)
+        pre_grad.reshape((pre_grad.shape[0], nc, block)),
+        up_whole,
+        (((1, 2), (1, 3)), ((), ())),
+        preferred_element_type=jnp.float32,
+    ).reshape((pre_grad.shape[0], n_row * nr * block))
+    summed_up, summed_down = ring_reduce(grad_view(features3, pre_grad), masks_up, summed_down)
     grad_down = unpack(summed_down.astype(jnp.float32), flat_down)
     grad_up = unpack(summed_up, flat_up)
 

time: 890 us -> 834 us (0.937)
  local copies, waits for them, and re-layouts: 335 us -> 207 us
  waiting for transfers between devices: 287 us -> 353 us
    reduce_scatter x1, waiting for transfers between devices: 30.6 us -> 112 us  [shards(): lax.psum_scatter(sent_down, 'row', scatter_dimension=0, tiled=True)[0]]
    reshape x2 -> x0, local copies, waits for them, and re-layouts: 65 us -> none  [kept_blocks(): view = partial.astype(jnp.bfloat16).reshape((n_row * nr, block, nc, block))]
    ppermute x7, waiting for transfers between devices: 62.4 us -> 1.2 us  [ring_reduce(): in_a = lax.ppermute(acc_a, 'row', right).astype(jnp.float32)]
    ppermute x7, waiting for transfers between devices: 0.58 us -> 53.6 us  [ring_reduce(): in_b = lax.ppermute(acc_b, 'row', left).astype(jnp.float32)]
    unnamed x42 -> x36, local copies, waits for them, and re-layouts: 64.6 us -> 23.5 us
    transpose x3 -> x0, local copies, waits for them, and re-layouts: 35.9 us -> none  [from_blocks(): x = jnp.moveaxis(x, k + 1, k + 2)]
    dot_general x0 -> x1, local copies, waits for them, and re-layouts: none -> 28.4 us  [shards(): lax.dot_general(pre_grad.reshape((pre_grad.shape[0], nc, block)), up_whol...]
    another operation x3 -> x2, local copies, waits for them, and re-layouts: 29.2 us -> 0.86 us  [the longest x1 28.3 us: from_blocks(): x = blocks.reshape(lead + (nr, nc, block, block))]
  transfers between devices with their start and end apart: 33 -> 33, of which waited for: 19 -> 17; matrix products, arithmetic and copies ran while one was open for 55% -> 43% of each run, Pallas kernels for 0% -> 0%
where the time goes in v8:
time: 834 us; the launch traced here: 826 us
  waiting for transfers between devices  353 us (42%)
  local copies, waits for them, and re-layouts  207 us (25%)
  starting transfers between devices  97 us (12%)
  other arithmetic  87.8 us (11%)
  matrix products  66.9 us (8%)
  between operations  14.6 us (2%)
    ppermute x7, waiting for transfers between devices, ring_gather(): b = lax.ppermute(b, 'row', left)  158 us
    reduce_scatter x1, waiting for transfers between devices, shards(): lax.psum_scatter(sent_down, 'row', scatter_dimension=0, tiled=True)[0]  112 us
    ppermute x7, starting transfers between devices, ring_gather(): b = lax.ppermute(b, 'row', left)  81.5 us
    gather x3, local copies, waits for them, and re-layouts, kept_blocks(): return view.at[rows, :, cols, :].get(mode='promise_in_bounds')  60.8 us
    ppermute x7, waiting for transfers between devices, ring_reduce(): in_b = lax.ppermute(acc_b, 'row', left).astype(jnp.float32)  53.6 us
    gather x2, local copies, waits for them, and re-layouts, rebuild(): dense = got.at[at(k).reshape(-1)].get(mode='promise_in_bounds')  49.2 us
    dot_general x1, local copies, waits for them, and re-layouts, shards(): lax.dot_general(pre_grad.reshape((pre_grad.shape[0], nc, block)), up_whol...  28.4 us
    ppermute x7, waiting for transfers between devices, ring_gather(): a = lax.ppermute(a, 'row', right)  27.1 us
  transfers between devices with their start and end apart: 33, of which 17 were waited for; matrix products, arithmetic and copies ran while one was open for 43% of the time, Pallas kernels for 0%

profile of v8, /device:TPU:0, one launch (start us, length us, event | category | flops | bytes accessed | tf_op | source)
XLA Modules:
  0.0 825.9 jit_solution(9413240336515538241)
XLA Ops:
  39.8 18.0 %collective-permute-done.7 = bf16[25,128,128]{2,1,0:T(8,128)(2,1)S(1)} collective-permute-done((bf16[25,128,128]{2,1,0:T(8,128)(2,1)S(1)}, bf16[25,128,128]{2,1,0:T(8,128)(2,1)S(1)}, u32[]{:S(2)}, u32[]{:S(2)}) %collective-permute-start.7) | collective-permute-done | bytes 819232 | tf_op jit(solution)/shard_map/ppermute | solution.py:158
  59.9 22.6 %collective-permute-done.8 = bf16[25,128,128]{2,1,0:T(8,128)(2,1)} collective-permute-done((bf16[25,128,128]{2,1,0:T(8,128)(2,1)S(1)}, bf16[25,128,128]{2,1,0:T(8,128)(2,1)}, u32[]{:S(2)}, u32[]{:S(2)}) %collective-permute-start.8) | collective-permute-done | bytes 819232 | tf_op jit(solution)/shard_map/ppermute | solution.py:158
  91.2 30.1 %collective-permute-done.9 = bf16[25,128,128]{2,1,0:T(8,128)(2,1)} collective-permute-done((bf16[25,128,128]{2,1,0:T(8,128)(2,1)}, bf16[25,128,128]{2,1,0:T(8,128)(2,1)}, u32[]{:S(2)}, u32[]{:S(2)}) %collective-permute-start.9) | collective-permute-done | bytes 819232 | tf_op jit(solution)/shard_map/ppermute | solution.py:158
  121.3 22.6 %collective-permute-start.10 = (bf16[25,128,128]{2,1,0:T(8,128)(2,1)}, bf16[25,128,128]{2,1,0:T(8,128)(2,1)}, u32[]{:S(2)}, u32[]{:S(2)}) collective-permute-start(bf16[25,128,128]{2,1,0:T(8,128)(2,1)} %collective-permute-done.9), channel_id=1, source_target_pairs={{0,8},{4,0},{12,4},{20,12},{28,20},{24,28},{16,24},{8,16},{1,9},{5... | collective-permute-start | bytes 2457608 | tf_op jit(solution)/shard_map/ppermute | solution.py:158
  147.8 17.2 %collective-permute-done.10 = bf16[25,128,128]{2,1,0:T(8,128)(2,1)} collective-permute-done((bf16[25,128,128]{2,1,0:T(8,128)(2,1)}, bf16[25,128,128]{2,1,0:T(8,128)(2,1)}, u32[]{:S(2)}, u32[]{:S(2)}) %collective-permute-start.10) | collective-permute-done | bytes 819232 | tf_op jit(solution)/shard_map/ppermute | solution.py:158
  173.9 25.7 %collective-permute-done.11 = bf16[25,128,128]{2,1,0:T(8,128)(2,1)S(1)} collective-permute-done((bf16[25,128,128]{2,1,0:T(8,128)(2,1)}, bf16[25,128,128]{2,1,0:T(8,128)(2,1)S(1)}, u32[]{:S(2)}, u32[]{:S(2)}) %collective-permute-start.11) | collective-permute-done | bytes 819232 | tf_op jit(solution)/shard_map/ppermute | solution.py:158
  199.6 21.4 %collective-permute-start.12 = (bf16[25,128,128]{2,1,0:T(8,128)(2,1)S(1)}, bf16[25,128,128]{2,1,0:T(8,128)(2,1)S(1)}, u32[]{:S(2)}, u32[]{:S(2)}) collective-permute-start(bf16[25,128,128]{2,1,0:T(8,128)(2,1)S(1)} %collective-permute-done.11), channel_id=1, source_target_pairs={{0,8},{4,0},{12,4},{20,12},{28,20},{24,28},{16,24},{8,16},{1,9},{5... | collective-permute-start | bytes 2457608 | tf_op jit(solution)/shard_map/ppermute | solution.py:158
  228.7 23.8 %collective-permute-done.12 = bf16[25,128,128]{2,1,0:T(8,128)(2,1)S(1)} collective-permute-done((bf16[25,128,128]{2,1,0:T(8,128)(2,1)S(1)}, bf16[25,128,128]{2,1,0:T(8,128)(2,1)S(1)}, u32[]{:S(2)}, u32[]{:S(2)}) %collective-permute-start.12) | collective-permute-done | bytes 819232 | tf_op jit(solution)/shard_map/ppermute | solution.py:158
  252.5 24.5 %collective-permute-start.13 = (bf16[25,128,128]{2,1,0:T(8,128)(2,1)S(1)}, bf16[25,128,128]{2,1,0:T(8,128)(2,1)S(1)}, u32[]{:S(2)}, u32[]{:S(2)}) collective-permute-start(bf16[25,128,128]{2,1,0:T(8,128)(2,1)S(1)} %collective-permute-done.12), channel_id=1, source_target_pairs={{0,8},{4,0},{12,4},{20,12},{28,20},{24,28},{16,24},{8,16},{1,9},{5... | collective-permute-start | bytes 2457608 | tf_op jit(solution)/shard_map/ppermute | solution.py:158
  283.8 21.0 %collective-permute-done.13 = bf16[25,128,128]{2,1,0:T(8,128)(2,1)S(1)} collective-permute-done((bf16[25,128,128]{2,1,0:T(8,128)(2,1)S(1)}, bf16[25,128,128]{2,1,0:T(8,128)(2,1)S(1)}, u32[]{:S(2)}, u32[]{:S(2)}) %collective-permute-start.13) | collective-permute-done | bytes 819232 | tf_op jit(solution)/shard_map/ppermute | solution.py:158
  305.8 19.6 %collective-permute-done.6 = bf16[25,128,128]{2,1,0:T(8,128)(2,1)S(1)} collective-permute-done((bf16[25,128,128]{2,1,0:T(8,128)(2,1)S(1)}, bf16[25,128,128]{2,1,0:T(8,128)(2,1)S(1)}, u32[]{:S(2)}, u32[]{:S(2)}) %collective-permute-start.6) | collective-permute-done | bytes 819232 | tf_op jit(solution)/shard_map/ppermute | solution.py:157
  326.4 10.1 %pad_maximum_fusion = bf16[400,128,128]{2,1,0:T(8,128)(2,1)} fusion(bf16[200,128,128]{2,1,0:T(8,128)(2,1)} %bitcast.271, bf16[200,128,128]{2,1,0:T(8,128)(2,1)} %bitcast.270), kind=kLoop, calls=%fused_computation.19 | loop fusion | flops 6553600 | bytes 26214400 | tf_op jit(solution)/shard_map/concatenate | solution.py:161
  342.4 23.9 %gather_fusion.3 = bf16[768,128,128]{2,1,0:T(8,128)(2,1)} fusion(bf16[400,128,128]{2,1,0:T(8,128)(2,1)} %pad_maximum_fusion, s32[1024]{0:T(1024)S(1)} %get-tuple-element.81), kind=kCustom, calls=%fused_computation.3 | custom fusion | bytes 50334720 | tf_op jit(solution)/shard_map/gather | solution.py:194
  367.5 12.4 %fusion.85 = f32[24,128,256,1]{2,1,0,3:T(8,128)S(1)} fusion(bf16[32,24,128,128]{3,2,1,0:T(8,128)(2,1)} %bitcast.237, bf16[256,32,128,1]{0,2,3,1:T(8,128)(2,1)} %bitcast.268), kind=kOutput, calls=%fused_computation.220 | convolution fusion | flops 6442450944 | bytes 30408704 | tf_op jit(solution)/shard_map/dot_general | solution.py:237
  380.0 12.8 %convert_bitcast_fusion.1 = bf16[32,128,24,128]{1,3,0,2:T(8,128)(2,1)} fusion(bf16[256,32,128,1]{0,2,1,3:T(8,128)(2,1)} %bitcast.274, f32[24,128,256,1]{2,1,0,3:T(8,128)S(1)} %fusion.85), kind=kOutput, calls=%fused_computation.18 | convolution fusion | flops 6458966016 | bytes 30408704 | tf_op jit(solution)/shard_map/dot_general | solution.py:244
  392.8 24.6 %gather_fusion.5 = bf16[384,128,128]{1,2,0:T(8,128)(2,1)} fusion(bf16[32,128,24,128]{1,3,0,2:T(8,128)(2,1)} %convert_bitcast_fusion.1, s32[384]{0:T(512)S(1)} %reshape.769), kind=kCustom, calls=%fused_computation.5 | custom fusion | bytes 25168896 | tf_op jit(solution)/shard_map/gather | solution.py:205
  423.2 25.3 %gather_fusion.6 = bf16[768,128,128]{2,1,0:T(8,128)(2,1)} fusion(bf16[400,128,128]{2,1,0:T(8,128)(2,1)} %all-gather.9.cloned.1.call-done, s32[1024]{0:T(1024)S(1)} %get-tuple-element.79), kind=kCustom, calls=%fused_computation.6 | custom fusion | bytes 50334720 | tf_op jit(solution)/shard_map/gather | solution.py:194
  448.4 14.2 %fusion.17 = bf16[256,24,128]{0,2,1:T(8,128)(2,1)} fusion(f32[24,128,256,1]{2,1,0,3:T(8,128)S(1)} %fusion.85, bf16[32,24,128,128]{3,2,1,0:T(8,128)(2,1)} %bitcast.241, bf16[256,32,128,1]{0,2,3,1:T(8,128)(2,1)} %bitcast.275), kind=kOutput, calls=%fused_computation.38 | convolution fusion | flops 6450315264 | bytes 31981568 | tf_op jit(solution)/shard_map/dot_general | solution.py:237
  462.6 13.9 %convert_bitcast_fusion = bf16[32,128,24,128]{1,3,0,2:T(8,128)(2,1)} fusion(bf16[256,32,128,1]{0,2,1,3:T(8,128)(2,1)} %bitcast.269, bf16[256,24,128]{0,2,1:T(8,128)(2,1)} %fusion.17), kind=kOutput, calls=%fused_computation.17 | convolution fusion | flops 6455033856 | bytes 28835840 | tf_op jit(solution)/shard_map/dot_general | solution.py:244
  476.5 18.4 %gather_fusion.9 = bf16[192,128,128]{1,2,0:T(8,128)(2,1)} fusion(bf16[32,128,24,128]{1,3,0,2:T(8,128)(2,1)} %convert_bitcast_fusion, s32[192]{0:T(256)S(1)} %reshape.799), kind=kCustom, calls=%fused_computation.9 | custom fusion | bytes 12584448 | tf_op jit(solution)/shard_map/gather | solution.py:205
  494.9 17.8 %gather_fusion.12 = bf16[192,128,128]{1,2,0:T(8,128)(2,1)} fusion(bf16[32,128,24,128]{1,3,0,2:T(8,128)(2,1)} %convert_bitcast_fusion, s32[192]{0:T(256)S(1)} %reshape.821), kind=kCustom, calls=%fused_computation.12 | custom fusion | bytes 12584448 | tf_op jit(solution)/shard_map/gather | solution.py:205
  512.7 112.0 %reduce-scatter.5.cloned.1.call-done = bf16[1,48,128,128]{2,3,1,0:T(8,128)(2,1)} async-done(((bf16[8,48,128,128]{2,3,1,0:T(8,128)(2,1)}), bf16[1,48,128,128]{2,3,1,0:T(8,128)(2,1)}) %reduce-scatter.5.cloned.1.call-update) | async-done | bytes 1572880 | tf_op jit(solution)/shard_map/reduce_scatter | solution.py:254
  629.2 16.1 %collective-permute-done.21 = bf16[24,128,128]{1,2,0:T(8,128)(2,1)S(1)} collective-permute-done((bf16[24,128,128]{1,2,0:T(8,128)(2,1)S(1)}, bf16[24,128,128]{1,2,0:T(8,128)(2,1)S(1)}, u32[]{:S(2)}, u32[]{:S(2)}) %collective-permute-start.21) | collective-permute-done | bytes 786464 | tf_op jit(solution)/shard_map/ppermute | solution.py:218
  650.2 15.0 %collective-permute-done.22 = bf16[24,128,128]{1,2,0:T(8,128)(2,1)S(1)} collective-permute-done((bf16[24,128,128]{1,2,0:T(8,128)(2,1)S(1)}, bf16[24,128,128]{1,2,0:T(8,128)(2,1)S(1)}, u32[]{:S(2)}, u32[]{:S(2)}) %collective-permute-start.22) | collective-permute-done | bytes 786464 | tf_op jit(solution)/shard_map/ppermute | solution.py:218
  670.1 14.1 %collective-permute-done.23 = bf16[24,128,128]{1,2,0:T(8,128)(2,1)S(1)} collective-permute-done((bf16[24,128,128]{1,2,0:T(8,128)(2,1)S(1)}, bf16[24,128,128]{1,2,0:T(8,128)(2,1)S(1)}, u32[]{:S(2)}, u32[]{:S(2)}) %collective-permute-start.23) | collective-permute-done | bytes 786464 | tf_op jit(solution)/shard_map/ppermute | solution.py:218
  689.1 28.4 %copy.92 = bf16[32,128,24,128]{3,2,1,0:T(8,128)(2,1)} copy(bf16[32,128,24,128]{3,1,2,0:T(8,128)(2,1)} %bitcast.238) | data formatting | bytes 50331648 | tf_op jit(solution)/shard_map/dot_general | solution.py:259
  724.1 13.6 %fusion.9 = bf16[256,4096]{1,0:T(8,128)(2,1)} fusion(bf16[256,24,128]{0,2,1:T(8,128)(2,1)S(1)} %copy-done.1, bf16[4096,24,128]{2,1,0:T(8,128)(2,1)} %bitcast.240), kind=kOutput, calls=%fused_computation.31 | convolution fusion | flops 6443499520 | bytes 28835840 | tf_op jit(solution)/shard_map/dot_general | solution.py:259
  743.2 6.7 copy.99
  758.6 8.5 %collective-permute-done.26 = bf16[24,128,128]{1,2,0:T(8,128)(2,1)S(1)} collective-permute-done((bf16[24,128,128]{1,2,0:T(8,128)(2,1)S(1)}, bf16[24,128,128]{1,2,0:T(8,128)(2,1)S(1)}, u32[]{:S(2)}, u32[]{:S(2)}) %collective-permute-start.26) | collective-permute-done | bytes 786464 | tf_op jit(solution)/shard_map/ppermute | solution.py:218
  773.7 11.7 %multiply_subtract_fusion = (f32[512,3072]{1,0:T(8,128)}, f32[512,3072]{1,0:T(8,128)}, f32[512,3072]{1,0:T(8,128)}) fusion(f32[512,3072]{1,0:T(8,128)S(1)} %bitcast.261, f32[64,8,24,128]{3,2,1,0:T(8,128)S(1)} %bitcast.264, f32[512,3072]{1,0:T(8,128)} %param.28, f32[512,3072]{1,0:T(8,128)} %param.29), kind=kLoop, calls=%fused_computation.28 | loop fusion | flops 20447232 | bytes 44040192 | tf_op jit(solution)/shard_map/sub | solution.py:32
  793.6 6.7 copy.97
  806.4 12.8 %multiply_subtract_fusion.1 = (f32[512,3072]{1,0:T(8,128)}, f32[512,3072]{1,0:T(8,128)}, f32[512,3072]{1,0:T(8,128)}) fusion(f32[512,3072]{1,0:T(8,128)S(1)} %bitcast.263, f32[64,8,24,128]{3,2,1,0:T(8,128)} %bitcast.265, f32[512,3072]{1,0:T(8,128)} %param.26, f32[512,3072]{1,0:T(8,128)} %param.27), kind=kLoop, calls=%fused_computation.29 | loop fusion | flops 20447232 | bytes 44040192 | tf_op jit(solution)/shard_map/sub | solution.py:32
  (204 shorter events, 145.8 us)
Async XLA Ops:
  7.2 360.3 %all-gather.5.cloned.1.call-start = ((), (), s32[]{:S(2)}) async-start(), calls=%async_computation.2 | async-start | bytes 2621440 | tf_op jit(solution)/shard_map/all_gather | solution.py:188
  9.3 370.7 %all-gather.7.cloned.1.call-start = ((), (), s32[]{:S(2)}) async-start(), calls=%async_computation.3 | async-start | bytes 2621440 | tf_op jit(solution)/shard_map/all_gather | solution.py:189
  11.4 406.0 %all-gather.9.cloned.1.call-start = ((), (), s32[]{:S(2)}) async-start(), calls=%async_computation.6 | async-start | bytes 14745600 | tf_op jit(solution)/shard_map/all_gather | solution.py:180
  24.5 600.2 %reduce-scatter.5.cloned.1.call-start = ((), (), s32[]{:S(2)}) async-start(), calls=%async_computation.5 | async-start | bytes 14155776 | tf_op jit(solution)/shard_map/reduce_scatter | solution.py:254
  36.7 21.2 %collective-permute-start.7 = (bf16[25,128,128]{2,1,0:T(8,128)(2,1)S(1)}, bf16[25,128,128]{2,1,0:T(8,128)(2,1)S(1)}, u32[]{:S(2)}, u32[]{:S(2)}) collective-permute-start(bf16[25,128,128]{2,1,0:T(8,128)(2,1)S(1)} %get-tuple-element.72), channel_id=1, source_target_pairs={{0,8},{4,0},{12,4},{20,12},{28,20},{24,28},{16,24},{8,16},{1,9},{5... | collective-permute-start | bytes 2457608 | tf_op jit(solution)/shard_map/ppermute | solution.py:158
  39.8 19.9 %collective-permute-start = (bf16[25,128,128]{2,1,0:T(8,128)(2,1)S(1)}, bf16[25,128,128]{2,1,0:T(8,128)(2,1)S(1)}, u32[]{:S(2)}, u32[]{:S(2)}) collective-permute-start(bf16[25,128,128]{2,1,0:T(8,128)(2,1)S(1)} %slice.193), channel_id=1, source_target_pairs={{0,4},{4,12},{12,20},{20,28},{28,24},{24,16},{16,8},{8,0},{1,5},{5... | collective-permute-start | bytes 2457608 | tf_op jit(solution)/shard_map/ppermute | solution.py:157
  57.9 24.6 %collective-permute-start.8 = (bf16[25,128,128]{2,1,0:T(8,128)(2,1)S(1)}, bf16[25,128,128]{2,1,0:T(8,128)(2,1)}, u32[]{:S(2)}, u32[]{:S(2)}) collective-permute-start(bf16[25,128,128]{2,1,0:T(8,128)(2,1)S(1)} %collective-permute-done.7), channel_id=1, source_target_pairs={{0,8},{4,0},{12,4},{20,12},{28,20},{24,28},{16,24},{8,16},{1,9},{5... | collective-permute-start | bytes 2457608 | tf_op jit(solution)/shard_map/ppermute | solution.py:158
  59.7 30.9 %collective-permute-start.1 = (bf16[25,128,128]{2,1,0:T(8,128)(2,1)S(1)}, bf16[25,128,128]{2,1,0:T(8,128)(2,1)}, u32[]{:S(2)}, u32[]{:S(2)}) collective-permute-start(bf16[25,128,128]{2,1,0:T(8,128)(2,1)S(1)} %collective-permute-done), channel_id=1, source_target_pairs={{0,4},{4,12},{12,20},{20,28},{28,24},{24,16},{16,8},{8,0},{1,5},{5... | collective-permute-start | bytes 2457608 | tf_op jit(solution)/shard_map/ppermute | solution.py:157
  82.5 38.8 %collective-permute-start.9 = (bf16[25,128,128]{2,1,0:T(8,128)(2,1)}, bf16[25,128,128]{2,1,0:T(8,128)(2,1)}, u32[]{:S(2)}, u32[]{:S(2)}) collective-permute-start(bf16[25,128,128]{2,1,0:T(8,128)(2,1)} %collective-permute-done.8), channel_id=1, source_target_pairs={{0,8},{4,0},{12,4},{20,12},{28,20},{24,28},{16,24},{8,16},{1,9},{5... | collective-permute-start | bytes 2457608 | tf_op jit(solution)/shard_map/ppermute | solution.py:158
  90.6 56.2 %collective-permute-start.2 = (bf16[25,128,128]{2,1,0:T(8,128)(2,1)}, bf16[25,128,128]{2,1,0:T(8,128)(2,1)S(1)}, u32[]{:S(2)}, u32[]{:S(2)}) collective-permute-start(bf16[25,128,128]{2,1,0:T(8,128)(2,1)} %collective-permute-done.1), channel_id=1, source_target_pairs={{0,4},{4,12},{12,20},{20,28},{28,24},{24,16},{16,8},{8,0},{1,5},{5... | collective-permute-start | bytes 2457608 | tf_op jit(solution)/shard_map/ppermute | solution.py:157
  121.3 43.7 %collective-permute-start.10 = (bf16[25,128,128]{2,1,0:T(8,128)(2,1)}, bf16[25,128,128]{2,1,0:T(8,128)(2,1)}, u32[]{:S(2)}, u32[]{:S(2)}) collective-permute-start(bf16[25,128,128]{2,1,0:T(8,128)(2,1)} %collective-permute-done.9), channel_id=1, source_target_pairs={{0,8},{4,0},{12,4},{20,12},{28,20},{24,28},{16,24},{8,16},{1,9},{5... | collective-permute-start | bytes 2457608 | tf_op jit(solution)/shard_map/ppermute | solution.py:158
  146.8 21.6 %collective-permute-start.3 = (bf16[25,128,128]{2,1,0:T(8,128)(2,1)S(1)}, bf16[25,128,128]{2,1,0:T(8,128)(2,1)}, u32[]{:S(2)}, u32[]{:S(2)}) collective-permute-start(bf16[25,128,128]{2,1,0:T(8,128)(2,1)S(1)} %collective-permute-done.2), channel_id=1, source_target_pairs={{0,4},{4,12},{12,20},{20,28},{28,24},{24,16},{16,8},{8,0},{1,5},{5... | collective-permute-start | bytes 2457608 | tf_op jit(solution)/shard_map/ppermute | solution.py:157
  165.0 34.6 %collective-permute-start.11 = (bf16[25,128,128]{2,1,0:T(8,128)(2,1)}, bf16[25,128,128]{2,1,0:T(8,128)(2,1)S(1)}, u32[]{:S(2)}, u32[]{:S(2)}) collective-permute-start(bf16[25,128,128]{2,1,0:T(8,128)(2,1)} %collective-permute-done.10), channel_id=1, source_target_pairs={{0,8},{4,0},{12,4},{20,12},{28,20},{24,28},{16,24},{8,16},{1,9},{5... | collective-permute-start | bytes 2457608 | tf_op jit(solution)/shard_map/ppermute | solution.py:158
  168.4 54.7 %collective-permute-start.4 = (bf16[25,128,128]{2,1,0:T(8,128)(2,1)}, bf16[25,128,128]{2,1,0:T(8,128)(2,1)S(1)}, u32[]{:S(2)}, u32[]{:S(2)}) collective-permute-start(bf16[25,128,128]{2,1,0:T(8,128)(2,1)} %collective-permute-done.3), channel_id=1, source_target_pairs={{0,4},{4,12},{12,20},{20,28},{28,24},{24,16},{16,8},{8,0},{1,5},{5... | collective-permute-start | bytes 2457608 | tf_op jit(solution)/shard_map/ppermute | solution.py:157
  199.6 52.9 %collective-permute-start.12 = (bf16[25,128,128]{2,1,0:T(8,128)(2,1)S(1)}, bf16[25,128,128]{2,1,0:T(8,128)(2,1)S(1)}, u32[]{:S(2)}, u32[]{:S(2)}) collective-permute-start(bf16[25,128,128]{2,1,0:T(8,128)(2,1)S(1)} %collective-permute-done.11), channel_id=1, source_target_pairs={{0,8},{4,0},{12,4},{20,12},{28,20},{24,28},{16,24},{8,16},{1,9},{5... | collective-permute-start | bytes 2457608 | tf_op jit(solution)/shard_map/ppermute | solution.py:158
  223.1 57.6 %collective-permute-start.5 = (bf16[25,128,128]{2,1,0:T(8,128)(2,1)S(1)}, bf16[25,128,128]{2,1,0:T(8,128)(2,1)S(1)}, u32[]{:S(2)}, u32[]{:S(2)}) collective-permute-start(bf16[25,128,128]{2,1,0:T(8,128)(2,1)S(1)} %collective-permute-done.4), channel_id=1, source_target_pairs={{0,4},{4,12},{12,20},{20,28},{28,24},{24,16},{16,8},{8,0},{1,5},{5... | collective-permute-start | bytes 2457608 | tf_op jit(solution)/shard_map/ppermute | solution.py:157
  252.5 52.3 %collective-permute-start.13 = (bf16[25,128,128]{2,1,0:T(8,128)(2,1)S(1)}, bf16[25,128,128]{2,1,0:T(8,128)(2,1)S(1)}, u32[]{:S(2)}, u32[]{:S(2)}) collective-permute-start(bf16[25,128,128]{2,1,0:T(8,128)(2,1)S(1)} %collective-permute-done.12), channel_id=1, source_target_pairs={{0,8},{4,0},{12,4},{20,12},{28,20},{24,28},{16,24},{8,16},{1,9},{5... | collective-permute-start | bytes 2457608 | tf_op jit(solution)/shard_map/ppermute | solution.py:158
  280.7 44.7 %collective-permute-start.6 = (bf16[25,128,128]{2,1,0:T(8,128)(2,1)S(1)}, bf16[25,128,128]{2,1,0:T(8,128)(2,1)S(1)}, u32[]{:S(2)}, u32[]{:S(2)}) collective-permute-start(bf16[25,128,128]{2,1,0:T(8,128)(2,1)S(1)} %collective-permute-done.5), channel_id=1, source_target_pairs={{0,4},{4,12},{12,20},{20,28},{28,24},{24,16},{16,8},{8,0},{1,5},{5... | collective-permute-start | bytes 2457608 | tf_op jit(solution)/shard_map/ppermute | solution.py:157
  417.4 401.8 %reduce-scatter.3.cloned.1.call-start = ((), (), s32[]{:S(2)}) async-start(), calls=%async_computation.4 | async-start | bytes 2621440 | tf_op jit(solution)/shard_map/reduce_scatter | solution.py:269
  625.9 19.4 %collective-permute-start.21 = (bf16[24,128,128]{1,2,0:T(8,128)(2,1)S(1)}, bf16[24,128,128]{1,2,0:T(8,128)(2,1)S(1)}, u32[]{:S(2)}, u32[]{:S(2)}) collective-permute-start(bf16[24,128,128]{1,2,0:T(8,128)(2,1)S(1)} %slice_bitcast_fusion), channel_id=1, source_target_pairs={{0,8},{4,0},{12,4},{20,12},{28,20},{24,28},{16,24},{8,16},{1,9},{5... | collective-permute-start | bytes 2359304 | tf_op jit(solution)/shard_map/ppermute | solution.py:218
  627.2 19.9 %collective-permute-start.14 = (bf16[24,128,128]{1,2,0:T(8,128)(2,1)S(1)}, bf16[24,128,128]{1,2,0:T(8,128)(2,1)S(1)}, u32[]{:S(2)}, u32[]{:S(2)}) collective-permute-start(bf16[24,128,128]{1,2,0:T(8,128)(2,1)S(1)} %slice_bitcast_fusion.1), channel_id=1, source_target_pairs={{0,4},{4,12},{12,20},{20,28},{28,24},{24,16},{16,8},{8,0},{1,5},{5... | collective-permute-start | bytes 2359304 | tf_op jit(solution)/shard_map/ppermute | solution.py:217
  646.7 18.5 %collective-permute-start.22 = (bf16[24,128,128]{1,2,0:T(8,128)(2,1)S(1)}, bf16[24,128,128]{1,2,0:T(8,128)(2,1)S(1)}, u32[]{:S(2)}, u32[]{:S(2)}) collective-permute-start(bf16[24,128,128]{1,2,0:T(8,128)(2,1)S(1)} %fusion.29), channel_id=1, source_target_pairs={{0,8},{4,0},{12,4},{20,12},{28,20},{24,28},{16,24},{8,16},{1,9},{5... | collective-permute-start | bytes 2359304 | tf_op jit(solution)/shard_map/ppermute | solution.py:218
  648.4 18.8 %collective-permute-start.15 = (bf16[24,128,128]{1,2,0:T(8,128)(2,1)S(1)}, bf16[24,128,128]{1,2,0:T(8,128)(2,1)S(1)}, u32[]{:S(2)}, u32[]{:S(2)}) collective-permute-start(bf16[24,128,128]{1,2,0:T(8,128)(2,1)S(1)} %fusion.35), channel_id=1, source_target_pairs={{0,4},{4,12},{12,20},{20,28},{28,24},{24,16},{16,8},{8,0},{1,5},{5... | collective-permute-start | bytes 2359304 | tf_op jit(solution)/shard_map/ppermute | solution.py:217
  666.6 17.6 %collective-permute-start.23 = (bf16[24,128,128]{1,2,0:T(8,128)(2,1)S(1)}, bf16[24,128,128]{1,2,0:T(8,128)(2,1)S(1)}, u32[]{:S(2)}, u32[]{:S(2)}) collective-permute-start(bf16[24,128,128]{1,2,0:T(8,128)(2,1)S(1)} %fusion.28), channel_id=1, source_target_pairs={{0,8},{4,0},{12,4},{20,12},{28,20},{24,28},{16,24},{8,16},{1,9},{5... | collective-permute-start | bytes 2359304 | tf_op jit(solution)/shard_map/ppermute | solution.py:218
  668.6 17.9 %collective-permute-start.16 = (bf16[24,128,128]{1,2,0:T(8,128)(2,1)S(1)}, bf16[24,128,128]{1,2,0:T(8,128)(2,1)S(1)}, u32[]{:S(2)}, u32[]{:S(2)}) collective-permute-start(bf16[24,128,128]{1,2,0:T(8,128)(2,1)S(1)} %fusion.34), channel_id=1, source_target_pairs={{0,4},{4,12},{12,20},{20,28},{28,24},{24,16},{16,8},{8,0},{1,5},{5... | collective-permute-start | bytes 2359304 | tf_op jit(solution)/shard_map/ppermute | solution.py:217
  685.6 32.0 %collective-permute-start.24 = (bf16[24,128,128]{1,2,0:T(8,128)(2,1)S(1)}, bf16[24,128,128]{1,2,0:T(8,128)(2,1)S(1)}, u32[]{:S(2)}, u32[]{:S(2)}) collective-permute-start(bf16[24,128,128]{1,2,0:T(8,128)(2,1)S(1)} %fusion.27), channel_id=1, source_target_pairs={{0,8},{4,0},{12,4},{20,12},{28,20},{24,28},{16,24},{8,16},{1,9},{5... | collective-permute-start | bytes 2359304 | tf_op jit(solution)/shard_map/ppermute | solution.py:218
  687.9 32.8 %collective-permute-start.17 = (bf16[24,128,128]{1,2,0:T(8,128)(2,1)S(1)}, bf16[24,128,128]{1,2,0:T(8,128)(2,1)S(1)}, u32[]{:S(2)}, u32[]{:S(2)}) collective-permute-start(bf16[24,128,128]{1,2,0:T(8,128)(2,1)S(1)} %fusion.33), channel_id=1, source_target_pairs={{0,4},{4,12},{12,20},{20,28},{28,24},{24,16},{16,8},{8,0},{1,5},{5... | collective-permute-start | bytes 2359304 | tf_op jit(solution)/shard_map/ppermute | solution.py:217
  719.8 30.0 %collective-permute-start.25 = (bf16[24,128,128]{1,2,0:T(8,128)(2,1)}, bf16[24,128,128]{1,2,0:T(8,128)(2,1)}, u32[]{:S(2)}, u32[]{:S(2)}) collective-permute-start(bf16[24,128,128]{1,2,0:T(8,128)(2,1)} %fusion.26), channel_id=1, source_target_pairs={{0,8},{4,0},{12,4},{20,12},{28,20},{24,28},{16,24},{8,16},{1,9},{5... | collective-permute-start | bytes 2359304 | tf_op jit(solution)/shard_map/ppermute | solution.py:218
  723.0 29.6 %collective-permute-start.18 = (bf16[24,128,128]{1,2,0:T(8,128)(2,1)}, bf16[24,128,128]{1,2,0:T(8,128)(2,1)}, u32[]{:S(2)}, u32[]{:S(2)}) collective-permute-start(bf16[24,128,128]{1,2,0:T(8,128)(2,1)} %fusion.32), channel_id=1, source_target_pairs={{0,4},{4,12},{12,20},{20,28},{28,24},{24,16},{16,8},{8,0},{1,5},{5... | collective-permute-start | bytes 2359304 | tf_op jit(solution)/shard_map/ppermute | solution.py:217
  751.4 15.6 %collective-permute-start.26 = (bf16[24,128,128]{1,2,0:T(8,128)(2,1)S(1)}, bf16[24,128,128]{1,2,0:T(8,128)(2,1)S(1)}, u32[]{:S(2)}, u32[]{:S(2)}) collective-permute-start(bf16[24,128,128]{1,2,0:T(8,128)(2,1)S(1)} %fusion.25), channel_id=1, source_target_pairs={{0,8},{4,0},{12,4},{20,12},{28,20},{24,28},{16,24},{8,16},{1,9},{5... | collective-permute-start | bytes 2359304 | tf_op jit(solution)/shard_map/ppermute | solution.py:218
  754.4 16.3 %collective-permute-start.19 = (bf16[24,128,128]{1,2,0:T(8,128)(2,1)S(1)}, bf16[24,128,128]{1,2,0:T(8,128)(2,1)S(1)}, u32[]{:S(2)}, u32[]{:S(2)}) collective-permute-start(bf16[24,128,128]{1,2,0:T(8,128)(2,1)S(1)} %fusion.31), channel_id=1, source_target_pairs={{0,4},{4,12},{12,20},{20,28},{28,24},{24,16},{16,8},{8,0},{1,5},{5... | collective-permute-start | bytes 2359304 | tf_op jit(solution)/shard_map/ppermute | solution.py:217
  769.3 16.0 %collective-permute-start.27 = (bf16[24,128,128]{1,2,0:T(8,128)(2,1)}, bf16[24,128,128]{1,2,0:T(8,128)(2,1)}, u32[]{:S(2)}, u32[]{:S(2)}) collective-permute-start(bf16[24,128,128]{1,2,0:T(8,128)(2,1)} %fusion.24), channel_id=1, source_target_pairs={{0,8},{4,0},{12,4},{20,12},{28,20},{24,28},{16,24},{8,16},{1,9},{5... | collective-permute-start | bytes 2359304 | tf_op jit(solution)/shard_map/ppermute | solution.py:218
  (11 other events, 332.2 us)
Sparse Core Ops, SparseCore 0:
  10.1 25.2 all-gather.4
  37.6 22.5 all-gather.6
  63.0 261.9 all-gather.8
  417.5 207.1 reduce-scatter.4
  737.9 31.1 reduce-scatter.2

commit v9 on v8

--- a/solution.py
+++ b/solution.py
@@ -177,7 +177,8 @@
         )
 
     got_up = ring_gather(package(w_up, flat_up))
-    got_down = lax.all_gather(package(w_down, flat_down), "row", axis=0)
+    got_up, package_down = lax.optimization_barrier((got_up, package(w_down, flat_down)))
+    got_down = lax.all_gather(package_down, "row", axis=0)
     mask_blocks = got_up.at[where_is(jnp.full((n_row, 1), mask_slot, jnp.int32))[:, 0]].get(
         mode="promise_in_bounds"
     )

time: 834 us -> 772 us (0.926)
  starting transfers between devices: 97 us -> 31 us
    all_gather x1, waiting for transfers between devices: 0.01 us -> 98.3 us  [shards(): got_down = lax.all_gather(package_down, 'row', axis=0)]
    ppermute x7, waiting for transfers between devices: 158 us -> 77.2 us  [ring_gather(): b = lax.ppermute(b, 'row', left)]
    ppermute x7, starting transfers between devices: 81.5 us -> 10.5 us  [ring_gather(): b = lax.ppermute(b, 'row', left)]
    ppermute x7, waiting for transfers between devices: 27.1 us -> 9.24 us  [ring_gather(): a = lax.ppermute(a, 'row', right)]
    unnamed x36 -> x48, local copies, waits for them, and re-layouts: 23.5 us -> 23.4 us
  transfers between devices with their start and end apart: 33 -> 33, of which waited for: 17 -> 18; matrix products, arithmetic and copies ran while one was open for 43% -> 47% of each run, Pallas kernels for 0% -> 0%
where the time goes in v9:
time: 772 us; the launch traced here: 763 us
  waiting for transfers between devices  353 us (46%)
  local copies, waits for them, and re-layouts  211 us (27%)
  other arithmetic  86.4 us (11%)
  matrix products  67 us (9%)
  starting transfers between devices  31 us (4%)
  between operations  14.9 us (2%)
    reduce_scatter x1, waiting for transfers between devices, shards(): lax.psum_scatter(sent_down, 'row', scatter_dimension=0, tiled=True)[0]  113 us
    all_gather x1, waiting for transfers between devices, shards(): got_down = lax.all_gather(package_down, 'row', axis=0)  98.3 us
    ppermute x7, waiting for transfers between devices, ring_gather(): b = lax.ppermute(b, 'row', left)  77.2 us
    gather x3, local copies, waits for them, and re-layouts, kept_blocks(): return view.at[rows, :, cols, :].get(mode='promise_in_bounds')  60.8 us
    ppermute x7, waiting for transfers between devices, ring_reduce(): in_b = lax.ppermute(acc_b, 'row', left).astype(jnp.float32)  53.6 us
    gather x2, local copies, waits for them, and re-layouts, rebuild(): dense = got.at[at(k).reshape(-1)].get(mode='promise_in_bounds')  50.1 us
    dot_general x1, local copies, waits for them, and re-layouts, shards(): lax.dot_general(pre_grad.reshape((pre_grad.shape[0], nc, block)), up_whol...  28.4 us
    dot_general x2, matrix products, forward(): lax.dot_general(rows3, w4, (((1, 2), (0, 2)), ((), ())), preferred_elemen...  26.7 us
  transfers between devices with their start and end apart: 33, of which 18 were waited for; matrix products, arithmetic and copies ran while one was open for 47% of the time, Pallas kernels for 0%

profile of v9, /device:TPU:0, one launch (start us, length us, event | category | flops | bytes accessed | tf_op | source)
XLA Modules:
  0.0 763.2 jit_solution(10714794758692268931)
XLA Ops:
  27.0 18.3 %collective-permute-done.7 = bf16[25,128,128]{2,1,0:T(8,128)(2,1)S(1)} collective-permute-done((bf16[25,128,128]{2,1,0:T(8,128)(2,1)S(1)}, bf16[25,128,128]{2,1,0:T(8,128)(2,1)S(1)}, u32[]{:S(2)}, u32[]{:S(2)}) %collective-permute-start.7) | collective-permute-done | bytes 819232 | tf_op jit(solution)/shard_map/ppermute | solution.py:158
  47.9 17.1 %collective-permute-done.8 = bf16[25,128,128]{2,1,0:T(8,128)(2,1)S(1)} collective-permute-done((bf16[25,128,128]{2,1,0:T(8,128)(2,1)S(1)}, bf16[25,128,128]{2,1,0:T(8,128)(2,1)S(1)}, u32[]{:S(2)}, u32[]{:S(2)}) %collective-permute-start.8) | collective-permute-done | bytes 819232 | tf_op jit(solution)/shard_map/ppermute | solution.py:158
  72.4 11.6 %collective-permute-done.9 = bf16[25,128,128]{2,1,0:T(8,128)(2,1)} collective-permute-done((bf16[25,128,128]{2,1,0:T(8,128)(2,1)S(1)}, bf16[25,128,128]{2,1,0:T(8,128)(2,1)}, u32[]{:S(2)}, u32[]{:S(2)}) %collective-permute-start.9) | collective-permute-done | bytes 819232 | tf_op jit(solution)/shard_map/ppermute | solution.py:158
  93.6 8.7 %collective-permute-done.10 = bf16[25,128,128]{2,1,0:T(8,128)(2,1)} collective-permute-done((bf16[25,128,128]{2,1,0:T(8,128)(2,1)}, bf16[25,128,128]{2,1,0:T(8,128)(2,1)}, u32[]{:S(2)}, u32[]{:S(2)}) %collective-permute-start.10) | collective-permute-done | bytes 819232 | tf_op jit(solution)/shard_map/ppermute | solution.py:158
  113.1 7.9 %collective-permute-done.11 = bf16[25,128,128]{2,1,0:T(8,128)(2,1)S(1)} collective-permute-done((bf16[25,128,128]{2,1,0:T(8,128)(2,1)}, bf16[25,128,128]{2,1,0:T(8,128)(2,1)S(1)}, u32[]{:S(2)}, u32[]{:S(2)}) %collective-permute-start.11) | collective-permute-done | bytes 819232 | tf_op jit(solution)/shard_map/ppermute | solution.py:158
  132.8 6.6 collective-permute-done.12
  147.7 7.1 collective-permute-done.13
  159.7 10.1 %pad_maximum_fusion = bf16[400,128,128]{2,1,0:T(8,128)(2,1)} fusion(bf16[200,128,128]{2,1,0:T(8,128)(2,1)} %bitcast.271, bf16[200,128,128]{2,1,0:T(8,128)(2,1)} %bitcast.270), kind=kLoop, calls=%fused_computation.19 | loop fusion | flops 6553600 | bytes 26214400 | tf_op jit(solution)/shard_map/concatenate | solution.py:161
  172.2 5.4 gather_fusion.2
  178.1 25.0 %gather_fusion.3 = bf16[768,128,128]{2,1,0:T(8,128)(2,1)} fusion(bf16[400,128,128]{2,1,0:T(8,128)(2,1)} %pad_maximum_fusion, s32[1024]{0:T(1024)S(1)} %get-tuple-element.85), kind=kCustom, calls=%fused_computation.3 | custom fusion | bytes 50334720 | tf_op jit(solution)/shard_map/gather | solution.py:195
  204.4 12.5 %fusion.85 = f32[24,128,256,1]{2,1,0,3:T(8,128)S(1)} fusion(bf16[32,24,128,128]{3,2,1,0:T(8,128)(2,1)} %bitcast.237, bf16[256,32,128,1]{0,2,3,1:T(8,128)(2,1)} %bitcast.268), kind=kOutput, calls=%fused_computation.220 | convolution fusion | flops 6442450944 | bytes 30408704 | tf_op jit(solution)/shard_map/dot_general | solution.py:238
  216.9 12.9 %convert_bitcast_fusion.1 = bf16[32,128,24,128]{1,3,0,2:T(8,128)(2,1)} fusion(bf16[256,32,128,1]{0,2,1,3:T(8,128)(2,1)} %bitcast.274, f32[24,128,256,1]{2,1,0,3:T(8,128)S(1)} %fusion.85), kind=kOutput, calls=%fused_computation.18 | convolution fusion | flops 6458966016 | bytes 30408704 | tf_op jit(solution)/shard_map/dot_general | solution.py:245
  229.8 24.6 %gather_fusion.5 = bf16[384,128,128]{1,2,0:T(8,128)(2,1)} fusion(bf16[32,128,24,128]{1,3,0,2:T(8,128)(2,1)} %convert_bitcast_fusion.1, s32[384]{0:T(512)S(1)} %reshape.769), kind=kCustom, calls=%fused_computation.5 | custom fusion | bytes 25168896 | tf_op jit(solution)/shard_map/gather | solution.py:206
  254.4 98.3 %all-gather.9.cloned.1.call-done = bf16[400,128,128]{2,1,0:T(8,128)(2,1)} async-done(((bf16[50,128,128]{2,1,0:T(8,128)(2,1)}), bf16[400,128,128]{2,1,0:T(8,128)(2,1)}) %all-gather.9.cloned.1.call-update) | async-done | bytes 13107216 | tf_op jit(solution)/shard_map/all_gather | solution.py:181
  358.8 25.1 %gather_fusion.6 = bf16[768,128,128]{2,1,0:T(8,128)(2,1)} fusion(bf16[400,128,128]{2,1,0:T(8,128)(2,1)} %all-gather.9.cloned.1.call-done, s32[1024]{0:T(1024)S(1)} %get-tuple-element.83), kind=kCustom, calls=%fused_computation.6 | custom fusion | bytes 50334720 | tf_op jit(solution)/shard_map/gather | solution.py:195
  383.9 14.2 %fusion.17 = bf16[256,24,128]{0,2,1:T(8,128)(2,1)} fusion(f32[24,128,256,1]{2,1,0,3:T(8,128)S(1)} %fusion.85, bf16[32,24,128,128]{3,2,1,0:T(8,128)(2,1)} %bitcast.241, bf16[256,32,128,1]{0,2,3,1:T(8,128)(2,1)} %bitcast.275), kind=kOutput, calls=%fused_computation.38 | convolution fusion | flops 6450315264 | bytes 31981568 | tf_op jit(solution)/shard_map/dot_general | solution.py:238
  398.1 13.8 %convert_bitcast_fusion = bf16[32,128,24,128]{1,3,0,2:T(8,128)(2,1)} fusion(bf16[256,32,128,1]{0,2,1,3:T(8,128)(2,1)} %bitcast.269, bf16[256,24,128]{0,2,1:T(8,128)(2,1)} %fusion.17), kind=kOutput, calls=%fused_computation.17 | convolution fusion | flops 6455033856 | bytes 28835840 | tf_op jit(solution)/shard_map/dot_general | solution.py:245
  412.0 18.5 %gather_fusion.9 = bf16[192,128,128]{1,2,0:T(8,128)(2,1)} fusion(bf16[32,128,24,128]{1,3,0,2:T(8,128)(2,1)} %convert_bitcast_fusion, s32[192]{0:T(256)S(1)} %reshape.799), kind=kCustom, calls=%fused_computation.9 | custom fusion | bytes 12584448 | tf_op jit(solution)/shard_map/gather | solution.py:206
  430.5 17.7 %gather_fusion.12 = bf16[192,128,128]{1,2,0:T(8,128)(2,1)} fusion(bf16[32,128,24,128]{1,3,0,2:T(8,128)(2,1)} %convert_bitcast_fusion, s32[192]{0:T(256)S(1)} %reshape.821), kind=kCustom, calls=%fused_computation.12 | custom fusion | bytes 12584448 | tf_op jit(solution)/shard_map/gather | solution.py:206
  448.2 113.5 %reduce-scatter.5.cloned.1.call-done = bf16[1,48,128,128]{2,3,1,0:T(8,128)(2,1)} async-done(((bf16[8,48,128,128]{2,3,1,0:T(8,128)(2,1)}), bf16[1,48,128,128]{2,3,1,0:T(8,128)(2,1)}) %reduce-scatter.5.cloned.1.call-update) | async-done | bytes 1572880 | tf_op jit(solution)/shard_map/reduce_scatter | solution.py:255
  566.2 16.1 %collective-permute-done.21 = bf16[24,128,128]{1,2,0:T(8,128)(2,1)S(1)} collective-permute-done((bf16[24,128,128]{1,2,0:T(8,128)(2,1)S(1)}, bf16[24,128,128]{1,2,0:T(8,128)(2,1)S(1)}, u32[]{:S(2)}, u32[]{:S(2)}) %collective-permute-start.21) | collective-permute-done | bytes 786464 | tf_op jit(solution)/shard_map/ppermute | solution.py:219
  587.1 15.0 %collective-permute-done.22 = bf16[24,128,128]{1,2,0:T(8,128)(2,1)S(1)} collective-permute-done((bf16[24,128,128]{1,2,0:T(8,128)(2,1)S(1)}, bf16[24,128,128]{1,2,0:T(8,128)(2,1)S(1)}, u32[]{:S(2)}, u32[]{:S(2)}) %collective-permute-start.22) | collective-permute-done | bytes 786464 | tf_op jit(solution)/shard_map/ppermute | solution.py:219
  607.1 14.1 %collective-permute-done.23 = bf16[24,128,128]{1,2,0:T(8,128)(2,1)S(1)} collective-permute-done((bf16[24,128,128]{1,2,0:T(8,128)(2,1)S(1)}, bf16[24,128,128]{1,2,0:T(8,128)(2,1)S(1)}, u32[]{:S(2)}, u32[]{:S(2)}) %collective-permute-start.23) | collective-permute-done | bytes 786464 | tf_op jit(solution)/shard_map/ppermute | solution.py:219
  626.1 28.4 %copy.92 = bf16[32,128,24,128]{3,2,1,0:T(8,128)(2,1)} copy(bf16[32,128,24,128]{3,1,2,0:T(8,128)(2,1)} %bitcast.238) | data formatting | bytes 50331648 | tf_op jit(solution)/shard_map/dot_general | solution.py:260
  661.1 13.6 %fusion.9 = bf16[256,4096]{1,0:T(8,128)(2,1)} fusion(bf16[256,24,128]{0,2,1:T(8,128)(2,1)S(1)} %copy-done.1, bf16[4096,24,128]{2,1,0:T(8,128)(2,1)} %bitcast.240), kind=kOutput, calls=%fused_computation.31 | convolution fusion | flops 6443499520 | bytes 28835840 | tf_op jit(solution)/shard_map/dot_general | solution.py:260
  676.5 3.7 gather_fusion.14
  680.1 6.7 copy.99
  695.6 8.5 %collective-permute-done.26 = bf16[24,128,128]{1,2,0:T(8,128)(2,1)S(1)} collective-permute-done((bf16[24,128,128]{1,2,0:T(8,128)(2,1)S(1)}, bf16[24,128,128]{1,2,0:T(8,128)(2,1)S(1)}, u32[]{:S(2)}, u32[]{:S(2)}) %collective-permute-start.26) | collective-permute-done | bytes 786464 | tf_op jit(solution)/shard_map/ppermute | solution.py:219
  710.6 11.8 %multiply_subtract_fusion = (f32[512,3072]{1,0:T(8,128)}, f32[512,3072]{1,0:T(8,128)}, f32[512,3072]{1,0:T(8,128)}) fusion(f32[512,3072]{1,0:T(8,128)S(1)} %bitcast.261, f32[64,8,24,128]{3,2,1,0:T(8,128)S(1)} %bitcast.264, f32[512,3072]{1,0:T(8,128)} %param.28, f32[512,3072]{1,0:T(8,128)} %param.29), kind=kLoop, calls=%fused_computation.28 | loop fusion | flops 20447232 | bytes 44040192 | tf_op jit(solution)/shard_map/sub | solution.py:32
  730.7 6.7 copy.97
  737.4 6.1 broadcast_select_fusion.1
  743.5 12.8 %multiply_subtract_fusion.1 = (f32[512,3072]{1,0:T(8,128)}, f32[512,3072]{1,0:T(8,128)}, f32[512,3072]{1,0:T(8,128)}) fusion(f32[512,3072]{1,0:T(8,128)S(1)} %bitcast.263, f32[64,8,24,128]{3,2,1,0:T(8,128)} %bitcast.265, f32[512,3072]{1,0:T(8,128)} %param.26, f32[512,3072]{1,0:T(8,128)} %param.27), kind=kLoop, calls=%fused_computation.29 | loop fusion | flops 20447232 | bytes 44040192 | tf_op jit(solution)/shard_map/sub | solution.py:32
  (216 shorter events, 136.3 us)
Async XLA Ops:
  7.2 197.2 %all-gather.5.cloned.1.call-start = ((), (), s32[]{:S(2)}) async-start(), calls=%async_computation.2 | async-start | bytes 2621440 | tf_op jit(solution)/shard_map/all_gather | solution.py:189
  9.3 207.6 %all-gather.7.cloned.1.call-start = ((), (), s32[]{:S(2)}) async-start(), calls=%async_computation.3 | async-start | bytes 2621440 | tf_op jit(solution)/shard_map/all_gather | solution.py:190
  24.0 21.2 %collective-permute-start.7 = (bf16[25,128,128]{2,1,0:T(8,128)(2,1)S(1)}, bf16[25,128,128]{2,1,0:T(8,128)(2,1)S(1)}, u32[]{:S(2)}, u32[]{:S(2)}) collective-permute-start(bf16[25,128,128]{2,1,0:T(8,128)(2,1)S(1)} %get-tuple-element.76), channel_id=1, source_target_pairs={{0,8},{4,0},{12,4},{20,12},{28,20},{24,28},{16,24},{8,16},{1,9},{5... | collective-permute-start | bytes 2457608 | tf_op jit(solution)/shard_map/ppermute | solution.py:158
  26.9 20.1 %collective-permute-start = (bf16[25,128,128]{2,1,0:T(8,128)(2,1)S(1)}, bf16[25,128,128]{2,1,0:T(8,128)(2,1)S(1)}, u32[]{:S(2)}, u32[]{:S(2)}) collective-permute-start(bf16[25,128,128]{2,1,0:T(8,128)(2,1)S(1)} %slice.193), channel_id=1, source_target_pairs={{0,4},{4,12},{12,20},{20,28},{28,24},{24,16},{16,8},{8,0},{1,5},{5... | collective-permute-start | bytes 2457608 | tf_op jit(solution)/shard_map/ppermute | solution.py:157
  45.3 19.7 %collective-permute-start.8 = (bf16[25,128,128]{2,1,0:T(8,128)(2,1)S(1)}, bf16[25,128,128]{2,1,0:T(8,128)(2,1)S(1)}, u32[]{:S(2)}, u32[]{:S(2)}) collective-permute-start(bf16[25,128,128]{2,1,0:T(8,128)(2,1)S(1)} %collective-permute-done.7), channel_id=1, source_target_pairs={{0,8},{4,0},{12,4},{20,12},{28,20},{24,28},{16,24},{8,16},{1,9},{5... | collective-permute-start | bytes 2457608 | tf_op jit(solution)/shard_map/ppermute | solution.py:158
  47.1 20.4 %collective-permute-start.1 = (bf16[25,128,128]{2,1,0:T(8,128)(2,1)S(1)}, bf16[25,128,128]{2,1,0:T(8,128)(2,1)}, u32[]{:S(2)}, u32[]{:S(2)}) collective-permute-start(bf16[25,128,128]{2,1,0:T(8,128)(2,1)S(1)} %collective-permute-done), channel_id=1, source_target_pairs={{0,4},{4,12},{12,20},{20,28},{28,24},{24,16},{16,8},{8,0},{1,5},{5... | collective-permute-start | bytes 2457608 | tf_op jit(solution)/shard_map/ppermute | solution.py:157
  65.0 19.0 %collective-permute-start.9 = (bf16[25,128,128]{2,1,0:T(8,128)(2,1)S(1)}, bf16[25,128,128]{2,1,0:T(8,128)(2,1)}, u32[]{:S(2)}, u32[]{:S(2)}) collective-permute-start(bf16[25,128,128]{2,1,0:T(8,128)(2,1)S(1)} %collective-permute-done.8), channel_id=1, source_target_pairs={{0,8},{4,0},{12,4},{20,12},{28,20},{24,28},{16,24},{8,16},{1,9},{5... | collective-permute-start | bytes 2457608 | tf_op jit(solution)/shard_map/ppermute | solution.py:158
  67.4 285.2 %all-gather.9.cloned.1.call-start = ((), (), s32[]{:S(2)}) async-start(), calls=%async_computation.6 | async-start | bytes 14745600 | tf_op jit(solution)/shard_map/all_gather | solution.py:181
  67.5 21.0 %collective-permute-start.2 = (bf16[25,128,128]{2,1,0:T(8,128)(2,1)}, bf16[25,128,128]{2,1,0:T(8,128)(2,1)}, u32[]{:S(2)}, u32[]{:S(2)}) collective-permute-start(bf16[25,128,128]{2,1,0:T(8,128)(2,1)} %collective-permute-done.1), channel_id=1, source_target_pairs={{0,4},{4,12},{12,20},{20,28},{28,24},{24,16},{16,8},{8,0},{1,5},{5... | collective-permute-start | bytes 2457608 | tf_op jit(solution)/shard_map/ppermute | solution.py:157
  84.0 18.4 %collective-permute-start.10 = (bf16[25,128,128]{2,1,0:T(8,128)(2,1)}, bf16[25,128,128]{2,1,0:T(8,128)(2,1)}, u32[]{:S(2)}, u32[]{:S(2)}) collective-permute-start(bf16[25,128,128]{2,1,0:T(8,128)(2,1)} %collective-permute-done.9), channel_id=1, source_target_pairs={{0,8},{4,0},{12,4},{20,12},{28,20},{24,28},{16,24},{8,16},{1,9},{5... | collective-permute-start | bytes 2457608 | tf_op jit(solution)/shard_map/ppermute | solution.py:158
  88.5 18.5 %collective-permute-start.3 = (bf16[25,128,128]{2,1,0:T(8,128)(2,1)}, bf16[25,128,128]{2,1,0:T(8,128)(2,1)}, u32[]{:S(2)}, u32[]{:S(2)}) collective-permute-start(bf16[25,128,128]{2,1,0:T(8,128)(2,1)} %collective-permute-done.2), channel_id=1, source_target_pairs={{0,4},{4,12},{12,20},{20,28},{28,24},{24,16},{16,8},{8,0},{1,5},{5... | collective-permute-start | bytes 2457608 | tf_op jit(solution)/shard_map/ppermute | solution.py:157
  102.4 18.6 %collective-permute-start.11 = (bf16[25,128,128]{2,1,0:T(8,128)(2,1)}, bf16[25,128,128]{2,1,0:T(8,128)(2,1)S(1)}, u32[]{:S(2)}, u32[]{:S(2)}) collective-permute-start(bf16[25,128,128]{2,1,0:T(8,128)(2,1)} %collective-permute-done.10), channel_id=1, source_target_pairs={{0,8},{4,0},{12,4},{20,12},{28,20},{24,28},{16,24},{8,16},{1,9},{5... | collective-permute-start | bytes 2457608 | tf_op jit(solution)/shard_map/ppermute | solution.py:158
  106.9 18.6 %collective-permute-start.4 = (bf16[25,128,128]{2,1,0:T(8,128)(2,1)}, bf16[25,128,128]{2,1,0:T(8,128)(2,1)S(1)}, u32[]{:S(2)}, u32[]{:S(2)}) collective-permute-start(bf16[25,128,128]{2,1,0:T(8,128)(2,1)} %collective-permute-done.3), channel_id=1, source_target_pairs={{0,4},{4,12},{12,20},{20,28},{28,24},{24,16},{16,8},{8,0},{1,5},{5... | collective-permute-start | bytes 2457608 | tf_op jit(solution)/shard_map/ppermute | solution.py:157
  121.0 18.4 %collective-permute-start.12 = (bf16[25,128,128]{2,1,0:T(8,128)(2,1)S(1)}, bf16[25,128,128]{2,1,0:T(8,128)(2,1)S(1)}, u32[]{:S(2)}, u32[]{:S(2)}) collective-permute-start(bf16[25,128,128]{2,1,0:T(8,128)(2,1)S(1)} %collective-permute-done.11), channel_id=1, source_target_pairs={{0,8},{4,0},{12,4},{20,12},{28,20},{24,28},{16,24},{8,16},{1,9},{5... | collective-permute-start | bytes 2457608 | tf_op jit(solution)/shard_map/ppermute | solution.py:158
  125.6 18.4 %collective-permute-start.5 = (bf16[25,128,128]{2,1,0:T(8,128)(2,1)S(1)}, bf16[25,128,128]{2,1,0:T(8,128)(2,1)S(1)}, u32[]{:S(2)}, u32[]{:S(2)}) collective-permute-start(bf16[25,128,128]{2,1,0:T(8,128)(2,1)S(1)} %collective-permute-done.4), channel_id=1, source_target_pairs={{0,4},{4,12},{12,20},{20,28},{28,24},{24,16},{16,8},{8,0},{1,5},{5... | collective-permute-start | bytes 2457608 | tf_op jit(solution)/shard_map/ppermute | solution.py:157
  139.4 15.4 %collective-permute-start.13 = (bf16[25,128,128]{2,1,0:T(8,128)(2,1)S(1)}, bf16[25,128,128]{2,1,0:T(8,128)(2,1)S(1)}, u32[]{:S(2)}, u32[]{:S(2)}) collective-permute-start(bf16[25,128,128]{2,1,0:T(8,128)(2,1)S(1)} %collective-permute-done.12), channel_id=1, source_target_pairs={{0,8},{4,0},{12,4},{20,12},{28,20},{24,28},{16,24},{8,16},{1,9},{5... | collective-permute-start | bytes 2457608 | tf_op jit(solution)/shard_map/ppermute | solution.py:158
  169.9 391.8 %reduce-scatter.5.cloned.1.call-start = ((), (), s32[]{:S(2)}) async-start(), calls=%async_computation.5 | async-start | bytes 14155776 | tf_op jit(solution)/shard_map/reduce_scatter | solution.py:255
  352.7 403.6 %reduce-scatter.3.cloned.1.call-start = ((), (), s32[]{:S(2)}) async-start(), calls=%async_computation.4 | async-start | bytes 2621440 | tf_op jit(solution)/shard_map/reduce_scatter | solution.py:270
  562.8 19.4 %collective-permute-start.21 = (bf16[24,128,128]{1,2,0:T(8,128)(2,1)S(1)}, bf16[24,128,128]{1,2,0:T(8,128)(2,1)S(1)}, u32[]{:S(2)}, u32[]{:S(2)}) collective-permute-start(bf16[24,128,128]{1,2,0:T(8,128)(2,1)S(1)} %slice_bitcast_fusion), channel_id=1, source_target_pairs={{0,8},{4,0},{12,4},{20,12},{28,20},{24,28},{16,24},{8,16},{1,9},{5... | collective-permute-start | bytes 2359304 | tf_op jit(solution)/shard_map/ppermute | solution.py:219
  564.1 19.9 %collective-permute-start.14 = (bf16[24,128,128]{1,2,0:T(8,128)(2,1)S(1)}, bf16[24,128,128]{1,2,0:T(8,128)(2,1)S(1)}, u32[]{:S(2)}, u32[]{:S(2)}) collective-permute-start(bf16[24,128,128]{1,2,0:T(8,128)(2,1)S(1)} %slice_bitcast_fusion.1), channel_id=1, source_target_pairs={{0,4},{4,12},{12,20},{20,28},{28,24},{24,16},{16,8},{8,0},{1,5},{5... | collective-permute-start | bytes 2359304 | tf_op jit(solution)/shard_map/ppermute | solution.py:218
  583.6 18.5 %collective-permute-start.22 = (bf16[24,128,128]{1,2,0:T(8,128)(2,1)S(1)}, bf16[24,128,128]{1,2,0:T(8,128)(2,1)S(1)}, u32[]{:S(2)}, u32[]{:S(2)}) collective-permute-start(bf16[24,128,128]{1,2,0:T(8,128)(2,1)S(1)} %fusion.29), channel_id=1, source_target_pairs={{0,8},{4,0},{12,4},{20,12},{28,20},{24,28},{16,24},{8,16},{1,9},{5... | collective-permute-start | bytes 2359304 | tf_op jit(solution)/shard_map/ppermute | solution.py:219
  585.4 18.8 %collective-permute-start.15 = (bf16[24,128,128]{1,2,0:T(8,128)(2,1)S(1)}, bf16[24,128,128]{1,2,0:T(8,128)(2,1)S(1)}, u32[]{:S(2)}, u32[]{:S(2)}) collective-permute-start(bf16[24,128,128]{1,2,0:T(8,128)(2,1)S(1)} %fusion.35), channel_id=1, source_target_pairs={{0,4},{4,12},{12,20},{20,28},{28,24},{24,16},{16,8},{8,0},{1,5},{5... | collective-permute-start | bytes 2359304 | tf_op jit(solution)/shard_map/ppermute | solution.py:218
  603.5 17.6 %collective-permute-start.23 = (bf16[24,128,128]{1,2,0:T(8,128)(2,1)S(1)}, bf16[24,128,128]{1,2,0:T(8,128)(2,1)S(1)}, u32[]{:S(2)}, u32[]{:S(2)}) collective-permute-start(bf16[24,128,128]{1,2,0:T(8,128)(2,1)S(1)} %fusion.28), channel_id=1, source_target_pairs={{0,8},{4,0},{12,4},{20,12},{28,20},{24,28},{16,24},{8,16},{1,9},{5... | collective-permute-start | bytes 2359304 | tf_op jit(solution)/shard_map/ppermute | solution.py:219
  605.6 17.9 %collective-permute-start.16 = (bf16[24,128,128]{1,2,0:T(8,128)(2,1)S(1)}, bf16[24,128,128]{1,2,0:T(8,128)(2,1)S(1)}, u32[]{:S(2)}, u32[]{:S(2)}) collective-permute-start(bf16[24,128,128]{1,2,0:T(8,128)(2,1)S(1)} %fusion.34), channel_id=1, source_target_pairs={{0,4},{4,12},{12,20},{20,28},{28,24},{24,16},{16,8},{8,0},{1,5},{5... | collective-permute-start | bytes 2359304 | tf_op jit(solution)/shard_map/ppermute | solution.py:218
  622.5 32.0 %collective-permute-start.24 = (bf16[24,128,128]{1,2,0:T(8,128)(2,1)S(1)}, bf16[24,128,128]{1,2,0:T(8,128)(2,1)S(1)}, u32[]{:S(2)}, u32[]{:S(2)}) collective-permute-start(bf16[24,128,128]{1,2,0:T(8,128)(2,1)S(1)} %fusion.27), channel_id=1, source_target_pairs={{0,8},{4,0},{12,4},{20,12},{28,20},{24,28},{16,24},{8,16},{1,9},{5... | collective-permute-start | bytes 2359304 | tf_op jit(solution)/shard_map/ppermute | solution.py:219
  624.9 32.8 %collective-permute-start.17 = (bf16[24,128,128]{1,2,0:T(8,128)(2,1)S(1)}, bf16[24,128,128]{1,2,0:T(8,128)(2,1)S(1)}, u32[]{:S(2)}, u32[]{:S(2)}) collective-permute-start(bf16[24,128,128]{1,2,0:T(8,128)(2,1)S(1)} %fusion.33), channel_id=1, source_target_pairs={{0,4},{4,12},{12,20},{20,28},{28,24},{24,16},{16,8},{8,0},{1,5},{5... | collective-permute-start | bytes 2359304 | tf_op jit(solution)/shard_map/ppermute | solution.py:218
  656.8 30.0 %collective-permute-start.25 = (bf16[24,128,128]{1,2,0:T(8,128)(2,1)}, bf16[24,128,128]{1,2,0:T(8,128)(2,1)}, u32[]{:S(2)}, u32[]{:S(2)}) collective-permute-start(bf16[24,128,128]{1,2,0:T(8,128)(2,1)} %fusion.26), channel_id=1, source_target_pairs={{0,8},{4,0},{12,4},{20,12},{28,20},{24,28},{16,24},{8,16},{1,9},{5... | collective-permute-start | bytes 2359304 | tf_op jit(solution)/shard_map/ppermute | solution.py:219
  660.0 29.6 %collective-permute-start.18 = (bf16[24,128,128]{1,2,0:T(8,128)(2,1)}, bf16[24,128,128]{1,2,0:T(8,128)(2,1)}, u32[]{:S(2)}, u32[]{:S(2)}) collective-permute-start(bf16[24,128,128]{1,2,0:T(8,128)(2,1)} %fusion.32), channel_id=1, source_target_pairs={{0,4},{4,12},{12,20},{20,28},{28,24},{24,16},{16,8},{8,0},{1,5},{5... | collective-permute-start | bytes 2359304 | tf_op jit(solution)/shard_map/ppermute | solution.py:218
  688.4 15.6 %collective-permute-start.26 = (bf16[24,128,128]{1,2,0:T(8,128)(2,1)S(1)}, bf16[24,128,128]{1,2,0:T(8,128)(2,1)S(1)}, u32[]{:S(2)}, u32[]{:S(2)}) collective-permute-start(bf16[24,128,128]{1,2,0:T(8,128)(2,1)S(1)} %fusion.25), channel_id=1, source_target_pairs={{0,8},{4,0},{12,4},{20,12},{28,20},{24,28},{16,24},{8,16},{1,9},{5... | collective-permute-start | bytes 2359304 | tf_op jit(solution)/shard_map/ppermute | solution.py:219
  691.4 16.4 %collective-permute-start.19 = (bf16[24,128,128]{1,2,0:T(8,128)(2,1)S(1)}, bf16[24,128,128]{1,2,0:T(8,128)(2,1)S(1)}, u32[]{:S(2)}, u32[]{:S(2)}) collective-permute-start(bf16[24,128,128]{1,2,0:T(8,128)(2,1)S(1)} %fusion.31), channel_id=1, source_target_pairs={{0,4},{4,12},{12,20},{20,28},{28,24},{24,16},{16,8},{8,0},{1,5},{5... | collective-permute-start | bytes 2359304 | tf_op jit(solution)/shard_map/ppermute | solution.py:218
  706.3 16.1 %collective-permute-start.27 = (bf16[24,128,128]{1,2,0:T(8,128)(2,1)}, bf16[24,128,128]{1,2,0:T(8,128)(2,1)}, u32[]{:S(2)}, u32[]{:S(2)}) collective-permute-start(bf16[24,128,128]{1,2,0:T(8,128)(2,1)} %fusion.24), channel_id=1, source_target_pairs={{0,8},{4,0},{12,4},{20,12},{28,20},{24,28},{16,24},{8,16},{1,9},{5... | collective-permute-start | bytes 2359304 | tf_op jit(solution)/shard_map/ppermute | solution.py:219
  710.1 15.1 %collective-permute-start.20 = (bf16[24,128,128]{1,2,0:T(8,128)(2,1)}, bf16[24,128,128]{1,2,0:T(8,128)(2,1)}, u32[]{:S(2)}, u32[]{:S(2)}) collective-permute-start(bf16[24,128,128]{1,2,0:T(8,128)(2,1)} %fusion.30), channel_id=1, source_target_pairs={{0,4},{4,12},{12,20},{20,28},{28,24},{24,16},{16,8},{8,0},{1,5},{5... | collective-permute-start | bytes 2359304 | tf_op jit(solution)/shard_map/ppermute | solution.py:218
  (17 other events, 305.6 us)
Sparse Core Ops, SparseCore 0:
  10.1 25.2 all-gather.4
  67.6 22.5 all-gather.6
  170.0 182.5 all-gather.8
  356.1 205.5 reduce-scatter.4
  674.8 31.1 reduce-scatter.2

commit v10 on v9

--- a/solution.py
+++ b/solution.py
@@ -263,13 +263,14 @@
         (((1, 2), (1, 3)), ((), ())),
         preferred_element_type=jnp.float32,
     ).reshape((pre_grad.shape[0], n_row * nr * block))
-    summed_up, summed_down = ring_reduce(grad_view(features3, pre_grad), masks_up, summed_down)
+    tokens_part = partial_tokens.astype(jnp.bfloat16)
+    summed_up, (summed_down, tokens_part) = ring_reduce(
+        grad_view(features3, pre_grad), masks_up, (summed_down, tokens_part)
+    )
     grad_down = unpack(summed_down.astype(jnp.float32), flat_down)
     grad_up = unpack(summed_up, flat_up)
 
-    token_grad = lax.psum_scatter(
-        partial_tokens.astype(jnp.bfloat16), "col", scatter_dimension=1, tiled=True
-    )
+    token_grad = lax.psum_scatter(tokens_part, "col", scatter_dimension=1, tiled=True)
     new_up, new_moment_up, new_second_up = adam_update(w_up, moment_up, second_up, grad_up)
     new_down, new_moment_down, new_second_down = adam_update(
         w_down, moment_down, second_down, grad_down

time: 772 us -> 742 us (0.961)
  waiting for transfers between devices: 353 us -> 324 us
    ppermute x7, waiting for transfers between devices: 1.25 us -> 65.9 us  [ring_reduce(): in_a = lax.ppermute(acc_a, 'row', right).astype(jnp.float32)]
    ppermute x7, waiting for transfers between devices: 53.6 us -> 0.76 us  [ring_reduce(): in_b = lax.ppermute(acc_b, 'row', left).astype(jnp.float32)]
    reduce_scatter x1, waiting for transfers between devices: 113 us -> 72 us  [shards(): lax.psum_scatter(sent_down, 'row', scatter_dimension=0, tiled=True)[0]]
    unnamed x48 -> x52, local copies, waits for them, and re-layouts: 23.4 us -> 23.5 us
  transfers between devices with their start and end apart: 33 -> 33, of which waited for: 18 -> 21; matrix products, arithmetic and copies ran while one was open for 47% -> 49% of each run, Pallas kernels for 0% -> 0%
where the time goes in v10:
time: 742 us; the launch traced here: 733 us
  waiting for transfers between devices  324 us (44%)
  local copies, waits for them, and re-layouts  209 us (28%)
  other arithmetic  85.8 us (12%)
  matrix products  67.8 us (9%)
  starting transfers between devices  31.3 us (4%)
  between operations  14.9 us (2%)
    all_gather x1, waiting for transfers between devices, shards(): got_down = lax.all_gather(package_down, 'row', axis=0)  98.9 us
    ppermute x7, waiting for transfers between devices, ring_gather(): b = lax.ppermute(b, 'row', left)  77 us
    reduce_scatter x1, waiting for transfers between devices, shards(): lax.psum_scatter(sent_down, 'row', scatter_dimension=0, tiled=True)[0]  72 us
    ppermute x7, waiting for transfers between devices, ring_reduce(): in_a = lax.ppermute(acc_a, 'row', right).astype(jnp.float32)  65.9 us
    gather x3, local copies, waits for them, and re-layouts, kept_blocks(): return view.at[rows, :, cols, :].get(mode='promise_in_bounds')  60.5 us
    gather x2, local copies, waits for them, and re-layouts, rebuild(): dense = got.at[at(k).reshape(-1)].get(mode='promise_in_bounds')  48.8 us
    dot_general x1, local copies, waits for them, and re-layouts, shards(): lax.dot_general(pre_grad.reshape((pre_grad.shape[0], nc, block)), up_whol...  28.5 us
    dot_general x2, matrix products, forward(): lax.dot_general(rows3, w4, (((1, 2), (0, 2)), ((), ())), preferred_elemen...  27 us
  transfers between devices with their start and end apart: 33, of which 21 were waited for; matrix products, arithmetic and copies ran while one was open for 49% of the time, Pallas kernels for 0%

profile of v10, /device:TPU:0, one launch (start us, length us, event | category | flops | bytes accessed | tf_op | source)
XLA Modules:
  0.0 732.9 jit_solution(3107231345037344406)
XLA Ops:
  26.9 18.3 %collective-permute-done.7 = bf16[25,128,128]{2,1,0:T(8,128)(2,1)S(1)} collective-permute-done((bf16[25,128,128]{2,1,0:T(8,128)(2,1)S(1)}, bf16[25,128,128]{2,1,0:T(8,128)(2,1)S(1)}, u32[]{:S(2)}, u32[]{:S(2)}) %collective-permute-start.7) | collective-permute-done | bytes 819232 | tf_op jit(solution)/shard_map/ppermute | solution.py:158
  47.8 17.0 %collective-permute-done.8 = bf16[25,128,128]{2,1,0:T(8,128)(2,1)S(1)} collective-permute-done((bf16[25,128,128]{2,1,0:T(8,128)(2,1)S(1)}, bf16[25,128,128]{2,1,0:T(8,128)(2,1)S(1)}, u32[]{:S(2)}, u32[]{:S(2)}) %collective-permute-start.8) | collective-permute-done | bytes 819232 | tf_op jit(solution)/shard_map/ppermute | solution.py:158
  72.2 11.5 %collective-permute-done.9 = bf16[25,128,128]{2,1,0:T(8,128)(2,1)} collective-permute-done((bf16[25,128,128]{2,1,0:T(8,128)(2,1)S(1)}, bf16[25,128,128]{2,1,0:T(8,128)(2,1)}, u32[]{:S(2)}, u32[]{:S(2)}) %collective-permute-start.9) | collective-permute-done | bytes 819232 | tf_op jit(solution)/shard_map/ppermute | solution.py:158
  93.4 8.8 %collective-permute-done.10 = bf16[25,128,128]{2,1,0:T(8,128)(2,1)} collective-permute-done((bf16[25,128,128]{2,1,0:T(8,128)(2,1)}, bf16[25,128,128]{2,1,0:T(8,128)(2,1)}, u32[]{:S(2)}, u32[]{:S(2)}) %collective-permute-start.10) | collective-permute-done | bytes 819232 | tf_op jit(solution)/shard_map/ppermute | solution.py:158
  112.8 7.9 %collective-permute-done.11 = bf16[25,128,128]{2,1,0:T(8,128)(2,1)S(1)} collective-permute-done((bf16[25,128,128]{2,1,0:T(8,128)(2,1)}, bf16[25,128,128]{2,1,0:T(8,128)(2,1)S(1)}, u32[]{:S(2)}, u32[]{:S(2)}) %collective-permute-start.11) | collective-permute-done | bytes 819232 | tf_op jit(solution)/shard_map/ppermute | solution.py:158
  132.6 6.6 collective-permute-done.12
  147.6 6.9 collective-permute-done.13
  159.6 10.1 %pad_maximum_fusion = bf16[400,128,128]{2,1,0:T(8,128)(2,1)} fusion(bf16[200,128,128]{2,1,0:T(8,128)(2,1)} %bitcast.271, bf16[200,128,128]{2,1,0:T(8,128)(2,1)} %bitcast.270), kind=kLoop, calls=%fused_computation.19 | loop fusion | flops 6553600 | bytes 26214400 | tf_op jit(solution)/shard_map/concatenate | solution.py:161
  172.1 5.3 gather_fusion.2
  179.1 24.8 %gather_fusion.3 = bf16[768,128,128]{2,1,0:T(8,128)(2,1)} fusion(bf16[400,128,128]{2,1,0:T(8,128)(2,1)} %pad_maximum_fusion, s32[1024]{0:T(1024)S(1)} %get-tuple-element.87), kind=kCustom, calls=%fused_computation.3 | custom fusion | bytes 50334720 | tf_op jit(solution)/shard_map/gather | solution.py:195
  203.9 12.6 %fusion.85 = f32[24,128,256,1]{2,1,0,3:T(8,128)S(1)} fusion(bf16[32,24,128,128]{3,2,1,0:T(8,128)(2,1)} %bitcast.237, bf16[256,32,128,1]{0,2,3,1:T(8,128)(2,1)} %bitcast.268), kind=kOutput, calls=%fused_computation.220 | convolution fusion | flops 6442450944 | bytes 30408704 | tf_op jit(solution)/shard_map/dot_general | solution.py:238
  216.5 12.9 %convert_bitcast_fusion.1 = bf16[32,128,24,128]{1,3,0,2:T(8,128)(2,1)} fusion(bf16[256,32,128,1]{0,2,1,3:T(8,128)(2,1)} %bitcast.274, f32[24,128,256,1]{2,1,0,3:T(8,128)S(1)} %fusion.85), kind=kOutput, calls=%fused_computation.18 | convolution fusion | flops 6458966016 | bytes 30408704 | tf_op jit(solution)/shard_map/dot_general | solution.py:245
  229.4 24.6 %gather_fusion.5 = bf16[384,128,128]{1,2,0:T(8,128)(2,1)} fusion(bf16[32,128,24,128]{1,3,0,2:T(8,128)(2,1)} %convert_bitcast_fusion.1, s32[384]{0:T(512)S(1)} %reshape.769), kind=kCustom, calls=%fused_computation.5 | custom fusion | bytes 25168896 | tf_op jit(solution)/shard_map/gather | solution.py:206
  254.0 98.9 %all-gather.9.cloned.1.call-done = bf16[400,128,128]{2,1,0:T(8,128)(2,1)} async-done(((bf16[50,128,128]{2,1,0:T(8,128)(2,1)}), bf16[400,128,128]{2,1,0:T(8,128)(2,1)}) %all-gather.9.cloned.1.call-update) | async-done | bytes 13107216 | tf_op jit(solution)/shard_map/all_gather | solution.py:181
  359.1 28.5 %copy.92 = bf16[32,128,24,128]{3,2,1,0:T(8,128)(2,1)} copy(bf16[32,128,24,128]{3,1,2,0:T(8,128)(2,1)} %bitcast.238) | data formatting | bytes 50331648 | tf_op jit(solution)/shard_map/dot_general | solution.py:260
  387.6 24.0 %gather_fusion.6 = bf16[768,128,128]{2,1,0:T(8,128)(2,1)} fusion(bf16[400,128,128]{2,1,0:T(8,128)(2,1)} %all-gather.9.cloned.1.call-done, s32[1024]{0:T(1024)S(1)} %get-tuple-element.85), kind=kCustom, calls=%fused_computation.6 | custom fusion | bytes 50334720 | tf_op jit(solution)/shard_map/gather | solution.py:195
  411.6 14.4 %fusion.17 = bf16[256,24,128]{0,2,1:T(8,128)(2,1)} fusion(f32[24,128,256,1]{2,1,0,3:T(8,128)S(1)} %fusion.85, bf16[32,24,128,128]{3,2,1,0:T(8,128)(2,1)} %bitcast.241, bf16[256,32,128,1]{0,2,3,1:T(8,128)(2,1)} %bitcast.275), kind=kOutput, calls=%fused_computation.38 | convolution fusion | flops 6450315264 | bytes 31981568 | tf_op jit(solution)/shard_map/dot_general | solution.py:238
  426.0 13.8 %convert_bitcast_fusion = bf16[32,128,24,128]{1,3,0,2:T(8,128)(2,1)} fusion(bf16[256,32,128,1]{0,2,1,3:T(8,128)(2,1)} %bitcast.269, bf16[256,24,128]{0,2,1:T(8,128)(2,1)} %fusion.17), kind=kOutput, calls=%fused_computation.17 | convolution fusion | flops 6455033856 | bytes 28835840 | tf_op jit(solution)/shard_map/dot_general | solution.py:245
  439.8 17.8 %gather_fusion.12 = bf16[192,128,128]{1,2,0:T(8,128)(2,1)} fusion(bf16[32,128,24,128]{1,3,0,2:T(8,128)(2,1)} %convert_bitcast_fusion, s32[192]{0:T(256)S(1)} %reshape.821), kind=kCustom, calls=%fused_computation.12 | custom fusion | bytes 12584448 | tf_op jit(solution)/shard_map/gather | solution.py:206
  457.6 18.1 %gather_fusion.9 = bf16[192,128,128]{1,2,0:T(8,128)(2,1)} fusion(bf16[32,128,24,128]{1,3,0,2:T(8,128)(2,1)} %convert_bitcast_fusion, s32[192]{0:T(256)S(1)} %reshape.799), kind=kCustom, calls=%fused_computation.9 | custom fusion | bytes 12584448 | tf_op jit(solution)/shard_map/gather | solution.py:206
  475.7 14.2 %fusion.9 = bf16[256,4096]{1,0:T(8,128)(2,1)} fusion(bf16[256,24,128]{0,2,1:T(8,128)(2,1)S(1)} %copy-done.1, bf16[4096,24,128]{2,1,0:T(8,128)(2,1)} %bitcast.240), kind=kOutput, calls=%fused_computation.31 | convolution fusion | flops 6443499520 | bytes 28835840 | tf_op jit(solution)/shard_map/dot_general | solution.py:260
  489.9 72.0 %reduce-scatter.3.cloned.1.call-done = bf16[1,48,128,128]{2,3,1,0:T(8,128)(2,1)} async-done(((bf16[8,48,128,128]{2,3,1,0:T(8,128)(2,1)}), bf16[1,48,128,128]{2,3,1,0:T(8,128)(2,1)}) %reduce-scatter.3.cloned.1.call-update) | async-done | bytes 1572880 | tf_op jit(solution)/shard_map/reduce_scatter | solution.py:255
  566.4 16.1 %collective-permute-done.14 = bf16[24,128,128]{1,2,0:T(8,128)(2,1)S(1)} collective-permute-done((bf16[24,128,128]{1,2,0:T(8,128)(2,1)S(1)}, bf16[24,128,128]{1,2,0:T(8,128)(2,1)S(1)}, u32[]{:S(2)}, u32[]{:S(2)}) %collective-permute-start.14) | collective-permute-done | bytes 786464 | tf_op jit(solution)/shard_map/ppermute | solution.py:218
  587.3 15.0 %collective-permute-done.15 = bf16[24,128,128]{1,2,0:T(8,128)(2,1)S(1)} collective-permute-done((bf16[24,128,128]{1,2,0:T(8,128)(2,1)S(1)}, bf16[24,128,128]{1,2,0:T(8,128)(2,1)S(1)}, u32[]{:S(2)}, u32[]{:S(2)}) %collective-permute-start.15) | collective-permute-done | bytes 786464 | tf_op jit(solution)/shard_map/ppermute | solution.py:218
  607.3 14.1 %collective-permute-done.16 = bf16[24,128,128]{1,2,0:T(8,128)(2,1)S(1)} collective-permute-done((bf16[24,128,128]{1,2,0:T(8,128)(2,1)S(1)}, bf16[24,128,128]{1,2,0:T(8,128)(2,1)S(1)}, u32[]{:S(2)}, u32[]{:S(2)}) %collective-permute-start.16) | collective-permute-done | bytes 786464 | tf_op jit(solution)/shard_map/ppermute | solution.py:218
  626.2 13.1 %collective-permute-done.17 = bf16[24,128,128]{1,2,0:T(8,128)(2,1)S(1)} collective-permute-done((bf16[24,128,128]{1,2,0:T(8,128)(2,1)S(1)}, bf16[24,128,128]{1,2,0:T(8,128)(2,1)S(1)}, u32[]{:S(2)}, u32[]{:S(2)}) %collective-permute-start.17) | collective-permute-done | bytes 786464 | tf_op jit(solution)/shard_map/ppermute | solution.py:218
  650.0 6.6 copy.99
  667.9 6.6 collective-permute-done.19
  681.1 11.8 %multiply_subtract_fusion = (f32[512,3072]{1,0:T(8,128)}, f32[512,3072]{1,0:T(8,128)}, f32[512,3072]{1,0:T(8,128)}) fusion(f32[512,3072]{1,0:T(8,128)S(1)} %bitcast.261, f32[64,8,24,128]{3,2,1,0:T(8,128)S(1)} %bitcast.264, f32[512,3072]{1,0:T(8,128)} %param.28, f32[512,3072]{1,0:T(8,128)} %param.29), kind=kLoop, calls=%fused_computation.28 | loop fusion | flops 20447232 | bytes 44040192 | tf_op jit(solution)/shard_map/sub | solution.py:32
  700.4 6.7 copy.97
  707.1 6.1 broadcast_select_fusion.1
  713.2 12.8 %multiply_subtract_fusion.1 = (f32[512,3072]{1,0:T(8,128)}, f32[512,3072]{1,0:T(8,128)}, f32[512,3072]{1,0:T(8,128)}) fusion(f32[512,3072]{1,0:T(8,128)S(1)} %bitcast.263, f32[64,8,24,128]{3,2,1,0:T(8,128)} %bitcast.265, f32[512,3072]{1,0:T(8,128)} %param.26, f32[512,3072]{1,0:T(8,128)} %param.27), kind=kLoop, calls=%fused_computation.29 | loop fusion | flops 20447232 | bytes 44040192 | tf_op jit(solution)/shard_map/sub | solution.py:32
  (220 shorter events, 140.4 us)
Async XLA Ops:
  7.2 196.8 %all-gather.5.cloned.1.call-start = ((), (), s32[]{:S(2)}) async-start(), calls=%async_computation.2 | async-start | bytes 2621440 | tf_op jit(solution)/shard_map/all_gather | solution.py:189
  9.3 207.2 %all-gather.7.cloned.1.call-start = ((), (), s32[]{:S(2)}) async-start(), calls=%async_computation.3 | async-start | bytes 2621440 | tf_op jit(solution)/shard_map/all_gather | solution.py:190
  23.9 21.3 %collective-permute-start.7 = (bf16[25,128,128]{2,1,0:T(8,128)(2,1)S(1)}, bf16[25,128,128]{2,1,0:T(8,128)(2,1)S(1)}, u32[]{:S(2)}, u32[]{:S(2)}) collective-permute-start(bf16[25,128,128]{2,1,0:T(8,128)(2,1)S(1)} %get-tuple-element.78), channel_id=1, source_target_pairs={{0,8},{4,0},{12,4},{20,12},{28,20},{24,28},{16,24},{8,16},{1,9},{5... | collective-permute-start | bytes 2457608 | tf_op jit(solution)/shard_map/ppermute | solution.py:158
  26.8 20.1 %collective-permute-start = (bf16[25,128,128]{2,1,0:T(8,128)(2,1)S(1)}, bf16[25,128,128]{2,1,0:T(8,128)(2,1)S(1)}, u32[]{:S(2)}, u32[]{:S(2)}) collective-permute-start(bf16[25,128,128]{2,1,0:T(8,128)(2,1)S(1)} %slice.193), channel_id=1, source_target_pairs={{0,4},{4,12},{12,20},{20,28},{28,24},{24,16},{16,8},{8,0},{1,5},{5... | collective-permute-start | bytes 2457608 | tf_op jit(solution)/shard_map/ppermute | solution.py:157
  45.2 19.6 %collective-permute-start.8 = (bf16[25,128,128]{2,1,0:T(8,128)(2,1)S(1)}, bf16[25,128,128]{2,1,0:T(8,128)(2,1)S(1)}, u32[]{:S(2)}, u32[]{:S(2)}) collective-permute-start(bf16[25,128,128]{2,1,0:T(8,128)(2,1)S(1)} %collective-permute-done.7), channel_id=1, source_target_pairs={{0,8},{4,0},{12,4},{20,12},{28,20},{24,28},{16,24},{8,16},{1,9},{5... | collective-permute-start | bytes 2457608 | tf_op jit(solution)/shard_map/ppermute | solution.py:158
  47.0 20.4 %collective-permute-start.1 = (bf16[25,128,128]{2,1,0:T(8,128)(2,1)S(1)}, bf16[25,128,128]{2,1,0:T(8,128)(2,1)}, u32[]{:S(2)}, u32[]{:S(2)}) collective-permute-start(bf16[25,128,128]{2,1,0:T(8,128)(2,1)S(1)} %collective-permute-done), channel_id=1, source_target_pairs={{0,4},{4,12},{12,20},{20,28},{28,24},{24,16},{16,8},{8,0},{1,5},{5... | collective-permute-start | bytes 2457608 | tf_op jit(solution)/shard_map/ppermute | solution.py:157
  64.8 18.9 %collective-permute-start.9 = (bf16[25,128,128]{2,1,0:T(8,128)(2,1)S(1)}, bf16[25,128,128]{2,1,0:T(8,128)(2,1)}, u32[]{:S(2)}, u32[]{:S(2)}) collective-permute-start(bf16[25,128,128]{2,1,0:T(8,128)(2,1)S(1)} %collective-permute-done.8), channel_id=1, source_target_pairs={{0,8},{4,0},{12,4},{20,12},{28,20},{24,28},{16,24},{8,16},{1,9},{5... | collective-permute-start | bytes 2457608 | tf_op jit(solution)/shard_map/ppermute | solution.py:158
  67.4 285.5 %all-gather.9.cloned.1.call-start = ((), (), s32[]{:S(2)}) async-start(), calls=%async_computation.6 | async-start | bytes 14745600 | tf_op jit(solution)/shard_map/all_gather | solution.py:181
  67.4 20.9 %collective-permute-start.2 = (bf16[25,128,128]{2,1,0:T(8,128)(2,1)}, bf16[25,128,128]{2,1,0:T(8,128)(2,1)}, u32[]{:S(2)}, u32[]{:S(2)}) collective-permute-start(bf16[25,128,128]{2,1,0:T(8,128)(2,1)} %collective-permute-done.1), channel_id=1, source_target_pairs={{0,4},{4,12},{12,20},{20,28},{28,24},{24,16},{16,8},{8,0},{1,5},{5... | collective-permute-start | bytes 2457608 | tf_op jit(solution)/shard_map/ppermute | solution.py:157
  83.7 18.4 %collective-permute-start.10 = (bf16[25,128,128]{2,1,0:T(8,128)(2,1)}, bf16[25,128,128]{2,1,0:T(8,128)(2,1)}, u32[]{:S(2)}, u32[]{:S(2)}) collective-permute-start(bf16[25,128,128]{2,1,0:T(8,128)(2,1)} %collective-permute-done.9), channel_id=1, source_target_pairs={{0,8},{4,0},{12,4},{20,12},{28,20},{24,28},{16,24},{8,16},{1,9},{5... | collective-permute-start | bytes 2457608 | tf_op jit(solution)/shard_map/ppermute | solution.py:158
  88.4 18.5 %collective-permute-start.3 = (bf16[25,128,128]{2,1,0:T(8,128)(2,1)}, bf16[25,128,128]{2,1,0:T(8,128)(2,1)}, u32[]{:S(2)}, u32[]{:S(2)}) collective-permute-start(bf16[25,128,128]{2,1,0:T(8,128)(2,1)} %collective-permute-done.2), channel_id=1, source_target_pairs={{0,4},{4,12},{12,20},{20,28},{28,24},{24,16},{16,8},{8,0},{1,5},{5... | collective-permute-start | bytes 2457608 | tf_op jit(solution)/shard_map/ppermute | solution.py:157
  102.1 18.6 %collective-permute-start.11 = (bf16[25,128,128]{2,1,0:T(8,128)(2,1)}, bf16[25,128,128]{2,1,0:T(8,128)(2,1)S(1)}, u32[]{:S(2)}, u32[]{:S(2)}) collective-permute-start(bf16[25,128,128]{2,1,0:T(8,128)(2,1)} %collective-permute-done.10), channel_id=1, source_target_pairs={{0,8},{4,0},{12,4},{20,12},{28,20},{24,28},{16,24},{8,16},{1,9},{5... | collective-permute-start | bytes 2457608 | tf_op jit(solution)/shard_map/ppermute | solution.py:158
  106.8 18.6 %collective-permute-start.4 = (bf16[25,128,128]{2,1,0:T(8,128)(2,1)}, bf16[25,128,128]{2,1,0:T(8,128)(2,1)S(1)}, u32[]{:S(2)}, u32[]{:S(2)}) collective-permute-start(bf16[25,128,128]{2,1,0:T(8,128)(2,1)} %collective-permute-done.3), channel_id=1, source_target_pairs={{0,4},{4,12},{12,20},{20,28},{28,24},{24,16},{16,8},{8,0},{1,5},{5... | collective-permute-start | bytes 2457608 | tf_op jit(solution)/shard_map/ppermute | solution.py:157
  120.8 18.4 %collective-permute-start.12 = (bf16[25,128,128]{2,1,0:T(8,128)(2,1)S(1)}, bf16[25,128,128]{2,1,0:T(8,128)(2,1)S(1)}, u32[]{:S(2)}, u32[]{:S(2)}) collective-permute-start(bf16[25,128,128]{2,1,0:T(8,128)(2,1)S(1)} %collective-permute-done.11), channel_id=1, source_target_pairs={{0,8},{4,0},{12,4},{20,12},{28,20},{24,28},{16,24},{8,16},{1,9},{5... | collective-permute-start | bytes 2457608 | tf_op jit(solution)/shard_map/ppermute | solution.py:158
  125.5 18.4 %collective-permute-start.5 = (bf16[25,128,128]{2,1,0:T(8,128)(2,1)S(1)}, bf16[25,128,128]{2,1,0:T(8,128)(2,1)S(1)}, u32[]{:S(2)}, u32[]{:S(2)}) collective-permute-start(bf16[25,128,128]{2,1,0:T(8,128)(2,1)S(1)} %collective-permute-done.4), channel_id=1, source_target_pairs={{0,4},{4,12},{12,20},{20,28},{28,24},{24,16},{16,8},{8,0},{1,5},{5... | collective-permute-start | bytes 2457608 | tf_op jit(solution)/shard_map/ppermute | solution.py:157
  139.2 15.3 %collective-permute-start.13 = (bf16[25,128,128]{2,1,0:T(8,128)(2,1)S(1)}, bf16[25,128,128]{2,1,0:T(8,128)(2,1)S(1)}, u32[]{:S(2)}, u32[]{:S(2)}) collective-permute-start(bf16[25,128,128]{2,1,0:T(8,128)(2,1)S(1)} %collective-permute-done.12), channel_id=1, source_target_pairs={{0,8},{4,0},{12,4},{20,12},{28,20},{24,28},{16,24},{8,16},{1,9},{5... | collective-permute-start | bytes 2457608 | tf_op jit(solution)/shard_map/ppermute | solution.py:158
  143.9 14.8 %collective-permute-start.6 = (bf16[25,128,128]{2,1,0:T(8,128)(2,1)S(1)}, bf16[25,128,128]{2,1,0:T(8,128)(2,1)S(1)}, u32[]{:S(2)}, u32[]{:S(2)}) collective-permute-start(bf16[25,128,128]{2,1,0:T(8,128)(2,1)S(1)} %collective-permute-done.5), channel_id=1, source_target_pairs={{0,4},{4,12},{12,20},{20,28},{28,24},{24,16},{16,8},{8,0},{1,5},{5... | collective-permute-start | bytes 2457608 | tf_op jit(solution)/shard_map/ppermute | solution.py:157
  169.8 392.1 %reduce-scatter.3.cloned.1.call-start = ((), (), s32[]{:S(2)}) async-start(), calls=%async_computation.4 | async-start | bytes 14155776 | tf_op jit(solution)/shard_map/reduce_scatter | solution.py:255
  352.9 373.1 %reduce-scatter.5.cloned.1.call-start = ((), (), s32[]{:S(2)}) async-start(), calls=%async_computation.5 | async-start | bytes 2621440 | tf_op jit(solution)/shard_map/reduce_scatter | solution.py:273
  563.1 19.4 %collective-permute-start.14 = (bf16[24,128,128]{1,2,0:T(8,128)(2,1)S(1)}, bf16[24,128,128]{1,2,0:T(8,128)(2,1)S(1)}, u32[]{:S(2)}, u32[]{:S(2)}) collective-permute-start(bf16[24,128,128]{1,2,0:T(8,128)(2,1)S(1)} %slice_bitcast_fusion.1), channel_id=1, source_target_pairs={{0,4},{4,12},{12,20},{20,28},{28,24},{24,16},{16,8},{8,0},{1,5},{5... | collective-permute-start | bytes 2359304 | tf_op jit(solution)/shard_map/ppermute | solution.py:218
  565.8 19.6 %collective-permute-start.21 = (bf16[24,128,128]{1,2,0:T(8,128)(2,1)S(1)}, bf16[24,128,128]{1,2,0:T(8,128)(2,1)S(1)}, u32[]{:S(2)}, u32[]{:S(2)}) collective-permute-start(bf16[24,128,128]{1,2,0:T(8,128)(2,1)S(1)} %slice_bitcast_fusion), channel_id=1, source_target_pairs={{0,8},{4,0},{12,4},{20,12},{28,20},{24,28},{16,24},{8,16},{1,9},{5... | collective-permute-start | bytes 2359304 | tf_op jit(solution)/shard_map/ppermute | solution.py:219
  583.8 18.5 %collective-permute-start.15 = (bf16[24,128,128]{1,2,0:T(8,128)(2,1)S(1)}, bf16[24,128,128]{1,2,0:T(8,128)(2,1)S(1)}, u32[]{:S(2)}, u32[]{:S(2)}) collective-permute-start(bf16[24,128,128]{1,2,0:T(8,128)(2,1)S(1)} %fusion.35), channel_id=1, source_target_pairs={{0,4},{4,12},{12,20},{20,28},{28,24},{24,16},{16,8},{8,0},{1,5},{5... | collective-permute-start | bytes 2359304 | tf_op jit(solution)/shard_map/ppermute | solution.py:218
  586.8 18.6 %collective-permute-start.22 = (bf16[24,128,128]{1,2,0:T(8,128)(2,1)S(1)}, bf16[24,128,128]{1,2,0:T(8,128)(2,1)S(1)}, u32[]{:S(2)}, u32[]{:S(2)}) collective-permute-start(bf16[24,128,128]{1,2,0:T(8,128)(2,1)S(1)} %fusion.29), channel_id=1, source_target_pairs={{0,8},{4,0},{12,4},{20,12},{28,20},{24,28},{16,24},{8,16},{1,9},{5... | collective-permute-start | bytes 2359304 | tf_op jit(solution)/shard_map/ppermute | solution.py:219
  603.7 17.6 %collective-permute-start.16 = (bf16[24,128,128]{1,2,0:T(8,128)(2,1)S(1)}, bf16[24,128,128]{1,2,0:T(8,128)(2,1)S(1)}, u32[]{:S(2)}, u32[]{:S(2)}) collective-permute-start(bf16[24,128,128]{1,2,0:T(8,128)(2,1)S(1)} %fusion.34), channel_id=1, source_target_pairs={{0,4},{4,12},{12,20},{20,28},{28,24},{24,16},{16,8},{8,0},{1,5},{5... | collective-permute-start | bytes 2359304 | tf_op jit(solution)/shard_map/ppermute | solution.py:218
  606.7 17.6 %collective-permute-start.23 = (bf16[24,128,128]{1,2,0:T(8,128)(2,1)S(1)}, bf16[24,128,128]{1,2,0:T(8,128)(2,1)S(1)}, u32[]{:S(2)}, u32[]{:S(2)}) collective-permute-start(bf16[24,128,128]{1,2,0:T(8,128)(2,1)S(1)} %fusion.28), channel_id=1, source_target_pairs={{0,8},{4,0},{12,4},{20,12},{28,20},{24,28},{16,24},{8,16},{1,9},{5... | collective-permute-start | bytes 2359304 | tf_op jit(solution)/shard_map/ppermute | solution.py:219
  622.7 16.7 %collective-permute-start.17 = (bf16[24,128,128]{1,2,0:T(8,128)(2,1)S(1)}, bf16[24,128,128]{1,2,0:T(8,128)(2,1)S(1)}, u32[]{:S(2)}, u32[]{:S(2)}) collective-permute-start(bf16[24,128,128]{1,2,0:T(8,128)(2,1)S(1)} %fusion.33), channel_id=1, source_target_pairs={{0,4},{4,12},{12,20},{20,28},{28,24},{24,16},{16,8},{8,0},{1,5},{5... | collective-permute-start | bytes 2359304 | tf_op jit(solution)/shard_map/ppermute | solution.py:218
  625.7 17.5 %collective-permute-start.24 = (bf16[24,128,128]{1,2,0:T(8,128)(2,1)S(1)}, bf16[24,128,128]{1,2,0:T(8,128)(2,1)S(1)}, u32[]{:S(2)}, u32[]{:S(2)}) collective-permute-start(bf16[24,128,128]{1,2,0:T(8,128)(2,1)S(1)} %fusion.27), channel_id=1, source_target_pairs={{0,8},{4,0},{12,4},{20,12},{28,20},{24,28},{16,24},{8,16},{1,9},{5... | collective-permute-start | bytes 2359304 | tf_op jit(solution)/shard_map/ppermute | solution.py:219
  641.6 16.0 %collective-permute-start.18 = (bf16[24,128,128]{1,2,0:T(8,128)(2,1)}, bf16[24,128,128]{1,2,0:T(8,128)(2,1)}, u32[]{:S(2)}, u32[]{:S(2)}) collective-permute-start(bf16[24,128,128]{1,2,0:T(8,128)(2,1)} %fusion.32), channel_id=1, source_target_pairs={{0,4},{4,12},{12,20},{20,28},{28,24},{24,16},{16,8},{8,0},{1,5},{5... | collective-permute-start | bytes 2359304 | tf_op jit(solution)/shard_map/ppermute | solution.py:218
  645.5 15.9 %collective-permute-start.25 = (bf16[24,128,128]{1,2,0:T(8,128)(2,1)}, bf16[24,128,128]{1,2,0:T(8,128)(2,1)}, u32[]{:S(2)}, u32[]{:S(2)}) collective-permute-start(bf16[24,128,128]{1,2,0:T(8,128)(2,1)} %fusion.26), channel_id=1, source_target_pairs={{0,8},{4,0},{12,4},{20,12},{28,20},{24,28},{16,24},{8,16},{1,9},{5... | collective-permute-start | bytes 2359304 | tf_op jit(solution)/shard_map/ppermute | solution.py:219
  659.3 15.2 %collective-permute-start.19 = (bf16[24,128,128]{1,2,0:T(8,128)(2,1)S(1)}, bf16[24,128,128]{1,2,0:T(8,128)(2,1)S(1)}, u32[]{:S(2)}, u32[]{:S(2)}) collective-permute-start(bf16[24,128,128]{1,2,0:T(8,128)(2,1)S(1)} %fusion.31), channel_id=1, source_target_pairs={{0,4},{4,12},{12,20},{20,28},{28,24},{24,16},{16,8},{8,0},{1,5},{5... | collective-permute-start | bytes 2359304 | tf_op jit(solution)/shard_map/ppermute | solution.py:218
  663.3 15.3 %collective-permute-start.26 = (bf16[24,128,128]{1,2,0:T(8,128)(2,1)S(1)}, bf16[24,128,128]{1,2,0:T(8,128)(2,1)S(1)}, u32[]{:S(2)}, u32[]{:S(2)}) collective-permute-start(bf16[24,128,128]{1,2,0:T(8,128)(2,1)S(1)} %fusion.25), channel_id=1, source_target_pairs={{0,8},{4,0},{12,4},{20,12},{28,20},{24,28},{16,24},{8,16},{1,9},{5... | collective-permute-start | bytes 2359304 | tf_op jit(solution)/shard_map/ppermute | solution.py:219
  676.8 16.1 %collective-permute-start.20 = (bf16[24,128,128]{1,2,0:T(8,128)(2,1)}, bf16[24,128,128]{1,2,0:T(8,128)(2,1)}, u32[]{:S(2)}, u32[]{:S(2)}) collective-permute-start(bf16[24,128,128]{1,2,0:T(8,128)(2,1)} %fusion.30), channel_id=1, source_target_pairs={{0,4},{4,12},{12,20},{20,28},{28,24},{24,16},{16,8},{8,0},{1,5},{5... | collective-permute-start | bytes 2359304 | tf_op jit(solution)/shard_map/ppermute | solution.py:218
  (19 other events, 358.7 us)
Sparse Core Ops, SparseCore 0:
  10.1 25.3 all-gather.4
  67.5 22.6 all-gather.6
  169.9 182.8 all-gather.8
  356.3 205.5 reduce-scatter.2
  656.7 31.4 reduce-scatter.4

commit v11 on v10

--- a/solution.py
+++ b/solution.py
@@ -158,11 +158,7 @@
             b = lax.ppermute(b, "row", left)
             got_a.append(a)
             got_b.append(b)
-        return jnp.concatenate(
-            [jnp.stack(got_a).reshape((n_row * half, block, block)),
-             jnp.stack(got_b).reshape((n_row * half, block, block))],
-            axis=0,
-        )
+        return jnp.stack(got_a + got_b).reshape((2 * n_row * half, block, block))
 
     q = place_of
     step_a = (p - q) % n_row

time: 742 us -> 854 us (1.15)
  waiting for transfers between devices: 324 us -> 438 us
  other arithmetic: 85.8 us -> 76.3 us
    ppermute x7, waiting for transfers between devices: 9.34 us -> 108 us  [ring_gather(): a = lax.ppermute(a, 'row', right)]
    ppermute x7, waiting for transfers between devices: 77 us -> 91.2 us  [ring_gather(): b = lax.ppermute(b, 'row', left)]
    concatenate x1 -> x0, other arithmetic: 10.1 us -> none  [ring_gather(): jnp.concatenate([jnp.stack(got_a).reshape((n_row * half, block, block)),...]
    unnamed x52 -> x56, local copies, waits for them, and re-layouts: 23.5 us -> 28.8 us
  transfers between devices with their start and end apart: 33 -> 33, of which waited for: 21 -> 24; matrix products, arithmetic and copies ran while one was open for 49% -> 40% of each run, Pallas kernels for 0% -> 0%
where the time goes in v11:
time: 854 us; the launch traced here: 845 us
  waiting for transfers between devices  438 us (51%)
  local copies, waits for them, and re-layouts  211 us (25%)
  other arithmetic  76.3 us (9%)
  matrix products  67.7 us (8%)
  starting transfers between devices  37.2 us (4%)
  between operations  14.8 us (2%)
    ppermute x7, waiting for transfers between devices, ring_gather(): a = lax.ppermute(a, 'row', right)  108 us
    all_gather x1, waiting for transfers between devices, shards(): got_down = lax.all_gather(package_down, 'row', axis=0)  99.9 us
    ppermute x7, waiting for transfers between devices, ring_gather(): b = lax.ppermute(b, 'row', left)  91.2 us
    reduce_scatter x1, waiting for transfers between devices, shards(): lax.psum_scatter(sent_down, 'row', scatter_dimension=0, tiled=True)[0]  72.1 us
    ppermute x7, waiting for transfers between devices, ring_reduce(): in_a = lax.ppermute(acc_a, 'row', right).astype(jnp.float32)  66 us
    gather x3, local copies, waits for them, and re-layouts, kept_blocks(): return view.at[rows, :, cols, :].get(mode='promise_in_bounds')  60.5 us
    gather x2, local copies, waits for them, and re-layouts, rebuild(): dense = got.at[at(k).reshape(-1)].get(mode='promise_in_bounds')  49.3 us
    unnamed x56, local copies, waits for them, and re-layouts  28.8 us
  transfers between devices with their start and end apart: 33, of which 24 were waited for; matrix products, arithmetic and copies ran while one was open for 40% of the time, Pallas kernels for 0%

profile of v11, /device:TPU:0, one launch (start us, length us, event | category | flops | bytes accessed | tf_op | source)
XLA Modules:
  0.0 844.7 jit_solution(1388570047980509353)
XLA Ops:
  22.0 18.3 %collective-permute-done = bf16[25,128,128]{2,1,0:T(8,128)(2,1)S(1)} collective-permute-done((bf16[25,128,128]{2,1,0:T(8,128)(2,1)S(1)}, bf16[25,128,128]{2,1,0:T(8,128)(2,1)S(1)}, u32[]{:S(2)}, u32[]{:S(2)}) %collective-permute-start) | collective-permute-done | bytes 819232 | tf_op jit(solution)/shard_map/ppermute | solution.py:157
  42.0 17.7 %collective-permute-done.1 = bf16[25,128,128]{2,1,0:T(8,128)(2,1)S(1)} collective-permute-done((bf16[25,128,128]{2,1,0:T(8,128)(2,1)S(1)}, bf16[25,128,128]{2,1,0:T(8,128)(2,1)S(1)}, u32[]{:S(2)}, u32[]{:S(2)}) %collective-permute-start.1) | collective-permute-done | bytes 819232 | tf_op jit(solution)/shard_map/ppermute | solution.py:157
  61.1 17.1 %collective-permute-done.2 = bf16[25,128,128]{2,1,0:T(8,128)(2,1)S(1)} collective-permute-done((bf16[25,128,128]{2,1,0:T(8,128)(2,1)S(1)}, bf16[25,128,128]{2,1,0:T(8,128)(2,1)S(1)}, u32[]{:S(2)}, u32[]{:S(2)}) %collective-permute-start.2) | collective-permute-done | bytes 819232 | tf_op jit(solution)/shard_map/ppermute | solution.py:157
  79.5 17.1 %collective-permute-done.3 = bf16[25,128,128]{2,1,0:T(8,128)(2,1)S(1)} collective-permute-done((bf16[25,128,128]{2,1,0:T(8,128)(2,1)S(1)}, bf16[25,128,128]{2,1,0:T(8,128)(2,1)S(1)}, u32[]{:S(2)}, u32[]{:S(2)}) %collective-permute-start.3) | collective-permute-done | bytes 819232 | tf_op jit(solution)/shard_map/ppermute | solution.py:157
  97.9 16.9 %collective-permute-done.4 = bf16[25,128,128]{2,1,0:T(8,128)(2,1)} collective-permute-done((bf16[25,128,128]{2,1,0:T(8,128)(2,1)S(1)}, bf16[25,128,128]{2,1,0:T(8,128)(2,1)}, u32[]{:S(2)}, u32[]{:S(2)}) %collective-permute-start.4) | collective-permute-done | bytes 819232 | tf_op jit(solution)/shard_map/ppermute | solution.py:157
  120.6 12.7 %collective-permute-done.5 = bf16[25,128,128]{2,1,0:T(8,128)(2,1)} collective-permute-done((bf16[25,128,128]{2,1,0:T(8,128)(2,1)}, bf16[25,128,128]{2,1,0:T(8,128)(2,1)}, u32[]{:S(2)}, u32[]{:S(2)}) %collective-permute-start.5) | collective-permute-done | bytes 819232 | tf_op jit(solution)/shard_map/ppermute | solution.py:157
  140.7 7.8 collective-permute-done.6
  153.9 15.2 %collective-permute-done.7 = bf16[25,128,128]{2,1,0:T(8,128)(2,1)S(1)} collective-permute-done((bf16[25,128,128]{2,1,0:T(8,128)(2,1)S(1)}, bf16[25,128,128]{2,1,0:T(8,128)(2,1)S(1)}, u32[]{:S(2)}, u32[]{:S(2)}) %collective-permute-start.7) | collective-permute-done | bytes 819232 | tf_op jit(solution)/shard_map/ppermute | solution.py:158
  170.2 17.2 %collective-permute-done.8 = bf16[25,128,128]{2,1,0:T(8,128)(2,1)S(1)} collective-permute-done((bf16[25,128,128]{2,1,0:T(8,128)(2,1)S(1)}, bf16[25,128,128]{2,1,0:T(8,128)(2,1)S(1)}, u32[]{:S(2)}, u32[]{:S(2)}) %collective-permute-start.8) | collective-permute-done | bytes 819232 | tf_op jit(solution)/shard_map/ppermute | solution.py:158
  188.5 17.3 %collective-permute-done.9 = bf16[25,128,128]{2,1,0:T(8,128)(2,1)S(1)} collective-permute-done((bf16[25,128,128]{2,1,0:T(8,128)(2,1)S(1)}, bf16[25,128,128]{2,1,0:T(8,128)(2,1)S(1)}, u32[]{:S(2)}, u32[]{:S(2)}) %collective-permute-start.9) | collective-permute-done | bytes 819232 | tf_op jit(solution)/shard_map/ppermute | solution.py:158
  209.4 15.6 %collective-permute-done.10 = bf16[25,128,128]{2,1,0:T(8,128)(2,1)} collective-permute-done((bf16[25,128,128]{2,1,0:T(8,128)(2,1)S(1)}, bf16[25,128,128]{2,1,0:T(8,128)(2,1)}, u32[]{:S(2)}, u32[]{:S(2)}) %collective-permute-start.10) | collective-permute-done | bytes 819232 | tf_op jit(solution)/shard_map/ppermute | solution.py:158
  232.1 13.0 %collective-permute-done.11 = bf16[25,128,128]{2,1,0:T(8,128)(2,1)} collective-permute-done((bf16[25,128,128]{2,1,0:T(8,128)(2,1)}, bf16[25,128,128]{2,1,0:T(8,128)(2,1)}, u32[]{:S(2)}, u32[]{:S(2)}) %collective-permute-start.11) | collective-permute-done | bytes 819232 | tf_op jit(solution)/shard_map/ppermute | solution.py:158
  257.4 9.3 %collective-permute-done.12 = bf16[25,128,128]{2,1,0:T(8,128)(2,1)} collective-permute-done((bf16[25,128,128]{2,1,0:T(8,128)(2,1)}, bf16[25,128,128]{2,1,0:T(8,128)(2,1)}, u32[]{:S(2)}, u32[]{:S(2)}) %collective-permute-start.12) | collective-permute-done | bytes 819232 | tf_op jit(solution)/shard_map/ppermute | solution.py:158
  289.7 25.3 %gather_fusion.3 = bf16[768,128,128]{2,1,0:T(8,128)(2,1)} fusion(bf16[400,128,128]{2,1,0:T(8,128)(2,1)} %bitcast.20, s32[1024]{0:T(1024)S(1)} %get-tuple-element.86), kind=kCustom, calls=%fused_computation.3 | custom fusion | bytes 50334720 | tf_op jit(solution)/shard_map/gather | solution.py:191
  314.9 12.5 %fusion.85 = f32[24,128,256,1]{2,1,0,3:T(8,128)S(1)} fusion(bf16[32,24,128,128]{3,2,1,0:T(8,128)(2,1)} %bitcast.236, bf16[256,32,128,1]{0,2,3,1:T(8,128)(2,1)} %bitcast.267), kind=kOutput, calls=%fused_computation.219 | convolution fusion | flops 6442450944 | bytes 30408704 | tf_op jit(solution)/shard_map/dot_general | solution.py:234
  327.5 12.9 %convert_bitcast_fusion.1 = bf16[32,128,24,128]{1,3,0,2:T(8,128)(2,1)} fusion(bf16[256,32,128,1]{0,2,1,3:T(8,128)(2,1)} %bitcast.271, f32[24,128,256,1]{2,1,0,3:T(8,128)S(1)} %fusion.85), kind=kOutput, calls=%fused_computation.18 | convolution fusion | flops 6458966016 | bytes 30408704 | tf_op jit(solution)/shard_map/dot_general | solution.py:241
  340.4 24.6 %gather_fusion.5 = bf16[384,128,128]{1,2,0:T(8,128)(2,1)} fusion(bf16[32,128,24,128]{1,3,0,2:T(8,128)(2,1)} %convert_bitcast_fusion.1, s32[384]{0:T(512)S(1)} %reshape.765), kind=kCustom, calls=%fused_computation.5 | custom fusion | bytes 25168896 | tf_op jit(solution)/shard_map/gather | solution.py:202
  364.9 99.9 %all-gather.9.cloned.1.call-done = bf16[400,128,128]{2,1,0:T(8,128)(2,1)} async-done(((bf16[50,128,128]{2,1,0:T(8,128)(2,1)}), bf16[400,128,128]{2,1,0:T(8,128)(2,1)}) %all-gather.9.cloned.1.call-update) | async-done | bytes 13107216 | tf_op jit(solution)/shard_map/all_gather | solution.py:177
  471.0 28.4 %copy.92 = bf16[32,128,24,128]{3,2,1,0:T(8,128)(2,1)} copy(bf16[32,128,24,128]{3,1,2,0:T(8,128)(2,1)} %bitcast.237) | data formatting | bytes 50331648 | tf_op jit(solution)/shard_map/dot_general | solution.py:256
  499.4 24.0 %gather_fusion.6 = bf16[768,128,128]{2,1,0:T(8,128)(2,1)} fusion(bf16[400,128,128]{2,1,0:T(8,128)(2,1)} %all-gather.9.cloned.1.call-done, s32[1024]{0:T(1024)S(1)} %get-tuple-element.84), kind=kCustom, calls=%fused_computation.6 | custom fusion | bytes 50334720 | tf_op jit(solution)/shard_map/gather | solution.py:191
  523.5 14.4 %fusion.17 = bf16[256,24,128]{0,2,1:T(8,128)(2,1)} fusion(f32[24,128,256,1]{2,1,0,3:T(8,128)S(1)} %fusion.85, bf16[32,24,128,128]{3,2,1,0:T(8,128)(2,1)} %bitcast.240, bf16[256,32,128,1]{0,2,3,1:T(8,128)(2,1)} %bitcast.272), kind=kOutput, calls=%fused_computation.37 | convolution fusion | flops 6450315264 | bytes 31981568 | tf_op jit(solution)/shard_map/dot_general | solution.py:234
  537.9 13.8 %convert_bitcast_fusion = bf16[32,128,24,128]{1,3,0,2:T(8,128)(2,1)} fusion(bf16[256,32,128,1]{0,2,1,3:T(8,128)(2,1)} %bitcast.268, bf16[256,24,128]{0,2,1:T(8,128)(2,1)} %fusion.17), kind=kOutput, calls=%fused_computation.17 | convolution fusion | flops 6455033856 | bytes 28835840 | tf_op jit(solution)/shard_map/dot_general | solution.py:241
  551.7 17.8 %gather_fusion.12 = bf16[192,128,128]{1,2,0:T(8,128)(2,1)} fusion(bf16[32,128,24,128]{1,3,0,2:T(8,128)(2,1)} %convert_bitcast_fusion, s32[192]{0:T(256)S(1)} %reshape.817), kind=kCustom, calls=%fused_computation.12 | custom fusion | bytes 12584448 | tf_op jit(solution)/shard_map/gather | solution.py:202
  569.5 18.1 %gather_fusion.9 = bf16[192,128,128]{1,2,0:T(8,128)(2,1)} fusion(bf16[32,128,24,128]{1,3,0,2:T(8,128)(2,1)} %convert_bitcast_fusion, s32[192]{0:T(256)S(1)} %reshape.795), kind=kCustom, calls=%fused_computation.9 | custom fusion | bytes 12584448 | tf_op jit(solution)/shard_map/gather | solution.py:202
  587.6 14.1 %fusion.9 = bf16[256,4096]{1,0:T(8,128)(2,1)} fusion(bf16[256,24,128]{0,2,1:T(8,128)(2,1)S(1)} %copy-done.1, bf16[4096,24,128]{2,1,0:T(8,128)(2,1)} %bitcast.239), kind=kOutput, calls=%fused_computation.30 | convolution fusion | flops 6443499520 | bytes 28835840 | tf_op jit(solution)/shard_map/dot_general | solution.py:256
  601.7 72.1 %reduce-scatter.3.cloned.1.call-done = bf16[1,48,128,128]{2,3,1,0:T(8,128)(2,1)} async-done(((bf16[8,48,128,128]{2,3,1,0:T(8,128)(2,1)}), bf16[1,48,128,128]{2,3,1,0:T(8,128)(2,1)}) %reduce-scatter.3.cloned.1.call-update) | async-done | bytes 1572880 | tf_op jit(solution)/shard_map/reduce_scatter | solution.py:251
  678.3 16.1 %collective-permute-done.14 = bf16[24,128,128]{1,2,0:T(8,128)(2,1)S(1)} collective-permute-done((bf16[24,128,128]{1,2,0:T(8,128)(2,1)S(1)}, bf16[24,128,128]{1,2,0:T(8,128)(2,1)S(1)}, u32[]{:S(2)}, u32[]{:S(2)}) %collective-permute-start.14) | collective-permute-done | bytes 786464 | tf_op jit(solution)/shard_map/ppermute | solution.py:214
  699.3 15.0 %collective-permute-done.15 = bf16[24,128,128]{1,2,0:T(8,128)(2,1)S(1)} collective-permute-done((bf16[24,128,128]{1,2,0:T(8,128)(2,1)S(1)}, bf16[24,128,128]{1,2,0:T(8,128)(2,1)S(1)}, u32[]{:S(2)}, u32[]{:S(2)}) %collective-permute-start.15) | collective-permute-done | bytes 786464 | tf_op jit(solution)/shard_map/ppermute | solution.py:214
  719.2 14.1 %collective-permute-done.16 = bf16[24,128,128]{1,2,0:T(8,128)(2,1)S(1)} collective-permute-done((bf16[24,128,128]{1,2,0:T(8,128)(2,1)S(1)}, bf16[24,128,128]{1,2,0:T(8,128)(2,1)S(1)}, u32[]{:S(2)}, u32[]{:S(2)}) %collective-permute-start.16) | collective-permute-done | bytes 786464 | tf_op jit(solution)/shard_map/ppermute | solution.py:214
  738.1 13.1 %collective-permute-done.17 = bf16[24,128,128]{1,2,0:T(8,128)(2,1)S(1)} collective-permute-done((bf16[24,128,128]{1,2,0:T(8,128)(2,1)S(1)}, bf16[24,128,128]{1,2,0:T(8,128)(2,1)S(1)}, u32[]{:S(2)}, u32[]{:S(2)}) %collective-permute-start.17) | collective-permute-done | bytes 786464 | tf_op jit(solution)/shard_map/ppermute | solution.py:214
  793.0 11.8 %multiply_subtract_fusion = (f32[512,3072]{1,0:T(8,128)}, f32[512,3072]{1,0:T(8,128)}, f32[512,3072]{1,0:T(8,128)}) fusion(f32[512,3072]{1,0:T(8,128)S(1)} %bitcast.260, f32[64,8,24,128]{3,2,1,0:T(8,128)S(1)} %bitcast.263, f32[512,3072]{1,0:T(8,128)} %param.28, f32[512,3072]{1,0:T(8,128)} %param.29), kind=kLoop, calls=%fused_computation.27 | loop fusion | flops 20447232 | bytes 44040192 | tf_op jit(solution)/shard_map/sub | solution.py:32
  825.0 12.8 %multiply_subtract_fusion.1 = (f32[512,3072]{1,0:T(8,128)}, f32[512,3072]{1,0:T(8,128)}, f32[512,3072]{1,0:T(8,128)}) fusion(f32[512,3072]{1,0:T(8,128)S(1)} %bitcast.262, f32[64,8,24,128]{3,2,1,0:T(8,128)} %bitcast.264, f32[512,3072]{1,0:T(8,128)} %param.26, f32[512,3072]{1,0:T(8,128)} %param.27), kind=kLoop, calls=%fused_computation.28 | loop fusion | flops 20447232 | bytes 44040192 | tf_op jit(solution)/shard_map/sub | solution.py:32
  (222 shorter events, 173.7 us)
Async XLA Ops:
  7.2 307.8 %all-gather.5.cloned.1.call-start = ((), (), s32[]{:S(2)}) async-start(), calls=%async_computation.2 | async-start | bytes 2621440 | tf_op jit(solution)/shard_map/all_gather | solution.py:185
  19.0 21.3 %collective-permute-start = (bf16[25,128,128]{2,1,0:T(8,128)(2,1)S(1)}, bf16[25,128,128]{2,1,0:T(8,128)(2,1)S(1)}, u32[]{:S(2)}, u32[]{:S(2)}) collective-permute-start(bf16[25,128,128]{2,1,0:T(8,128)(2,1)S(1)} %slice.193), channel_id=1, source_target_pairs={{0,4},{4,12},{12,20},{20,28},{28,24},{24,16},{16,8},{8,0},{1,5},{5... | collective-permute-start | bytes 2457608 | tf_op jit(solution)/shard_map/ppermute | solution.py:157
  40.3 19.4 %collective-permute-start.1 = (bf16[25,128,128]{2,1,0:T(8,128)(2,1)S(1)}, bf16[25,128,128]{2,1,0:T(8,128)(2,1)S(1)}, u32[]{:S(2)}, u32[]{:S(2)}) collective-permute-start(bf16[25,128,128]{2,1,0:T(8,128)(2,1)S(1)} %collective-permute-done), channel_id=1, source_target_pairs={{0,4},{4,12},{12,20},{20,28},{28,24},{24,16},{16,8},{8,0},{1,5},{5... | collective-permute-start | bytes 2457608 | tf_op jit(solution)/shard_map/ppermute | solution.py:157
  59.7 18.5 %collective-permute-start.2 = (bf16[25,128,128]{2,1,0:T(8,128)(2,1)S(1)}, bf16[25,128,128]{2,1,0:T(8,128)(2,1)S(1)}, u32[]{:S(2)}, u32[]{:S(2)}) collective-permute-start(bf16[25,128,128]{2,1,0:T(8,128)(2,1)S(1)} %collective-permute-done.1), channel_id=1, source_target_pairs={{0,4},{4,12},{12,20},{20,28},{28,24},{24,16},{16,8},{8,0},{1,5},{5... | collective-permute-start | bytes 2457608 | tf_op jit(solution)/shard_map/ppermute | solution.py:157
  78.2 18.4 %collective-permute-start.3 = (bf16[25,128,128]{2,1,0:T(8,128)(2,1)S(1)}, bf16[25,128,128]{2,1,0:T(8,128)(2,1)S(1)}, u32[]{:S(2)}, u32[]{:S(2)}) collective-permute-start(bf16[25,128,128]{2,1,0:T(8,128)(2,1)S(1)} %collective-permute-done.2), channel_id=1, source_target_pairs={{0,4},{4,12},{12,20},{20,28},{28,24},{24,16},{16,8},{8,0},{1,5},{5... | collective-permute-start | bytes 2457608 | tf_op jit(solution)/shard_map/ppermute | solution.py:157
  96.6 18.2 %collective-permute-start.4 = (bf16[25,128,128]{2,1,0:T(8,128)(2,1)S(1)}, bf16[25,128,128]{2,1,0:T(8,128)(2,1)}, u32[]{:S(2)}, u32[]{:S(2)}) collective-permute-start(bf16[25,128,128]{2,1,0:T(8,128)(2,1)S(1)} %collective-permute-done.3), channel_id=1, source_target_pairs={{0,4},{4,12},{12,20},{20,28},{28,24},{24,16},{16,8},{8,0},{1,5},{5... | collective-permute-start | bytes 2457608 | tf_op jit(solution)/shard_map/ppermute | solution.py:157
  114.8 18.4 %collective-permute-start.5 = (bf16[25,128,128]{2,1,0:T(8,128)(2,1)}, bf16[25,128,128]{2,1,0:T(8,128)(2,1)}, u32[]{:S(2)}, u32[]{:S(2)}) collective-permute-start(bf16[25,128,128]{2,1,0:T(8,128)(2,1)} %collective-permute-done.4), channel_id=1, source_target_pairs={{0,4},{4,12},{12,20},{20,28},{28,24},{24,16},{16,8},{8,0},{1,5},{5... | collective-permute-start | bytes 2457608 | tf_op jit(solution)/shard_map/ppermute | solution.py:157
  133.2 15.2 %collective-permute-start.6 = (bf16[25,128,128]{2,1,0:T(8,128)(2,1)}, bf16[25,128,128]{2,1,0:T(8,128)(2,1)S(1)}, u32[]{:S(2)}, u32[]{:S(2)}) collective-permute-start(bf16[25,128,128]{2,1,0:T(8,128)(2,1)} %collective-permute-done.5), channel_id=1, source_target_pairs={{0,4},{4,12},{12,20},{20,28},{28,24},{24,16},{16,8},{8,0},{1,5},{5... | collective-permute-start | bytes 2457608 | tf_op jit(solution)/shard_map/ppermute | solution.py:157
  150.7 18.4 %collective-permute-start.7 = (bf16[25,128,128]{2,1,0:T(8,128)(2,1)S(1)}, bf16[25,128,128]{2,1,0:T(8,128)(2,1)S(1)}, u32[]{:S(2)}, u32[]{:S(2)}) collective-permute-start(bf16[25,128,128]{2,1,0:T(8,128)(2,1)S(1)} %get-tuple-element.78), channel_id=1, source_target_pairs={{0,8},{4,0},{12,4},{20,12},{28,20},{24,28},{16,24},{8,16},{1,9},{5... | collective-permute-start | bytes 2457608 | tf_op jit(solution)/shard_map/ppermute | solution.py:158
  153.9 173.6 %all-gather.7.cloned.1.call-start = ((), (), s32[]{:S(2)}) async-start(), calls=%async_computation.3 | async-start | bytes 2621440 | tf_op jit(solution)/shard_map/all_gather | solution.py:186
  169.1 18.3 %collective-permute-start.8 = (bf16[25,128,128]{2,1,0:T(8,128)(2,1)S(1)}, bf16[25,128,128]{2,1,0:T(8,128)(2,1)S(1)}, u32[]{:S(2)}, u32[]{:S(2)}) collective-permute-start(bf16[25,128,128]{2,1,0:T(8,128)(2,1)S(1)} %collective-permute-done.7), channel_id=1, source_target_pairs={{0,8},{4,0},{12,4},{20,12},{28,20},{24,28},{16,24},{8,16},{1,9},{5... | collective-permute-start | bytes 2457608 | tf_op jit(solution)/shard_map/ppermute | solution.py:158
  187.5 18.4 %collective-permute-start.9 = (bf16[25,128,128]{2,1,0:T(8,128)(2,1)S(1)}, bf16[25,128,128]{2,1,0:T(8,128)(2,1)S(1)}, u32[]{:S(2)}, u32[]{:S(2)}) collective-permute-start(bf16[25,128,128]{2,1,0:T(8,128)(2,1)S(1)} %collective-permute-done.8), channel_id=1, source_target_pairs={{0,8},{4,0},{12,4},{20,12},{28,20},{24,28},{16,24},{8,16},{1,9},{5... | collective-permute-start | bytes 2457608 | tf_op jit(solution)/shard_map/ppermute | solution.py:158
  205.9 19.1 %collective-permute-start.10 = (bf16[25,128,128]{2,1,0:T(8,128)(2,1)S(1)}, bf16[25,128,128]{2,1,0:T(8,128)(2,1)}, u32[]{:S(2)}, u32[]{:S(2)}) collective-permute-start(bf16[25,128,128]{2,1,0:T(8,128)(2,1)S(1)} %collective-permute-done.9), channel_id=1, source_target_pairs={{0,8},{4,0},{12,4},{20,12},{28,20},{24,28},{16,24},{8,16},{1,9},{5... | collective-permute-start | bytes 2457608 | tf_op jit(solution)/shard_map/ppermute | solution.py:158
  209.3 255.5 %all-gather.9.cloned.1.call-start = ((), (), s32[]{:S(2)}) async-start(), calls=%async_computation.6 | async-start | bytes 14745600 | tf_op jit(solution)/shard_map/all_gather | solution.py:177
  225.0 20.2 %collective-permute-start.11 = (bf16[25,128,128]{2,1,0:T(8,128)(2,1)}, bf16[25,128,128]{2,1,0:T(8,128)(2,1)}, u32[]{:S(2)}, u32[]{:S(2)}) collective-permute-start(bf16[25,128,128]{2,1,0:T(8,128)(2,1)} %collective-permute-done.10), channel_id=1, source_target_pairs={{0,8},{4,0},{12,4},{20,12},{28,20},{24,28},{16,24},{8,16},{1,9},{5... | collective-permute-start | bytes 2457608 | tf_op jit(solution)/shard_map/ppermute | solution.py:158
  245.2 21.6 %collective-permute-start.12 = (bf16[25,128,128]{2,1,0:T(8,128)(2,1)}, bf16[25,128,128]{2,1,0:T(8,128)(2,1)}, u32[]{:S(2)}, u32[]{:S(2)}) collective-permute-start(bf16[25,128,128]{2,1,0:T(8,128)(2,1)} %collective-permute-done.11), channel_id=1, source_target_pairs={{0,8},{4,0},{12,4},{20,12},{28,20},{24,28},{16,24},{8,16},{1,9},{5... | collective-permute-start | bytes 2457608 | tf_op jit(solution)/shard_map/ppermute | solution.py:158
  280.3 393.5 %reduce-scatter.3.cloned.1.call-start = ((), (), s32[]{:S(2)}) async-start(), calls=%async_computation.4 | async-start | bytes 14155776 | tf_op jit(solution)/shard_map/reduce_scatter | solution.py:251
  464.9 372.9 %reduce-scatter.5.cloned.1.call-start = ((), (), s32[]{:S(2)}) async-start(), calls=%async_computation.5 | async-start | bytes 2621440 | tf_op jit(solution)/shard_map/reduce_scatter | solution.py:269
  675.0 19.4 %collective-permute-start.14 = (bf16[24,128,128]{1,2,0:T(8,128)(2,1)S(1)}, bf16[24,128,128]{1,2,0:T(8,128)(2,1)S(1)}, u32[]{:S(2)}, u32[]{:S(2)}) collective-permute-start(bf16[24,128,128]{1,2,0:T(8,128)(2,1)S(1)} %slice_bitcast_fusion.1), channel_id=1, source_target_pairs={{0,4},{4,12},{12,20},{20,28},{28,24},{24,16},{16,8},{8,0},{1,5},{5... | collective-permute-start | bytes 2359304 | tf_op jit(solution)/shard_map/ppermute | solution.py:214
  677.7 19.6 %collective-permute-start.21 = (bf16[24,128,128]{1,2,0:T(8,128)(2,1)S(1)}, bf16[24,128,128]{1,2,0:T(8,128)(2,1)S(1)}, u32[]{:S(2)}, u32[]{:S(2)}) collective-permute-start(bf16[24,128,128]{1,2,0:T(8,128)(2,1)S(1)} %slice_bitcast_fusion), channel_id=1, source_target_pairs={{0,8},{4,0},{12,4},{20,12},{28,20},{24,28},{16,24},{8,16},{1,9},{5... | collective-permute-start | bytes 2359304 | tf_op jit(solution)/shard_map/ppermute | solution.py:215
  695.8 18.5 %collective-permute-start.15 = (bf16[24,128,128]{1,2,0:T(8,128)(2,1)S(1)}, bf16[24,128,128]{1,2,0:T(8,128)(2,1)S(1)}, u32[]{:S(2)}, u32[]{:S(2)}) collective-permute-start(bf16[24,128,128]{1,2,0:T(8,128)(2,1)S(1)} %fusion.35), channel_id=1, source_target_pairs={{0,4},{4,12},{12,20},{20,28},{28,24},{24,16},{16,8},{8,0},{1,5},{5... | collective-permute-start | bytes 2359304 | tf_op jit(solution)/shard_map/ppermute | solution.py:214
  698.7 18.5 %collective-permute-start.22 = (bf16[24,128,128]{1,2,0:T(8,128)(2,1)S(1)}, bf16[24,128,128]{1,2,0:T(8,128)(2,1)S(1)}, u32[]{:S(2)}, u32[]{:S(2)}) collective-permute-start(bf16[24,128,128]{1,2,0:T(8,128)(2,1)S(1)} %fusion.29), channel_id=1, source_target_pairs={{0,8},{4,0},{12,4},{20,12},{28,20},{24,28},{16,24},{8,16},{1,9},{5... | collective-permute-start | bytes 2359304 | tf_op jit(solution)/shard_map/ppermute | solution.py:215
  715.7 17.6 %collective-permute-start.16 = (bf16[24,128,128]{1,2,0:T(8,128)(2,1)S(1)}, bf16[24,128,128]{1,2,0:T(8,128)(2,1)S(1)}, u32[]{:S(2)}, u32[]{:S(2)}) collective-permute-start(bf16[24,128,128]{1,2,0:T(8,128)(2,1)S(1)} %fusion.34), channel_id=1, source_target_pairs={{0,4},{4,12},{12,20},{20,28},{28,24},{24,16},{16,8},{8,0},{1,5},{5... | collective-permute-start | bytes 2359304 | tf_op jit(solution)/shard_map/ppermute | solution.py:214
  718.6 17.6 %collective-permute-start.23 = (bf16[24,128,128]{1,2,0:T(8,128)(2,1)S(1)}, bf16[24,128,128]{1,2,0:T(8,128)(2,1)S(1)}, u32[]{:S(2)}, u32[]{:S(2)}) collective-permute-start(bf16[24,128,128]{1,2,0:T(8,128)(2,1)S(1)} %fusion.28), channel_id=1, source_target_pairs={{0,8},{4,0},{12,4},{20,12},{28,20},{24,28},{16,24},{8,16},{1,9},{5... | collective-permute-start | bytes 2359304 | tf_op jit(solution)/shard_map/ppermute | solution.py:215
  734.6 16.7 %collective-permute-start.17 = (bf16[24,128,128]{1,2,0:T(8,128)(2,1)S(1)}, bf16[24,128,128]{1,2,0:T(8,128)(2,1)S(1)}, u32[]{:S(2)}, u32[]{:S(2)}) collective-permute-start(bf16[24,128,128]{1,2,0:T(8,128)(2,1)S(1)} %fusion.33), channel_id=1, source_target_pairs={{0,4},{4,12},{12,20},{20,28},{28,24},{24,16},{16,8},{8,0},{1,5},{5... | collective-permute-start | bytes 2359304 | tf_op jit(solution)/shard_map/ppermute | solution.py:214
  737.6 17.5 %collective-permute-start.24 = (bf16[24,128,128]{1,2,0:T(8,128)(2,1)S(1)}, bf16[24,128,128]{1,2,0:T(8,128)(2,1)S(1)}, u32[]{:S(2)}, u32[]{:S(2)}) collective-permute-start(bf16[24,128,128]{1,2,0:T(8,128)(2,1)S(1)} %fusion.27), channel_id=1, source_target_pairs={{0,8},{4,0},{12,4},{20,12},{28,20},{24,28},{16,24},{8,16},{1,9},{5... | collective-permute-start | bytes 2359304 | tf_op jit(solution)/shard_map/ppermute | solution.py:215
  753.5 16.0 %collective-permute-start.18 = (bf16[24,128,128]{1,2,0:T(8,128)(2,1)}, bf16[24,128,128]{1,2,0:T(8,128)(2,1)}, u32[]{:S(2)}, u32[]{:S(2)}) collective-permute-start(bf16[24,128,128]{1,2,0:T(8,128)(2,1)} %fusion.32), channel_id=1, source_target_pairs={{0,4},{4,12},{12,20},{20,28},{28,24},{24,16},{16,8},{8,0},{1,5},{5... | collective-permute-start | bytes 2359304 | tf_op jit(solution)/shard_map/ppermute | solution.py:214
  757.3 15.9 %collective-permute-start.25 = (bf16[24,128,128]{1,2,0:T(8,128)(2,1)}, bf16[24,128,128]{1,2,0:T(8,128)(2,1)}, u32[]{:S(2)}, u32[]{:S(2)}) collective-permute-start(bf16[24,128,128]{1,2,0:T(8,128)(2,1)} %fusion.26), channel_id=1, source_target_pairs={{0,8},{4,0},{12,4},{20,12},{28,20},{24,28},{16,24},{8,16},{1,9},{5... | collective-permute-start | bytes 2359304 | tf_op jit(solution)/shard_map/ppermute | solution.py:215
  771.2 15.3 %collective-permute-start.19 = (bf16[24,128,128]{1,2,0:T(8,128)(2,1)S(1)}, bf16[24,128,128]{1,2,0:T(8,128)(2,1)S(1)}, u32[]{:S(2)}, u32[]{:S(2)}) collective-permute-start(bf16[24,128,128]{1,2,0:T(8,128)(2,1)S(1)} %fusion.31), channel_id=1, source_target_pairs={{0,4},{4,12},{12,20},{20,28},{28,24},{24,16},{16,8},{8,0},{1,5},{5... | collective-permute-start | bytes 2359304 | tf_op jit(solution)/shard_map/ppermute | solution.py:214
  775.2 15.3 %collective-permute-start.26 = (bf16[24,128,128]{1,2,0:T(8,128)(2,1)S(1)}, bf16[24,128,128]{1,2,0:T(8,128)(2,1)S(1)}, u32[]{:S(2)}, u32[]{:S(2)}) collective-permute-start(bf16[24,128,128]{1,2,0:T(8,128)(2,1)S(1)} %fusion.25), channel_id=1, source_target_pairs={{0,8},{4,0},{12,4},{20,12},{28,20},{24,28},{16,24},{8,16},{1,9},{5... | collective-permute-start | bytes 2359304 | tf_op jit(solution)/shard_map/ppermute | solution.py:215
  788.7 16.1 %collective-permute-start.20 = (bf16[24,128,128]{1,2,0:T(8,128)(2,1)}, bf16[24,128,128]{1,2,0:T(8,128)(2,1)}, u32[]{:S(2)}, u32[]{:S(2)}) collective-permute-start(bf16[24,128,128]{1,2,0:T(8,128)(2,1)} %fusion.30), channel_id=1, source_target_pairs={{0,4},{4,12},{12,20},{20,28},{28,24},{24,16},{16,8},{8,0},{1,5},{5... | collective-permute-start | bytes 2359304 | tf_op jit(solution)/shard_map/ppermute | solution.py:214
  792.7 14.0 %collective-permute-start.27 = (bf16[24,128,128]{1,2,0:T(8,128)(2,1)}, bf16[24,128,128]{1,2,0:T(8,128)(2,1)}, u32[]{:S(2)}, u32[]{:S(2)}) collective-permute-start(bf16[24,128,128]{1,2,0:T(8,128)(2,1)} %fusion.24), channel_id=1, source_target_pairs={{0,8},{4,0},{12,4},{20,12},{28,20},{24,28},{16,24},{8,16},{1,9},{5... | collective-permute-start | bytes 2359304 | tf_op jit(solution)/shard_map/ppermute | solution.py:215
  (20 other events, 602.7 us)
Sparse Core Ops, SparseCore 0:
  154.0 22.8 all-gather.4
  209.4 22.8 all-gather.6
  280.4 184.3 all-gather.8
  468.3 205.4 reduce-scatter.2
  768.6 31.4 reduce-scatter.4
